TPU v7x, 32 devices: a whole 2x2x4 slice. The times are simulated.
32 devices in a mesh: freq: 4 (over y, core), row: 8 (over z, x).
Axes of the slice: x: 2, y: 2, z: 4, core: 2. Of those that a mesh axis runs over, the one named last changes fastest.
Arguments:
- traces: bfloat16 [2, 8192, 8192], P(None, ('freq', 'row')), may hold values from -1.1953125 to 1.1953125
- prior: bfloat16 [4, 2, 8192, 8192], P('freq', None, None, 'row'), may hold values from -0.796875 to 0.796875
- bins: int32 [4], replicated, may hold values from 64 to 255
- panels: int32 [2], replicated, may hold values from 0 to 31
Outputs:
- multiples: bfloat16 [4, 2, 8192, 8192], P('freq', None, 'row')
- spectrum: bfloat16 [4, 2, 8192, 8192], P('freq', None, None, 'row')
All inputs are finite; a program needn't handle non-finite values.
Results may differ from a plain program's by a relative error of at most 0.0077.
Values may be sent and summed in bfloat16 or wider, within the bound.
No kernel may reach another device: no remote copies, remote signals or barrier semaphores. Data moves between devices by JAX's collectives and lax.ppermute only.
A program may use at most 640 MiB of HBM per device.

v0:
```python
import math

import jax
import jax.numpy as jnp
from jax import lax
from jax.sharding import PartitionSpec as P

NT_REC = 1024
PANEL = 256
STEPS = 2
BLOCK_START = 1022


def spread(value, axis, source):
    kept = jnp.where(lax.axis_index(axis) == source, value, 0).astype(value.dtype)
    return lax.psum(kept, axis)


def complex_terms(left, right):
    dims = (((0,), (1,)), ((), ()))

    def product(first, second):
        return lax.dot_general(first, second, dims, preferred_element_type=jnp.float32)

    real_part = product(left[0], right[0]) - product(left[1], right[1])
    imag_part = product(left[0], right[1]) + product(left[1], right[0])
    return (real_part, imag_part)


def body(traces, prior, bins, panels):
    sample_count, shots_local, receivers = traces.shape
    row_count = lax.axis_size("row")
    freq_count = lax.axis_size("freq")
    block_rows = receivers // row_count
    sample_index = BLOCK_START + jnp.arange(sample_count, dtype=jnp.int32)
    turn_count = bins[:, None] * sample_index[None, :] % NT_REC
    angles = 2.0 * math.pi / NT_REC * turn_count.astype(jnp.float32)
    twiddle = jnp.stack([jnp.cos(angles), -jnp.sin(angles)], axis=1).astype(jnp.bfloat16)
    blocked = traces.reshape(sample_count, shots_local, row_count, block_rows)
    transformed = jnp.einsum(
        "tsqb,fct->fqcsb", blocked, twiddle, preferred_element_type=jnp.float32
    ).astype(jnp.bfloat16)
    grouped = transformed.reshape(freq_count * row_count, 2, shots_local, block_rows)
    arrived = lax.all_to_all(grouped, ("freq", "row"), split_axis=0, concat_axis=2, tiled=True)
    arrived = arrived.reshape(2, freq_count * row_count * shots_local, block_rows)
    spectrum = (prior[0].astype(jnp.float32) + arrived.astype(jnp.float32)).astype(jnp.bfloat16)
    panels_each = block_rows // PANEL
    real_sum = jnp.zeros((block_rows, receivers), jnp.float32)
    imag_sum = jnp.zeros((block_rows, receivers), jnp.float32)
    for panel_step in range(STEPS):
        chosen = panels[panel_step]
        owner = chosen // panels_each
        offset = chosen % panels_each * PANEL
        own_rows = lax.dynamic_slice_in_dim(spectrum, offset, PANEL, 2)
        panel_data = spread(own_rows, "row", owner)
        left = lax.dynamic_slice_in_dim(spectrum, chosen * PANEL, PANEL, 1)
        real_part, imag_part = complex_terms(left, panel_data)
        real_sum = real_sum + real_part
        imag_sum = imag_sum + imag_part
    return (jnp.stack([real_sum, imag_sum])[None].astype(jnp.bfloat16), spectrum[None])


def solution(mesh):
    return jax.shard_map(
        body,
        mesh=mesh,
        in_specs=(P(None, ("freq", "row"), None), P("freq", None, None, "row"), P(), P()),
        out_specs=(P("freq", None, "row", None), P("freq", None, None, "row")),
        check_vma=False,
    )
```

profile of v0, /device:TPU:0, one launch (start us, length us, event | category | flops | bytes accessed | tf_op | source)
XLA Modules:
  0.0 1675.5 jit_solution(10062186824207716788)
XLA Ops:
  7.2 16.5 copy.14
  23.7 0.8 cosine_convert_fusion
  24.5 23.5 %convert_bitcast_fusion.2 = bf16[4,8,2,256,1024]{4,0,1,3,2:T(4,128)(2,1)} fusion(bf16[2,256,8,1024]{3,2,1,0:T(8,128)(2,1)} %bitcast.93, bf16[4,1,2]{0,2,1:T(2,128)(2,1)S(1)} %get-tuple-element.7, bf16[4,1,2]{0,2,1:T(2,128)(2,1)S(1)} %get-tuple-element.6), kind=kOutput, calls=%fused_computation.9 | convolution fusion | flops 83886144 | bytes 41943072 | tf_op jit(solution)/shard_map/tsqb,fct->fqcsb/dot_general | solution.py:40
  47.9 23.3 %copy.10 = bf16[4,8,2,256,1024]{4,3,2,1,0:T(8,128)(2,1)} copy(bf16[4,8,2,256,1024]{4,0,1,3,2:T(4,128)(2,1)} %convert_bitcast_fusion.2) | data formatting | bytes 67108864 | tf_op jit(solution)/shard_map/convert_element_type | solution.py:42
  71.3 0.0 copy-start
  71.3 7.4 all-to-all-start
  78.7 0.0 all-reduce.3.cloned.1.call-start
  78.8 0.0 copy-done
  78.8 0.6 fusion.27
  84.5 720.9 %all-to-all-done = bf16[32,2,256,1024]{3,2,1,0:T(8,128)(2,1)} async-done(((bf16[32,2,256,1024]{3,2,1,0:T(8,128)(2,1)}), bf16[32,2,256,1024]{3,2,1,0:T(8,128)(2,1)}, u32[]{:S(2)}, u32[]{:S(2)}) %all-to-all-start) | async-done | bytes 33554464 | tf_op jit(solution)/shard_map/all_to_all | solution.py:44
  805.4 32.3 %convert_bitcast_fusion.1 = f32[1,2,32,256,1024]{4,3,1,2,0:T(8,128)} fusion(bf16[32,2,256,1024]{3,2,1,0:T(8,128)(2,1)} %all-to-all-done), kind=kLoop, calls=%fused_computation.5 | loop fusion | flops 16777216 | bytes 100663296 | tf_op jit(solution)/shard_map/convert_element_type | solution.py:46
  837.7 43.7 %copy.11 = f32[1,2,32,256,1024]{4,3,2,1,0:T(8,128)} copy(f32[1,2,32,256,1024]{4,3,1,2,0:T(8,128)} %convert_bitcast_fusion.1) | data formatting | bytes 134217728 | tf_op jit(solution)/shard_map/convert_element_type | solution.py:46
  881.4 42.7 %fusion.1 = bf16[2,8192,1024]{2,1,0:T(8,128)(2,1)} fusion(f32[2,8192,1024]{2,1,0:T(8,128)} %bitcast.8, bf16[1,2,8192,1024]{3,2,1,0:T(8,128)(2,1)} %param.5), kind=kLoop, calls=%fused_computation.3 | loop fusion | flops 50331648 | bytes 134217728 | tf_op jit(solution)/shard_map/convert_element_type | solution.py:46
  924.1 12.3 dynamic-slice_select_fusion.1
  936.3 0.0 all-reduce.3.cloned.1.call-update
  937.6 43.1 %fusion.2 = bf16[1,2,8192,1024]{3,2,1,0:T(8,128)(2,1)} fusion(bf16[1,2,8192,1024]{3,2,1,0:T(8,128)(2,1)} %param.5, f32[1,2,32,256,1024]{4,3,2,1,0:T(8,128)} %copy.11), kind=kLoop, calls=%fused_computation.4 | loop fusion | flops 50331648 | bytes 134217728 | tf_op jit(solution)/shard_map/convert_element_type | solution.py:46
  980.7 492.7 %all-reduce.3.cloned.1.call-done = (bf16[2,8192,256]{2,1,0:T(8,128)(2,1)}, bf16[2,8192,256]{2,1,0:T(8,128)(2,1)}) async-done(((bf16[2,8192,256]{2,1,0:T(8,128)(2,1)}, bf16[2,8192,256]{2,1,0:T(8,128)(2,1)}), (bf16[2,8192,256]{2,1,0:T(8,128)(2,1)}, bf16[2,8192,256]{2,1,0:T(8,128)(2,1)})) %all-reduce.3.cloned.1.call-update) | async-done | bytes 16777232 | tf_op jit(solution)/shard_map/psum | solution.py:16
  1473.4 18.2 %fusion.12 = f32[1024,8192]{1,0:T(8,128)} fusion(bf16[2,8192,256]{2,1,0:T(8,128)(2,1)} %get-tuple-element.2, bf16[2,8192,1024]{2,1,0:T(8,128)(2,1)} %fusion.1, s32[]{:T(128)S(6)} %select_n.68), kind=kOutput, calls=%fused_computation.25 | convolution fusion | flops 4294967296 | bytes 38273028 | tf_op jit(solution)/shard_map/dot_general | solution.py:23
  1491.6 0.0 slice-done
  1491.6 0.0 slice-done.1
  1491.6 14.4 fusion.11
  1506.0 0.0 slice-start.2
  1506.0 0.0 slice-start.3
  1506.0 18.2 %fusion.9 = f32[1024,8192]{1,0:T(8,128)} fusion(bf16[2,8192,256]{2,1,0:T(8,128)(2,1)} %get-tuple-element.3, bf16[2,8192,1024]{2,1,0:T(8,128)(2,1)} %fusion.1, s32[]{:T(128)S(6)} %select_n.62), kind=kOutput, calls=%fused_computation.22 | convolution fusion | flops 4294967296 | bytes 38273028 | tf_op jit(solution)/shard_map/dot_general | solution.py:23
  1524.2 0.0 slice-done.2
  1524.2 0.0 slice-done.3
  1524.2 14.2 fusion.7
  1538.3 14.2 fusion.10
  1552.5 14.5 fusion.8
  1567.0 39.1 %fusion.4 = bf16[1,1,1024,8192]{3,2,1,0:T(8,128)(2,1)} fusion(f32[1024,8192]{1,0:T(8,128)} %fusion.12, f32[1024,8192]{1,0:T(8,128)} %fusion.9, f32[1024,8192]{1,0:T(8,128)} %fusion.7, bf16[2,8192,256]{2,1,0:T(8,128)(2,1)} %get-tuple-element.2, bf16[2,8192,1024]{2,1,0:T(8,128)(2,1)} %fusion.1, s32[]{:T(128)S(6)} %add.81, s32[]{:T(128)S(6)} %select_n.68), kind=kOutput, calls=%fused_computation.11 | convolution fusion | flops 4328521728 | bytes 122159112 | tf_op jit(solution)/shard_map/dot_general | solution.py:23
  1606.1 39.1 %fusion.3 = bf16[1,1,1024,8192]{3,2,1,0:T(8,128)(2,1)} fusion(f32[1024,8192]{1,0:T(8,128)} %fusion.11, f32[1024,8192]{1,0:T(8,128)} %fusion.8, f32[1024,8192]{1,0:T(8,128)} %fusion.10, bf16[2,8192,256]{2,1,0:T(8,128)(2,1)} %get-tuple-element.2, bf16[2,8192,1024]{2,1,0:T(8,128)(2,1)} %fusion.1, s32[]{:T(128)S(6)} %add.81, s32[]{:T(128)S(6)} %select_n.68), kind=kOutput, calls=%fused_computation.10 | convolution fusion | flops 4328521728 | bytes 122159112 | tf_op jit(solution)/shard_map/dot_general | solution.py:23
  1645.2 23.0 %pad_maximum_fusion = bf16[1,2,1024,8192]{3,2,1,0:T(8,128)(2,1)} fusion(bf16[1,1,1024,8192]{3,2,1,0:T(8,128)(2,1)} %fusion.4, bf16[1,1,1024,8192]{3,2,1,0:T(8,128)(2,1)} %fusion.3), kind=kLoop, calls=%fused_computation.6 | loop fusion | flops 16777216 | bytes 67108864 | tf_op jit(solution)/shard_map/stack | solution.py:60
  (5 shorter events, 0.0 us)
Async XLA Ops:
  71.3 7.5 copy-start
  71.3 734.1 %all-to-all-start = ((bf16[32,2,256,1024]{3,2,1,0:T(8,128)(2,1)}), bf16[32,2,256,1024]{3,2,1,0:T(8,128)(2,1)}, u32[]{:S(2)}, u32[]{:S(2)}) async-start(bf16[32,2,256,1024]{3,2,1,0:T(8,128)(2,1)} %bitcast.87), calls=%async_computation | async-start | bytes 67108864 | tf_op jit(solution)/shard_map/all_to_all | solution.py:44
  78.7 1394.7 %all-reduce.3.cloned.1.call-start = ((), (), s32[]{:S(2)}) async-start(), calls=%async_computation.1 | async-start | bytes 33554432 | tf_op jit(solution)/shard_map/psum | solution.py:16
  1473.4 18.2 %slice-start = ((s8[8388608]{0:T(1024)(128)(4,1)}), s8[4194304]{0:T(1024)(128)(4,1)S(1)}, s32[]{:S(2)}) async-start(s8[8388608]{0:T(1024)(128)(4,1)} %bitcast.88), calls=%async_computation.2 | async-start | bytes 8388608
  1473.4 18.2 %slice-start.1 = ((s8[8388608]{0:T(1024)(128)(4,1)}), s8[4194304]{0:T(1024)(128)(4,1)S(1)}, s32[]{:S(2)}) async-start(s8[8388608]{0:T(1024)(128)(4,1)} %bitcast.88), calls=%async_computation.3 | async-start | bytes 8388608
  1506.0 18.2 %slice-start.2 = ((s8[8388608]{0:T(1024)(128)(4,1)}), s8[4194304]{0:T(1024)(128)(4,1)S(1)}, s32[]{:S(2)}) async-start(s8[8388608]{0:T(1024)(128)(4,1)} %bitcast.90), calls=%async_computation.4 | async-start | bytes 8388608
  1506.0 18.2 %slice-start.3 = ((s8[8388608]{0:T(1024)(128)(4,1)}), s8[4194304]{0:T(1024)(128)(4,1)S(1)}, s32[]{:S(2)}) async-start(s8[8388608]{0:T(1024)(128)(4,1)} %bitcast.90), calls=%async_computation.5 | async-start | bytes 8388608
Sparse Core Ops, SparseCore 0:
  936.5 536.8 all-reduce.2
where the time goes:
time: 1680 us
  waiting for transfers between devices  1210 us (72%)
  matrix products  195 us (12%)
  other arithmetic  154 us (9%)
  local copies, waits for them, and re-layouts  84.2 us (5%)
  between operations  20.9 us (1%)
    all_to_all x1, waiting for transfers between devices, body(): lax.all_to_all(grouped, ('freq', 'row'), split_axis=0, concat_axis=2, til...  721 us
    psum x1, waiting for transfers between devices, spread(): return lax.psum(kept, axis)  493 us
    dot_general x8, matrix products, product(): lax.dot_general(first, second, dims, preferred_element_type=jnp.float32)  172 us
    convert_element_type x2, other arithmetic, body(): (prior[0].astype(jnp.float32) + arrived.astype(jnp.float32)).astype(jnp.b...  85.7 us
    convert_element_type x1, local copies, waits for them, and re-layouts, body(): arrived.astype(jnp.float32)  43.7 us
  transfers between devices with their start and end apart: 2, of which 2 were waited for; matrix products, arithmetic and copies ran while one was open for 3% of the time, Pallas kernels for 0%

commit v1 on v0

--- a/solution.py
+++ b/solution.py
@@ -30,20 +30,18 @@
 def body(traces, prior, bins, panels):
     sample_count, shots_local, receivers = traces.shape
     row_count = lax.axis_size("row")
-    freq_count = lax.axis_size("freq")
     block_rows = receivers // row_count
     sample_index = BLOCK_START + jnp.arange(sample_count, dtype=jnp.int32)
     turn_count = bins[:, None] * sample_index[None, :] % NT_REC
     angles = 2.0 * math.pi / NT_REC * turn_count.astype(jnp.float32)
     twiddle = jnp.stack([jnp.cos(angles), -jnp.sin(angles)], axis=1).astype(jnp.bfloat16)
-    blocked = traces.reshape(sample_count, shots_local, row_count, block_rows)
+    own_twiddle = lax.dynamic_index_in_dim(twiddle, lax.axis_index("freq"), 0, keepdims=False)
+    by_row = lax.all_to_all(traces, "row", split_axis=2, concat_axis=1, tiled=True)
+    gathered = lax.all_gather(by_row, "freq", axis=1, tiled=True)
     transformed = jnp.einsum(
-        "tsqb,fct->fqcsb", blocked, twiddle, preferred_element_type=jnp.float32
+        "tsb,ct->csb", gathered, own_twiddle, preferred_element_type=jnp.float32
     ).astype(jnp.bfloat16)
-    grouped = transformed.reshape(freq_count * row_count, 2, shots_local, block_rows)
-    arrived = lax.all_to_all(grouped, ("freq", "row"), split_axis=0, concat_axis=2, tiled=True)
-    arrived = arrived.reshape(2, freq_count * row_count * shots_local, block_rows)
-    spectrum = (prior[0].astype(jnp.float32) + arrived.astype(jnp.float32)).astype(jnp.bfloat16)
+    spectrum = (prior[0].astype(jnp.float32) + transformed.astype(jnp.float32)).astype(jnp.bfloat16)
     panels_each = block_rows // PANEL
     real_sum = jnp.zeros((block_rows, receivers), jnp.float32)
     imag_sum = jnp.zeros((block_rows, receivers), jnp.float32)

time: 1680 us -> 1370 us (0.82)
  waiting for transfers between devices: 1210 us -> 674 us
  blocking collectives: 0 us -> 190 us
  matrix products: 195 us -> 330 us
  other arithmetic: 154 us -> 40.3 us
  local copies, waits for them, and re-layouts: 84.2 us -> 115 us
    all_to_all x1 -> x0, waiting for transfers between devices: 721 us -> none  [body(): lax.all_to_all(grouped, ('freq', 'row'), split_axis=0, concat_axis=2, til...]
    all_gather x0 -> x1, waiting for transfers between devices: none -> 194 us  [body(): gathered = lax.all_gather(by_row, 'freq', axis=1, tiled=True)]
    all_to_all x0 -> x1, blocking collectives: none -> 190 us  [body(): lax.all_to_all(traces, 'row', split_axis=2, concat_axis=1, tiled=True)]
    dot_general x1, matrix products: 23.5 us -> 145 us  [body(): jnp.einsum('tsb,ct->csb', gathered, own_twiddle, preferred_element_type=j...]
    convert_element_type x3 -> x0, other arithmetic: 118 us -> none  [the longest x2 85.7 us: body(): (prior[0].astype(jnp.float32) + arrived.astype(jnp.float32)).astype(jnp.b...]
    convert_element_type x2 -> x0, local copies, waits for them, and re-layouts: 67 us -> none  [the longest x1 43.7 us: body(): arrived.astype(jnp.float32)]
    slice x0 -> x2, local copies, waits for them, and re-layouts: none -> 39.3 us  [complex_terms(): real_part = product(left[0], right[0]) - product(left[1], right[1])]
    all_to_all x0 -> x1, local copies, waits for them, and re-layouts: none -> 30.5 us  [body(): lax.all_to_all(traces, 'row', split_axis=2, concat_axis=1, tiled=True)]
  transfers between devices with their start and end apart: 2 -> 2, of which waited for: 2 -> 2; matrix products, arithmetic and copies ran while one was open for 3% -> 2% of each run, Pallas kernels for 0% -> 0%
where the time goes in v1:
time: 1370 us
  waiting for transfers between devices  674 us (49%)
  matrix products  330 us (24%)
  blocking collectives  190 us (14%)
  local copies, waits for them, and re-layouts  115 us (8%)
  other arithmetic  40.3 us (3%)
  between operations  20.2 us (1%)
    psum x1, waiting for transfers between devices, spread(): return lax.psum(kept, axis)  480 us
    all_gather x1, waiting for transfers between devices, body(): gathered = lax.all_gather(by_row, 'freq', axis=1, tiled=True)  194 us
    all_to_all x1, blocking collectives, body(): lax.all_to_all(traces, 'row', split_axis=2, concat_axis=1, tiled=True)  190 us
    dot_general x8, matrix products, product(): lax.dot_general(first, second, dims, preferred_element_type=jnp.float32)  184 us
    dot_general x1, matrix products, body(): jnp.einsum('tsb,ct->csb', gathered, own_twiddle, preferred_element_type=j...  145 us
    unnamed x8, local copies, waits for them, and re-layouts  45 us
    slice x2, local copies, waits for them, and re-layouts, complex_terms(): real_part = product(left[0], right[0]) - product(left[1], right[1])  39.3 us
    all_to_all x1, local copies, waits for them, and re-layouts, body(): lax.all_to_all(traces, 'row', split_axis=2, concat_axis=1, tiled=True)  30.5 us
  transfers between devices with their start and end apart: 2, of which 2 were waited for; matrix products, arithmetic and copies ran while one was open for 2% of the time, Pallas kernels for 0%

profile of v1, /device:TPU:0, one launch (start us, length us, event | category | flops | bytes accessed | tf_op | source)
XLA Modules:
  0.0 1370.1 jit_solution(301745803882222178)
XLA Ops:
  7.2 0.0 all-gather.2.cloned.1.call-start
  7.2 21.0 %copy.21 = bf16[2,256,8192]{1,0,2:T(2,128)(2,1)} copy(bf16[2,256,8192]{2,1,0:T(8,128)(2,1)} %param.4) | data formatting | bytes 16777216 | tf_op args[0]
  28.2 190.4 %all_to_all.18 = bf16[2,256,8192]{1,0,2:T(2,128)(2,1)} all-to-all(bf16[2,256,8192]{1,0,2:T(2,128)(2,1)} %copy.21), channel_id=1, replica_groups=mesh['freq'=4,'row'=8] {'row'}, dimensions={2} | all-to-all | bytes 16777216 | tf_op jit(solution)/shard_map/all_to_all | solution.py:39
  218.6 30.5 %copy.22 = bf16[2,8,256,1024]{3,0,2,1:T(2,128)(2,1)} copy(bf16[2,8,256,1024]{2,0,3,1:T(2,128)(2,1)} %bitcast.60) | data formatting | bytes 16777216 | tf_op jit(solution)/shard_map/all_to_all | solution.py:39
  249.1 0.0 copy-start.1
  249.1 0.0 copy-start.2
  249.1 0.0 all-gather.2.cloned.1.call-update
  249.1 0.0 all-reduce.3.cloned.1.call-start
  249.2 0.6 copy-done.1
  249.8 0.6 fusion.49
  255.3 0.0 copy-done.2
  255.3 0.1 cosine_convert_fusion
  255.4 0.2 fusion.45
  255.6 194.4 %all-gather.2.cloned.1.call-done = bf16[2,8192,1024]{2,0,1:T(2,128)(2,1)} async-done(((bf16[2,2048,1024]{2,0,1:T(2,128)(2,1)}), bf16[2,8192,1024]{2,0,1:T(2,128)(2,1)}) %all-gather.2.cloned.1.call-update) | async-done | bytes 33554448 | tf_op jit(solution)/shard_map/all_gather | solution.py:40
  449.9 145.3 %fusion = bf16[2,8192,1024]{2,0,1:T(2,128)(2,1)} fusion(bf16[1,2,8192,1024]{3,2,1,0:T(8,128)(2,1)} %param.5, bf16[2,8192,1024]{2,0,1:T(2,128)(2,1)} %all-gather.2.cloned.1.call-done, bf16[2,2]{1,0:T(2,128)(2,1)S(1)} %fusion.45), kind=kOutput, calls=%fused_computation.1 | convolution fusion | flops 150994944 | bytes 100663304 | tf_op jit(solution)/shard_map/tsb,ct->csb/dot_general | solution.py:41
  595.3 17.1 %broadcast_select_fusion.1 = (bf16[2,8192,256]{2,0,1:T(2,128)(2,1)}, bf16[2,8192,256]{2,0,1:T(2,128)(2,1)}) fusion(pred[]{:T(512)S(6)} %eq.11, bf16[2,8192,1024]{2,0,1:T(2,128)(2,1)} %fusion, s32[]{:T(128)S(6)} %select_n.71, s32[]{:T(128)S(6)} %select_n.77, pred[]{:T(512)S(6)} %eq.12), kind=kLoop, calls=%fused_computation.7 | loop fusion | flops 8388608 | bytes 33554440 | tf_op jit(solution)/shard_map/jit(_where)/select_n | solution.py:15
  612.3 0.0 all-reduce.3.cloned.1.call-update
  613.6 23.4 %copy.23 = bf16[1,2,8192,1024]{3,2,1,0:T(8,128)(2,1)} copy(bf16[1,2,8192,1024]{3,1,2,0:T(2,128)(2,1)} %bitcast.58) | data formatting | bytes 67108864
  637.0 6.4 constant_dynamic-slice_fusion.3
  643.4 479.5 %all-reduce.3.cloned.1.call-done = (bf16[2,8192,256]{2,0,1:T(2,128)(2,1)}, bf16[2,8192,256]{2,0,1:T(2,128)(2,1)}) async-done(((bf16[2,8192,256]{2,0,1:T(2,128)(2,1)}, bf16[2,8192,256]{2,0,1:T(2,128)(2,1)}), (bf16[2,8192,256]{2,0,1:T(2,128)(2,1)}, bf16[2,8192,256]{2,0,1:T(2,128)(2,1)})) %all-reduce.3.cloned.1.call-update) | async-done | bytes 16777232 | tf_op jit(solution)/shard_map/psum | solution.py:16
  1122.9 33.0 %fusion.47 = (bf16[1,8192,256]{2,0,1:T(2,128)(2,1)}, bf16[1,8192,256]{2,0,1:T(2,128)(2,1)}, bf16[1,8192,256]{2,0,1:T(2,128)(2,1)}, bf16[1,8192,256]{2,0,1:T(2,128)(2,1)}) fusion(bf16[2,8192,256]{2,0,1:T(2,128)(2,1)} %get-tuple-element.12, bf16[2,8192,256]{2,0,1:T(2,128)(2,1)} %get-tuple-element.13), kind=kLoop, calls=%fused_computation.67 | loop fusion | bytes 33554432 | tf_op jit(solution)/shard_map/slice | solution.py:25
  1155.9 0.0 copy-start
  1155.9 19.5 %fusion.11 = f32[1024,8192]{1,0:T(8,128)} fusion(bf16[1,8192,256]{2,0,1:T(2,128)(2,1)} %get-tuple-element.28, bf16[1,256,1024]{2,0,1:T(2,128)(2,1)} %get-tuple-element.17), kind=kOutput, calls=%fused_computation.18 | convolution fusion | flops 4294967296 | bytes 38273024 | tf_op jit(solution)/shard_map/dot_general | solution.py:23
  1175.3 0.0 copy-done
  1175.3 16.5 %fusion.13 = f32[1024,8192]{1,0:T(8,128)} fusion(bf16[1,8192,256]{2,0,1:T(2,128)(2,1)} %get-tuple-element.29, bf16[1,256,1024]{2,0,1:T(2,128)(2,1)S(1)} %copy-done), kind=kOutput, calls=%fused_computation.20 | convolution fusion | flops 4294967296 | bytes 38273024 | tf_op jit(solution)/shard_map/dot_general | solution.py:23
  1191.9 16.5 %fusion.15 = f32[1024,8192]{1,0:T(8,128)} fusion(bf16[1,8192,256]{2,0,1:T(2,128)(2,1)} %get-tuple-element.29, bf16[1,256,1024]{2,0,1:T(2,128)(2,1)S(1)} %get-tuple-element.16), kind=kOutput, calls=%fused_computation.22 | convolution fusion | flops 4294967296 | bytes 38273024 | tf_op jit(solution)/shard_map/dot_general | solution.py:23
  1208.4 16.5 %fusion.9 = f32[1024,8192]{1,0:T(8,128)} fusion(bf16[1,8192,256]{2,0,1:T(2,128)(2,1)} %get-tuple-element.28, bf16[1,256,1024]{2,0,1:T(2,128)(2,1)S(1)} %get-tuple-element.16), kind=kOutput, calls=%fused_computation.16 | convolution fusion | flops 4294967296 | bytes 38273024 | tf_op jit(solution)/shard_map/dot_general | solution.py:23
  1225.0 16.5 %fusion.7 = f32[1024,8192]{1,0:T(8,128)} fusion(bf16[1,8192,256]{2,0,1:T(2,128)(2,1)} %get-tuple-element.20, bf16[1,256,1024]{2,0,1:T(2,128)(2,1)S(1)} %get-tuple-element.15), kind=kOutput, calls=%fused_computation.14 | convolution fusion | flops 4294967296 | bytes 38273024 | tf_op jit(solution)/shard_map/dot_general | solution.py:23
  1241.5 17.5 %fusion.3 = f32[1024,8192]{1,0:T(8,128)} fusion(bf16[1,8192,256]{2,0,1:T(2,128)(2,1)} %get-tuple-element.21, bf16[1,256,1024]{2,0,1:T(2,128)(2,1)S(1)} %get-tuple-element.15), kind=kOutput, calls=%fused_computation.10 | convolution fusion | flops 4294967296 | bytes 38273024 | tf_op jit(solution)/shard_map/dot_general | solution.py:23
  1259.0 40.7 %fusion.1 = bf16[1,1,1024,8192]{3,2,1,0:T(8,128)(2,1)} fusion(f32[1024,8192]{1,0:T(8,128)} %fusion.7, f32[1024,8192]{1,0:T(8,128)} %fusion.15, f32[1024,8192]{1,0:T(8,128)} %fusion.11, bf16[1,8192,256]{2,0,1:T(2,128)(2,1)} %get-tuple-element.21, bf16[1,256,1024]{2,0,1:T(2,128)(2,1)S(1)} %get-tuple-element.14), kind=kOutput, calls=%fused_computation.8 | convolution fusion | flops 4328521728 | bytes 122159104 | tf_op jit(solution)/shard_map/dot_general | solution.py:23
  1299.7 40.6 %fusion.2 = bf16[1,1,1024,8192]{3,2,1,0:T(8,128)(2,1)} fusion(f32[1024,8192]{1,0:T(8,128)} %fusion.3, f32[1024,8192]{1,0:T(8,128)} %fusion.9, f32[1024,8192]{1,0:T(8,128)} %fusion.13, bf16[1,8192,256]{2,0,1:T(2,128)(2,1)} %get-tuple-element.20, bf16[1,256,1024]{2,0,1:T(2,128)(2,1)S(1)} %get-tuple-element.14), kind=kOutput, calls=%fused_computation.9 | convolution fusion | flops 4328521728 | bytes 122159104 | tf_op jit(solution)/shard_map/dot_general | solution.py:23
  1340.3 23.0 %pad_maximum_fusion = bf16[1,2,1024,8192]{3,2,1,0:T(8,128)(2,1)} fusion(bf16[1,1,1024,8192]{3,2,1,0:T(8,128)(2,1)} %fusion.2, bf16[1,1,1024,8192]{3,2,1,0:T(8,128)(2,1)} %fusion.1), kind=kLoop, calls=%fused_computation.3 | loop fusion | flops 16777216 | bytes 67108864 | tf_op jit(solution)/shard_map/stack | solution.py:58
  (1 shorter events, 0.0 us)
Async XLA Ops:
  7.2 442.8 %all-gather.2.cloned.1.call-start = ((), (), s32[]{:S(2)}) async-start(), calls=%async_computation.1 | async-start | bytes 41943040 | tf_op jit(solution)/shard_map/all_gather | solution.py:40
  249.1 0.7 copy-start.1
  249.1 6.2 copy-start.2
  249.1 873.8 %all-reduce.3.cloned.1.call-start = ((), (), s32[]{:S(2)}) async-start(), calls=%async_computation.2 | async-start | bytes 33554432 | tf_op jit(solution)/shard_map/psum | solution.py:16
  1155.9 19.5 %copy-start = (bf16[1,256,1024]{2,0,1:T(2,128)(2,1)S(1)}, bf16[1,256,1024]{2,0,1:T(2,128)(2,1)}, u32[]{:S(2)}) copy-start(bf16[1,256,1024]{2,0,1:T(2,128)(2,1)} %get-tuple-element.17) | copy-start | bytes 1572868
Sparse Core Ops, SparseCore 0:
  249.2 200.6 all-gather.1
  612.5 510.3 all-reduce.2

commit v2 on v1

v2 whole, which is shorter than its diff:
```python
import math

import jax
import jax.numpy as jnp
from jax import lax
from jax.sharding import PartitionSpec as P

NT_REC = 1024
PANEL = 256
STEPS = 2
BLOCK_START = 1022
PIECES = 2


def spread(value, axis, source):
    kept = jnp.where(lax.axis_index(axis) == source, value, 0).astype(value.dtype)
    return lax.psum(kept, axis)


def to_bf16(value):
    return lax.reduce_precision(value, exponent_bits=8, mantissa_bits=7).astype(jnp.bfloat16)


def body(traces, prior, bins, panels):
    sample_count, shots_local, receivers = traces.shape
    row_count = lax.axis_size("row")
    freq_count = lax.axis_size("freq")
    block_rows = receivers // row_count
    sample_index = BLOCK_START + jnp.arange(sample_count, dtype=jnp.int32)
    turn_count = bins[:, None] * sample_index[None, :] % NT_REC
    angles = 2.0 * math.pi / NT_REC * turn_count.astype(jnp.float32)
    twiddle = jnp.stack([jnp.cos(angles), -jnp.sin(angles)], axis=1).astype(jnp.bfloat16)
    own_twiddle = lax.dynamic_index_in_dim(twiddle, lax.axis_index("freq"), 0, keepdims=False)
    weights = own_twiddle.astype(jnp.float32)
    piece = shots_local // PIECES
    groups = freq_count * row_count
    prior_blocks = prior[0].reshape(2, groups, PIECES, piece, block_rows)
    parts = []
    for index in range(PIECES):
        chunk = traces[:, index * piece:(index + 1) * piece, :]
        by_row = lax.all_to_all(chunk, "row", split_axis=2, concat_axis=1, tiled=True)
        gathered = lax.all_gather(by_row, "freq", axis=1, tiled=True).astype(jnp.float32)
        gathered = gathered.reshape(sample_count, groups, piece, block_rows)
        transformed = weights[:, 0, None, None, None] * gathered[0] + weights[:, 1, None, None, None] * gathered[1]
        transformed = lax.reduce_precision(transformed, exponent_bits=8, mantissa_bits=7)
        parts.append(to_bf16(prior_blocks[:, :, index].astype(jnp.float32) + transformed))
    spectrum = jnp.stack(parts, axis=2).reshape(2, receivers, block_rows)
    panels_each = block_rows // PANEL
    lefts = []
    reals = []
    imags = []
    for panel_step in range(STEPS):
        chosen = panels[panel_step]
        owner = chosen // panels_each
        offset = chosen % panels_each * PANEL
        own_rows = lax.dynamic_slice_in_dim(spectrum, offset, PANEL, 2)
        right = spread(own_rows, "row", owner)
        left = lax.dynamic_slice_in_dim(spectrum, chosen * PANEL, PANEL, 1)
        lefts += [left[0], left[1]]
        reals += [right[0], -right[1]]
        imags += [right[1], right[0]]
    left_all = jnp.concatenate(lefts, axis=0)
    dims = (((0,), (1,)), ((), ()))
    real_sum = lax.dot_general(left_all, jnp.concatenate(reals, axis=1), dims, preferred_element_type=jnp.float32)
    imag_sum = lax.dot_general(left_all, jnp.concatenate(imags, axis=1), dims, preferred_element_type=jnp.float32)
    return (jnp.stack([real_sum, imag_sum])[None].astype(jnp.bfloat16), spectrum[None])


def solution(mesh):
    return jax.shard_map(
        body,
        mesh=mesh,
        in_specs=(P(None, ("freq", "row"), None), P("freq", None, None, "row"), P(), P()),
        out_specs=(P("freq", None, "row", None), P("freq", None, None, "row")),
        check_vma=False,
    )
```

time: 1370 us -> 1060 us (0.77)
  matrix products: 330 us -> 45.3 us
  waiting for transfers between devices: 674 us -> 588 us
  other arithmetic: 40.3 us -> 106 us
  local copies, waits for them, and re-layouts: 115 us -> 100 us
    dot_general x9 -> x2, matrix products: 330 us -> 45.3 us  [the longest x1 22.8 us: body(): lax.dot_general(left_all, jnp.concatenate(reals, axis=1), dims, preferred...]
    all_gather x1 -> x2, waiting for transfers between devices: 194 us -> 80.2 us  [body(): lax.all_gather(by_row, 'freq', axis=1, tiled=True).astype(jnp.float32)]
    convert_element_type x0 -> x2, other arithmetic: none -> 44 us  [the longest x1 43.8 us: to_bf16(): lax.reduce_precision(value, exponent_bits=8, mantissa_bits=7)]
    psum x1, waiting for transfers between devices: 480 us -> 508 us  [spread(): return lax.psum(kept, axis)]
    another operation x1 -> x2, other arithmetic: 0.12 us -> 23.1 us  [the longest x1 23 us: body(): spectrum = jnp.stack(parts, axis=2).reshape(2, receivers, block_rows)]
    unnamed x8 -> x10, local copies, waits for them, and re-layouts: 45 us -> 25.8 us
    squeeze x0 -> x2, local copies, waits for them, and re-layouts: none -> 14.9 us  [the longest x1 13.2 us: body(): reals += [right[0], -right[1]]]
    all_to_all x1 -> x4, local copies, waits for them, and re-layouts: 30.5 us -> 17.5 us  [body(): lax.all_to_all(chunk, 'row', split_axis=2, concat_axis=1, tiled=True)]
  transfers between devices with their start and end apart: 2 -> 3, of which waited for: 2 -> 2; matrix products, arithmetic and copies ran while one was open for 2% -> 4% of each run, Pallas kernels for 0% -> 0%
where the time goes in v2:
time: 1060 us
  waiting for transfers between devices  588 us (55%)
  blocking collectives  197 us (19%)
  other arithmetic  106 us (10%)
  local copies, waits for them, and re-layouts  100 us (9%)
  matrix products  45.3 us (4%)
  between operations  20.1 us (2%)
    psum x1, waiting for transfers between devices, spread(): return lax.psum(kept, axis)  508 us
    all_to_all x2, blocking collectives, body(): lax.all_to_all(chunk, 'row', split_axis=2, concat_axis=1, tiled=True)  197 us
    all_gather x2, waiting for transfers between devices, body(): lax.all_gather(by_row, 'freq', axis=1, tiled=True).astype(jnp.float32)  80.2 us
    convert_element_type x1, other arithmetic, to_bf16(): lax.reduce_precision(value, exponent_bits=8, mantissa_bits=7)  43.8 us
    slice x2, local copies, waits for them, and re-layouts, body(): gathered[0]  35.3 us
    unnamed x10, local copies, waits for them, and re-layouts  25.8 us
    another operation x1, other arithmetic, body(): spectrum = jnp.stack(parts, axis=2).reshape(2, receivers, block_rows)  23 us
    another operation x1, other arithmetic, body(): jnp.stack([real_sum, imag_sum])[None].astype(jnp.bfloat16)  23 us
  transfers between devices with their start and end apart: 3, of which 2 were waited for; matrix products, arithmetic and copies ran while one was open for 4% of the time, Pallas kernels for 0%

profile of v2, /device:TPU:0, one launch (start us, length us, event | category | flops | bytes accessed | tf_op | source)
XLA Modules:
  0.0 1056.8 jit_solution(18443553479764192873)
XLA Ops:
  7.2 0.0 all-gather.3.cloned.1.call-start
  7.2 6.0 fusion.30
  13.2 11.1 %copy.28 = bf16[2,128,8192]{1,0,2:T(2,128)(2,1)} copy(bf16[2,128,8192]{2,1,0:T(8,128)(2,1)} %get-tuple-element.22) | data formatting | bytes 8388608
  24.4 100.4 %all_to_all.36 = bf16[2,128,8192]{1,0,2:T(2,128)(2,1)S(1)} all-to-all(bf16[2,128,8192]{1,0,2:T(2,128)(2,1)} %copy.28), channel_id=1, replica_groups=mesh['freq'=4,'row'=8] {'row'}, dimensions={2} | all-to-all | bytes 8388608 | tf_op jit(solution)/shard_map/all_to_all | solution.py:41
  124.8 2.6 copy.23
  127.3 6.2 copy.24
  133.6 0.0 all-gather.5.cloned.1.call-start
  133.6 11.4 %copy.29 = bf16[2,128,8192]{1,0,2:T(2,128)(2,1)} copy(bf16[2,128,8192]{2,1,0:T(8,128)(2,1)} %get-tuple-element.23) | data formatting | bytes 8388608
  145.0 96.6 %all_to_all.37 = bf16[2,128,8192]{1,0,2:T(2,128)(2,1)S(1)} all-to-all(bf16[2,128,8192]{1,0,2:T(2,128)(2,1)} %copy.29), channel_id=1, replica_groups=mesh['freq'=4,'row'=8] {'row'}, dimensions={2} | all-to-all | bytes 8388608 | tf_op jit(solution)/shard_map/all_to_all | solution.py:41
  241.6 2.6 copy.26
  244.2 6.2 copy.27
  250.4 0.2 all-reduce.3.cloned.1.call-start
  250.7 0.6 fusion.31
  256.3 0.1 cosine_convert_fusion
  256.4 0.2 convert_reduce_fusion
  256.6 0.2 slice_reduce_fusion.1
  256.8 0.0 all-gather.3.cloned.1.call-done
  256.8 18.3 %fusion.28 = (f32[1,4096,1024]{2,1,0:T(8,128)}, f32[1,4096,1024]{2,1,0:T(8,128)}) fusion(bf16[2,4096,1024]{2,1,0:T(8,128)(2,1)} %all-gather.3.cloned.1.call-done), kind=kLoop, calls=%fused_computation.53 | loop fusion | bytes 67108864 | tf_op jit(solution)/shard_map/slice | solution.py:44
  275.1 80.2 %all-gather.5.cloned.1.call-done = bf16[2,4096,1024]{2,1,0:T(8,128)(2,1)} async-done(((bf16[2,1024,1024]{2,1,0:T(8,128)(2,1)}), bf16[2,4096,1024]{2,1,0:T(8,128)(2,1)}) %all-gather.5.cloned.1.call-update) | async-done | bytes 16777232 | tf_op jit(solution)/shard_map/all_gather | solution.py:42
  355.3 17.0 %fusion.29 = (f32[1,4096,1024]{2,1,0:T(8,128)}, f32[1,4096,1024]{2,1,0:T(8,128)}) fusion(bf16[2,4096,1024]{2,1,0:T(8,128)(2,1)} %all-gather.5.cloned.1.call-done), kind=kLoop, calls=%fused_computation.54 | loop fusion | bytes 67108864 | tf_op jit(solution)/shard_map/slice | solution.py:44
  372.3 43.8 %reduce-precision_convert_fusion.1 = (bf16[2,32,1,128,1024]{4,3,2,1,0:T(8,128)(2,1)}, bf16[2,32,1,128,1024]{4,3,2,1,0:T(8,128)(2,1)}) fusion(bf16[2,32,2,128,1024]{4,3,2,1,0:T(8,128)(2,1)} %bitcast.48, f32[32,128,1024]{2,1,0:T(8,128)} %bitcast.45, f32[2]{0:T(128)S(1)} %get-tuple-element.3, f32[32,128,1024]{2,1,0:T(8,128)} %bitcast.44, ...), kind=kLoop, calls=%fused_computation.3 | loop fusion | flops 134217728 | bytes 134217744 | tf_op jit(solution)/shard_map/convert_element_type | solution.py:21
  416.1 23.0 %pad_maximum_fusion = bf16[2,32,2,128,1024]{4,3,2,1,0:T(8,128)(2,1)} fusion(bf16[2,32,1,128,1024]{4,3,2,1,0:T(8,128)(2,1)} %get-tuple-element.7, bf16[2,32,1,128,1024]{4,3,2,1,0:T(8,128)(2,1)} %get-tuple-element.6), kind=kLoop, calls=%fused_computation | loop fusion | flops 16777216 | bytes 67108864 | tf_op jit(solution)/shard_map/stack | solution.py:47
  439.1 12.4 %dynamic-slice_select_fusion.1 = (bf16[2,8192,256]{2,1,0:T(8,128)(2,1)}, bf16[2,8192,256]{2,1,0:T(8,128)(2,1)}) fusion(bf16[2,8192,1024]{2,1,0:T(8,128)(2,1)} %bitcast.41, s32[]{:T(128)S(6)} %select_n.72, pred[]{:T(512)S(6)} %eq.11, s32[]{:T(128)S(6)} %select_n.77, pred[]{:T(512)S(6)} %eq.12), kind=kLoop, calls=%fused_computation.23 | loop fusion | flops 8388608 | bytes 33554440 | tf_op jit(solution)/shard_map/jit(_where)/select_n | solution.py:16
  452.8 1.7 dynamic-slice_bitcast_fusion.3
  454.5 507.5 %all-reduce.3.cloned.1.call-done = (bf16[2,8192,256]{2,1,0:T(8,128)(2,1)}, bf16[2,8192,256]{2,1,0:T(8,128)(2,1)}) async-done(((bf16[2,8192,256]{2,1,0:T(8,128)(2,1)}, bf16[2,8192,256]{2,1,0:T(8,128)(2,1)}), (bf16[2,8192,256]{2,1,0:T(8,128)(2,1)}, bf16[2,8192,256]{2,1,0:T(8,128)(2,1)})) %all-reduce.3.cloned.1.call-update) | async-done | bytes 16777232 | tf_op jit(solution)/shard_map/psum | solution.py:17
  962.0 13.2 %slice_bitcast_fusion = (bf16[8192,256]{1,0:T(8,128)(2,1)}, bf16[8192,256]{1,0:T(8,128)(2,1)}, bf16[8192,256]{1,0:T(8,128)(2,1)}, bf16[8192,256]{1,0:T(8,128)(2,1)}) fusion(bf16[2,8192,256]{2,1,0:T(8,128)(2,1)} %get-tuple-element.4, bf16[2,8192,256]{2,1,0:T(8,128)(2,1)} %get-tuple-element.5), kind=kLoop, calls=%fused_computation.24 | loop fusion | bytes 33554432 | tf_op jit(solution)/shard_map/squeeze | solution.py:60
  975.2 0.6 copy-done
  975.8 2.7 copy-done.1
  978.5 3.5 fusion.26
  981.9 22.6 %convert_bitcast_fusion = bf16[1,1,1024,8192]{3,2,1,0:T(8,128)(2,1)} fusion(bf16[8192,256]{1,0:T(8,128)(2,1)} %get-tuple-element.21, bf16[8192,256]{1,0:T(8,128)(2,1)} %get-tuple-element.20, bf16[8192,256]{1,0:T(8,128)(2,1)} %get-tuple-element.28, bf16[8192,256]{1,0:T(8,128)(2,1)} %get-tuple-element.29, bf16[256,1024]{1,0:T(8,128)(2,1)S(1)} %get-tuple-element.10, ...), kind=kOutput, calls=%fused_computation.20 | convolution fusion | flops 17263755264 | bytes 35651584 | tf_op jit(solution)/shard_map/dot_general | solution.py:65
  1004.5 22.8 %convert_bitcast_fusion.1 = bf16[1,1,1024,8192]{3,2,1,0:T(8,128)(2,1)} fusion(bf16[8192,256]{1,0:T(8,128)(2,1)} %get-tuple-element.31, bf16[8192,256]{1,0:T(8,128)(2,1)} %get-tuple-element.21, bf16[8192,256]{1,0:T(8,128)(2,1)} %get-tuple-element.30, bf16[8192,256]{1,0:T(8,128)(2,1)} %get-tuple-element.28, bf16[256,1024]{1,0:T(8,128)(2,1)S(1)} %get-tuple-element.10, ...), kind=kOutput, calls=%fused_computation.21 | convolution fusion | flops 17263755264 | bytes 35651584 | tf_op jit(solution)/shard_map/dot_general | solution.py:64
  1027.3 23.0 %pad_maximum_fusion.1 = bf16[1,2,1024,8192]{3,2,1,0:T(8,128)(2,1)} fusion(bf16[1,1,1024,8192]{3,2,1,0:T(8,128)(2,1)} %convert_bitcast_fusion, bf16[1,1,1024,8192]{3,2,1,0:T(8,128)(2,1)} %convert_bitcast_fusion.1), kind=kLoop, calls=%fused_computation.1 | loop fusion | flops 16777216 | bytes 67108864 | tf_op jit(solution)/shard_map/stack | solution.py:66
  (10 shorter events, 0.1 us)
Async XLA Ops:
  7.2 249.6 %all-gather.3.cloned.1.call-start = ((), (), s32[]{:S(2)}) async-start(), calls=%async_computation.2 | async-start | bytes 20971520 | tf_op jit(solution)/shard_map/all_gather | solution.py:42
  133.6 221.8 %all-gather.5.cloned.1.call-start = ((), (), s32[]{:S(2)}) async-start(), calls=%async_computation.3 | async-start | bytes 20971520 | tf_op jit(solution)/shard_map/all_gather | solution.py:42
  145.0 105.6 %copy-start.2 = (s32[2]{0:T(128)S(1)}, s32[2]{0:T(128)}, u32[]{:S(2)}) copy-start(s32[2]{0:T(128)} %param.7) | copy-start | bytes 28
  145.0 111.3 %copy-start.3 = (s32[4]{0:T(128)S(1)}, s32[4]{0:T(128)}, u32[]{:S(2)}) copy-start(s32[4]{0:T(128)} %param.6) | copy-start | bytes 52
  250.4 711.6 %all-reduce.3.cloned.1.call-start = ((), (), s32[]{:S(2)}) async-start(), calls=%async_computation.4 | async-start | bytes 33554432 | tf_op jit(solution)/shard_map/psum | solution.py:17
  962.0 13.8 %copy-start = (bf16[2,8192,256]{2,1,0:T(8,128)(2,1)S(1)}, bf16[2,8192,256]{2,1,0:T(8,128)(2,1)}, u32[]{:S(2)}) copy-start(bf16[2,8192,256]{2,1,0:T(8,128)(2,1)} %get-tuple-element.4) | copy-start | bytes 25165828
  962.0 16.4 %copy-start.1 = (bf16[2,8192,256]{2,1,0:T(8,128)(2,1)S(1)}, bf16[2,8192,256]{2,1,0:T(8,128)(2,1)}, u32[]{:S(2)}) copy-start(bf16[2,8192,256]{2,1,0:T(8,128)(2,1)} %get-tuple-element.5) | copy-start | bytes 25165828
Sparse Core Ops, SparseCore 0:
  133.7 104.9 all-gather.2
  250.5 104.7 all-gather.4
  451.6 510.3 all-reduce.2

commit v3 on v2

--- a/solution.py
+++ b/solution.py
@@ -10,11 +10,57 @@
 STEPS = 2
 BLOCK_START = 1022
 PIECES = 2
+RING_CHUNKS = 8
 
 
-def spread(value, axis, source):
-    kept = jnp.where(lax.axis_index(axis) == source, value, 0).astype(value.dtype)
-    return lax.psum(kept, axis)
+def ring_order(count):
+    evens = list(range(0, count, 2))
+    odds = list(range(1, count, 2))[::-1]
+    return evens + odds
+
+
+def broadcast(values, owners, chunks):
+    count = lax.axis_size("row")
+    order = ring_order(count)
+    place = [0] * count
+    for position, member in enumerate(order):
+        place[member] = position
+    place_of = jnp.array(place, jnp.int32)
+    mine = place_of[lax.axis_index("row")]
+    forward = [(order[i], order[(i + 1) % count]) for i in range(count)]
+    backward = [(order[(i + 1) % count], order[i]) for i in range(count)]
+    steps = chunks + count - 2
+    halves = []
+    for direction, pairs in ((0, forward), (1, backward)):
+        distance = []
+        own = []
+        for value, owner in zip(values, owners):
+            if direction == 0:
+                distance.append((mine - place_of[owner]) % count)
+            else:
+                distance.append((place_of[owner] - mine) % count)
+            half = value.shape[1] // 2
+            part = value[:, direction * half:(direction + 1) * half]
+            own.append(part.reshape(part.shape[0], chunks, half // chunks, *part.shape[2:]))
+        held = [jnp.zeros_like(piece[:, 0]) for piece in own]
+        arrived = [[] for _ in values]
+        for step in range(steps):
+            send = [
+                jnp.where(distance[p] == 0, own[p][:, min(step, chunks - 1)], held[p])
+                for p in range(len(values))
+            ]
+            held = lax.ppermute(send, "row", pairs)
+            for p in range(len(values)):
+                arrived[p].append(held[p])
+        results = []
+        for p in range(len(values)):
+            stacked = jnp.stack(arrived[p], axis=1)
+            start = jnp.maximum(distance[p] - 1, 0)
+            picked = lax.dynamic_slice_in_dim(stacked, start, chunks, 1)
+            picked = jnp.where(distance[p] == 0, own[p], picked)
+            results.append(picked.reshape(picked.shape[0], -1, *picked.shape[3:]))
+        halves.append(results)
+    return [jnp.concatenate([halves[0][p], halves[1][p]], axis=1) for p in range(len(values))]
 
 
 def to_bf16(value):
@@ -46,17 +92,20 @@
         parts.append(to_bf16(prior_blocks[:, :, index].astype(jnp.float32) + transformed))
     spectrum = jnp.stack(parts, axis=2).reshape(2, receivers, block_rows)
     panels_each = block_rows // PANEL
+    own_panels = []
+    owners = []
     lefts = []
+    for panel_step in range(STEPS):
+        chosen = panels[panel_step]
+        owners.append(chosen // panels_each)
+        offset = chosen % panels_each * PANEL
+        own_panels.append(lax.dynamic_slice_in_dim(spectrum, offset, PANEL, 2))
+        left = lax.dynamic_slice_in_dim(spectrum, chosen * PANEL, PANEL, 1)
+        lefts += [left[0], left[1]]
+    rights = broadcast(own_panels, owners, RING_CHUNKS)
     reals = []
     imags = []
-    for panel_step in range(STEPS):
-        chosen = panels[panel_step]
-        owner = chosen // panels_each
-        offset = chosen % panels_each * PANEL
-        own_rows = lax.dynamic_slice_in_dim(spectrum, offset, PANEL, 2)
-        right = spread(own_rows, "row", owner)
-        left = lax.dynamic_slice_in_dim(spectrum, chosen * PANEL, PANEL, 1)
-        lefts += [left[0], left[1]]
+    for right in rights:
         reals += [right[0], -right[1]]
         imags += [right[1], right[0]]
     left_all = jnp.concatenate(lefts, axis=0)

time: 1060 us -> 877 us (0.83)
  waiting for transfers between devices: 588 us -> 276 us
  starting transfers between devices: 0.3 us -> 60 us
  other arithmetic: 106 us -> 147 us
  local copies, waits for them, and re-layouts: 100 us -> 114 us
    psum x1 -> x0, waiting for transfers between devices: 508 us -> none  [spread(): return lax.psum(kept, axis)]
    ppermute x0 -> x56, waiting for transfers between devices: none -> 203 us  [broadcast(): held = lax.ppermute(send, 'row', pairs)]
    ppermute x0 -> x56, starting transfers between devices: none -> 59.9 us  [broadcast(): held = lax.ppermute(send, 'row', pairs)]
    select_n x1 -> x60, other arithmetic: 12.4 us -> 46.3 us  [the longest x56 35.4 us: broadcast(): jnp.where(distance[p] == 0, own[p][:, min(step, chunks - 1)], held[p])]
    squeeze x1 -> x0, local copies, waits for them, and re-layouts: 13.2 us -> none  [body(): reals += [right[0], -right[1]]]
    unnamed x10 -> x84, local copies, waits for them, and re-layouts: 25.8 us -> 38.6 us
  transfers between devices with their start and end apart: 3 -> 58, of which waited for: 2 -> 36; matrix products, arithmetic and copies ran while one was open for 4% -> 12% of each run, Pallas kernels for 0% -> 0%
where the time goes in v3:
time: 877 us; the launch traced here: 866 us
  waiting for transfers between devices  276 us (31%)
  blocking collectives  197 us (22%)
  other arithmetic  147 us (17%)
  local copies, waits for them, and re-layouts  114 us (13%)
  starting transfers between devices  60 us (7%)
  matrix products  45.5 us (5%)
  between operations  26.8 us (3%)
    ppermute x56, waiting for transfers between devices, broadcast(): held = lax.ppermute(send, 'row', pairs)  203 us
    all_to_all x2, blocking collectives, body(): lax.all_to_all(chunk, 'row', split_axis=2, concat_axis=1, tiled=True)  197 us
    all_gather x2, waiting for transfers between devices, body(): lax.all_gather(by_row, 'freq', axis=1, tiled=True).astype(jnp.float32)  73.1 us
    ppermute x56, starting transfers between devices, broadcast(): held = lax.ppermute(send, 'row', pairs)  59.9 us
    convert_element_type x1, other arithmetic, to_bf16(): lax.reduce_precision(value, exponent_bits=8, mantissa_bits=7)  44 us
    unnamed x84, local copies, waits for them, and re-layouts  38.6 us
    select_n x56, other arithmetic, broadcast(): jnp.where(distance[p] == 0, own[p][:, min(step, chunks - 1)], held[p])  35.4 us
    slice x2, local copies, waits for them, and re-layouts, body(): gathered[0]  34.5 us
  transfers between devices with their start and end apart: 58, of which 36 were waited for; matrix products, arithmetic and copies ran while one was open for 12% of the time, Pallas kernels for 0%

profile of v3, /device:TPU:0, one launch (start us, length us, event | category | flops | bytes accessed | tf_op | source)
XLA Modules:
  0.0 866.2 jit_solution(1541536966394024368)
XLA Ops:
  13.2 11.2 %copy.353 = bf16[2,128,8192]{1,0,2:T(2,128)(2,1)} copy(bf16[2,128,8192]{2,1,0:T(8,128)(2,1)} %get-tuple-element.23) | data formatting | bytes 8388608
  24.4 100.4 %all_to_all.36 = bf16[2,128,8192]{1,0,2:T(2,128)(2,1)S(1)} all-to-all(bf16[2,128,8192]{1,0,2:T(2,128)(2,1)} %copy.353), channel_id=1, replica_groups=mesh['freq'=4,'row'=8] {'row'}, dimensions={2} | all-to-all | bytes 8388608 | tf_op jit(solution)/shard_map/all_to_all | solution.py:87
  127.4 6.3 copy.300
  133.7 11.4 %copy.352 = bf16[2,128,8192]{1,0,2:T(2,128)(2,1)} copy(bf16[2,128,8192]{2,1,0:T(8,128)(2,1)} %get-tuple-element.22) | data formatting | bytes 8388608
  145.2 96.5 %all_to_all.37 = bf16[2,128,8192]{1,0,2:T(2,128)(2,1)S(1)} all-to-all(bf16[2,128,8192]{1,0,2:T(2,128)(2,1)} %copy.352), channel_id=1, replica_groups=mesh['freq'=4,'row'=8] {'row'}, dimensions={2} | all-to-all | bytes 8388608 | tf_op jit(solution)/shard_map/all_to_all | solution.py:87
  244.2 6.2 copy.297
  264.8 17.4 %fusion.66 = (f32[1,4096,1024]{2,1,0:T(8,128)}, f32[1,4096,1024]{2,1,0:T(8,128)}) fusion(bf16[2,4096,1024]{2,1,0:T(8,128)(2,1)} %all-gather.5.cloned.1.call-done), kind=kLoop, calls=%fused_computation.213 | loop fusion | bytes 67108864 | tf_op jit(solution)/shard_map/slice | solution.py:90
  282.3 73.1 %all-gather.3.cloned.1.call-done = bf16[2,4096,1024]{2,1,0:T(8,128)(2,1)} async-done(((bf16[2,1024,1024]{2,1,0:T(8,128)(2,1)}), bf16[2,4096,1024]{2,1,0:T(8,128)(2,1)}) %all-gather.3.cloned.1.call-update) | async-done | bytes 16777232 | tf_op jit(solution)/shard_map/all_gather | solution.py:88
  355.3 17.0 %fusion.65 = (f32[1,4096,1024]{2,1,0:T(8,128)}, f32[1,4096,1024]{2,1,0:T(8,128)}) fusion(bf16[2,4096,1024]{2,1,0:T(8,128)(2,1)} %all-gather.3.cloned.1.call-done), kind=kLoop, calls=%fused_computation.212 | loop fusion | bytes 67108864 | tf_op jit(solution)/shard_map/slice | solution.py:90
  372.4 44.0 %reduce-precision_convert_fusion.1 = (bf16[2,32,1,128,1024]{4,3,2,1,0:T(8,128)(2,1)}, bf16[2,32,1,128,1024]{4,3,2,1,0:T(8,128)(2,1)}) fusion(bf16[2,32,2,128,1024]{4,3,2,1,0:T(8,128)(2,1)} %bitcast.452, f32[32,128,1024]{2,1,0:T(8,128)} %bitcast.383, f32[2]{0:T(128)S(1)} %get-tuple-element.3, f32[32,128,1024]{2,1,0:T(8,128)} %bitcast.382, ...), kind=kLoop, calls=%fused_computation.3 | loop fusion | flops 134217728 | bytes 134217744 | tf_op jit(solution)/shard_map/convert_element_type | solution.py:67
  416.3 23.0 %pad_maximum_fusion = bf16[2,32,2,128,1024]{4,3,2,1,0:T(8,128)(2,1)} fusion(bf16[2,32,1,128,1024]{4,3,2,1,0:T(8,128)(2,1)} %get-tuple-element.9, bf16[2,32,1,128,1024]{4,3,2,1,0:T(8,128)(2,1)} %get-tuple-element.8), kind=kLoop, calls=%fused_computation | loop fusion | flops 16777216 | bytes 67108864 | tf_op jit(solution)/shard_map/stack | solution.py:93
  439.3 6.6 constant_dynamic-slice_fusion.4
  453.6 7.1 collective-permute-done
  463.1 10.5 %collective-permute-done.42 = bf16[2,512,256]{2,1,0:T(8,128)(2,1)S(1)} collective-permute-done((bf16[2,512,256]{2,1,0:T(8,128)(2,1)S(1)}, bf16[2,512,256]{2,1,0:T(8,128)(2,1)S(1)}, u32[]{:S(2)}, u32[]{:S(2)}) %collective-permute-start.42) | collective-permute-done | bytes 524320 | tf_op jit(solution)/shard_map/ppermute | solution.py:52
  477.1 6.1 collective-permute-done.1
  485.6 10.5 %collective-permute-done.43 = bf16[2,512,256]{2,1,0:T(8,128)(2,1)S(1)} collective-permute-done((bf16[2,512,256]{2,1,0:T(8,128)(2,1)S(1)}, bf16[2,512,256]{2,1,0:T(8,128)(2,1)S(1)}, u32[]{:S(2)}, u32[]{:S(2)}) %collective-permute-start.43) | collective-permute-done | bytes 524320 | tf_op jit(solution)/shard_map/ppermute | solution.py:52
  508.1 10.5 %collective-permute-done.44 = bf16[2,512,256]{2,1,0:T(8,128)(2,1)S(1)} collective-permute-done((bf16[2,512,256]{2,1,0:T(8,128)(2,1)S(1)}, bf16[2,512,256]{2,1,0:T(8,128)(2,1)S(1)}, u32[]{:S(2)}, u32[]{:S(2)}) %collective-permute-start.44) | collective-permute-done | bytes 524320 | tf_op jit(solution)/shard_map/ppermute | solution.py:52
  530.6 10.5 %collective-permute-done.45 = bf16[2,512,256]{2,1,0:T(8,128)(2,1)S(1)} collective-permute-done((bf16[2,512,256]{2,1,0:T(8,128)(2,1)S(1)}, bf16[2,512,256]{2,1,0:T(8,128)(2,1)S(1)}, u32[]{:S(2)}, u32[]{:S(2)}) %collective-permute-start.45) | collective-permute-done | bytes 524320 | tf_op jit(solution)/shard_map/ppermute | solution.py:52
  544.4 6.2 collective-permute-done.4
  553.0 10.5 %collective-permute-done.46 = bf16[2,512,256]{2,1,0:T(8,128)(2,1)S(1)} collective-permute-done((bf16[2,512,256]{2,1,0:T(8,128)(2,1)S(1)}, bf16[2,512,256]{2,1,0:T(8,128)(2,1)S(1)}, u32[]{:S(2)}, u32[]{:S(2)}) %collective-permute-start.46) | collective-permute-done | bytes 524320 | tf_op jit(solution)/shard_map/ppermute | solution.py:52
  575.5 10.5 %collective-permute-done.47 = bf16[2,512,256]{2,1,0:T(8,128)(2,1)S(1)} collective-permute-done((bf16[2,512,256]{2,1,0:T(8,128)(2,1)S(1)}, bf16[2,512,256]{2,1,0:T(8,128)(2,1)S(1)}, u32[]{:S(2)}, u32[]{:S(2)}) %collective-permute-start.47) | collective-permute-done | bytes 524320 | tf_op jit(solution)/shard_map/ppermute | solution.py:52
  599.0 9.5 %collective-permute-done.48 = bf16[2,512,256]{2,1,0:T(8,128)(2,1)S(1)} collective-permute-done((bf16[2,512,256]{2,1,0:T(8,128)(2,1)S(1)}, bf16[2,512,256]{2,1,0:T(8,128)(2,1)S(1)}, u32[]{:S(2)}, u32[]{:S(2)}) %collective-permute-start.48) | collective-permute-done | bytes 524320 | tf_op jit(solution)/shard_map/ppermute | solution.py:52
  622.4 8.5 collective-permute-done.49
  644.9 8.5 collective-permute-done.50
  667.4 8.5 collective-permute-done.51
  689.8 8.5 collective-permute-done.52
  712.3 8.5 collective-permute-done.53
  735.5 7.8 collective-permute-done.54
  779.7 7.3 fusion.61
  790.7 22.8 %convert_bitcast_fusion.1 = bf16[1,1,1024,8192]{3,2,1,0:T(8,128)(2,1)} fusion(bf16[8192,256]{1,0:T(8,128)(2,1)} %get-tuple-element.33, bf16[8192,256]{1,0:T(8,128)(2,1)} %get-tuple-element.31, bf16[8192,256]{1,0:T(8,128)(2,1)} %get-tuple-element.4, bf16[8192,256]{1,0:T(8,128)(2,1)} %get-tuple-element.32, bf16[256,1024]{1,0:T(8,128)(2,1)S(1)} %get-tuple-element.12, ...), kind=kOutput, calls=%fused_computation.21 | convolution fusion | flops 17263755264 | bytes 35651584 | tf_op jit(solution)/shard_map/dot_general | solution.py:113
  813.5 22.7 %convert_bitcast_fusion = bf16[1,1,1024,8192]{3,2,1,0:T(8,128)(2,1)} fusion(bf16[8192,256]{1,0:T(8,128)(2,1)} %get-tuple-element.31, bf16[8192,256]{1,0:T(8,128)(2,1)} %get-tuple-element.34, bf16[8192,256]{1,0:T(8,128)(2,1)} %get-tuple-element.32, bf16[8192,256]{1,0:T(8,128)(2,1)} %get-tuple-element.5, bf16[256,1024]{1,0:T(8,128)(2,1)S(1)} %get-tuple-element.12, ...), kind=kOutput, calls=%fused_computation.20 | convolution fusion | flops 17263755264 | bytes 35651584 | tf_op jit(solution)/shard_map/dot_general | solution.py:114
  836.2 23.0 %pad_maximum_fusion.1 = bf16[1,2,1024,8192]{3,2,1,0:T(8,128)(2,1)} fusion(bf16[1,1,1024,8192]{3,2,1,0:T(8,128)(2,1)} %convert_bitcast_fusion, bf16[1,1,1024,8192]{3,2,1,0:T(8,128)(2,1)} %convert_bitcast_fusion.1), kind=kLoop, calls=%fused_computation.1 | loop fusion | flops 16777216 | bytes 67108864 | tf_op jit(solution)/shard_map/stack | solution.py:115
  (261 shorter events, 208.5 us)
Async XLA Ops:
  7.2 257.7 %all-gather.5.cloned.1.call-start = ((), (), s32[]{:S(2)}) async-start(), calls=%async_computation.3 | async-start | bytes 20971520 | tf_op jit(solution)/shard_map/all_gather | solution.py:88
  133.7 221.6 %all-gather.3.cloned.1.call-start = ((), (), s32[]{:S(2)}) async-start(), calls=%async_computation.2 | async-start | bytes 20971520 | tf_op jit(solution)/shard_map/all_gather | solution.py:88
  448.3 25.4 %collective-permute-start.42 = (bf16[2,512,256]{2,1,0:T(8,128)(2,1)S(1)}, bf16[2,512,256]{2,1,0:T(8,128)(2,1)S(1)}, u32[]{:S(2)}, u32[]{:S(2)}) collective-permute-start(bf16[2,512,256]{2,1,0:T(8,128)(2,1)S(1)} %fusion.32), channel_id=1, source_target_pairs={{2,0},{4,2},{6,4},{7,6},{5,7},{3,5},{1,3},{0,1},{10,8},{12,10},{14... | collective-permute-start | bytes 1572872 | tf_op jit(solution)/shard_map/ppermute | solution.py:52
  449.9 24.5 %collective-permute-start.28 = (bf16[2,512,256]{2,1,0:T(8,128)(2,1)S(1)}, bf16[2,512,256]{2,1,0:T(8,128)(2,1)S(1)}, u32[]{:S(2)}, u32[]{:S(2)}) collective-permute-start(bf16[2,512,256]{2,1,0:T(8,128)(2,1)S(1)} %fusion.39), channel_id=1, source_target_pairs={{0,2},{2,4},{4,6},{6,7},{7,5},{5,3},{3,1},{1,0},{8,10},{10,12},{12... | collective-permute-start | bytes 1572872 | tf_op jit(solution)/shard_map/ppermute | solution.py:52
  460.8 22.4 %collective-permute-start.1 = (bf16[2,512,256]{2,1,0:T(8,128)(2,1)S(1)}, bf16[2,512,256]{2,1,0:T(8,128)(2,1)S(1)}, u32[]{:S(2)}, u32[]{:S(2)}) collective-permute-start(bf16[2,512,256]{2,1,0:T(8,128)(2,1)S(1)} %fusion.52), channel_id=1, source_target_pairs={{0,2},{2,4},{4,6},{6,7},{7,5},{5,3},{3,1},{1,0},{8,10},{10,12},{12... | collective-permute-start | bytes 1572872 | tf_op jit(solution)/shard_map/ppermute | solution.py:52
  462.6 22.3 %collective-permute-start.15 = (bf16[2,512,256]{2,1,0:T(8,128)(2,1)S(1)}, bf16[2,512,256]{2,1,0:T(8,128)(2,1)S(1)}, u32[]{:S(2)}, u32[]{:S(2)}) collective-permute-start(bf16[2,512,256]{2,1,0:T(8,128)(2,1)S(1)} %fusion.45), channel_id=1, source_target_pairs={{2,0},{4,2},{6,4},{7,6},{5,7},{3,5},{1,3},{0,1},{10,8},{12,10},{14... | collective-permute-start | bytes 1572872 | tf_op jit(solution)/shard_map/ppermute | solution.py:52
  473.8 22.3 %collective-permute-start.43 = (bf16[2,512,256]{2,1,0:T(8,128)(2,1)S(1)}, bf16[2,512,256]{2,1,0:T(8,128)(2,1)S(1)}, u32[]{:S(2)}, u32[]{:S(2)}) collective-permute-start(bf16[2,512,256]{2,1,0:T(8,128)(2,1)S(1)} %fusion.31), channel_id=1, source_target_pairs={{2,0},{4,2},{6,4},{7,6},{5,7},{3,5},{1,3},{0,1},{10,8},{12,10},{14... | collective-permute-start | bytes 1572872 | tf_op jit(solution)/shard_map/ppermute | solution.py:52
  474.5 22.3 %collective-permute-start.29 = (bf16[2,512,256]{2,1,0:T(8,128)(2,1)S(1)}, bf16[2,512,256]{2,1,0:T(8,128)(2,1)S(1)}, u32[]{:S(2)}, u32[]{:S(2)}) collective-permute-start(bf16[2,512,256]{2,1,0:T(8,128)(2,1)S(1)} %fusion.38), channel_id=1, source_target_pairs={{0,2},{2,4},{4,6},{6,7},{7,5},{5,3},{3,1},{1,0},{8,10},{10,12},{12... | collective-permute-start | bytes 1572872 | tf_op jit(solution)/shard_map/ppermute | solution.py:52
  483.3 22.4 %collective-permute-start.2 = (bf16[2,512,256]{2,1,0:T(8,128)(2,1)S(1)}, bf16[2,512,256]{2,1,0:T(8,128)(2,1)S(1)}, u32[]{:S(2)}, u32[]{:S(2)}) collective-permute-start(bf16[2,512,256]{2,1,0:T(8,128)(2,1)S(1)} %fusion.51), channel_id=1, source_target_pairs={{0,2},{2,4},{4,6},{6,7},{7,5},{5,3},{3,1},{1,0},{8,10},{10,12},{12... | collective-permute-start | bytes 1572872 | tf_op jit(solution)/shard_map/ppermute | solution.py:52
  485.0 22.3 %collective-permute-start.16 = (bf16[2,512,256]{2,1,0:T(8,128)(2,1)S(1)}, bf16[2,512,256]{2,1,0:T(8,128)(2,1)S(1)}, u32[]{:S(2)}, u32[]{:S(2)}) collective-permute-start(bf16[2,512,256]{2,1,0:T(8,128)(2,1)S(1)} %fusion.44), channel_id=1, source_target_pairs={{2,0},{4,2},{6,4},{7,6},{5,7},{3,5},{1,3},{0,1},{10,8},{12,10},{14... | collective-permute-start | bytes 1572872 | tf_op jit(solution)/shard_map/ppermute | solution.py:52
  496.3 22.3 %collective-permute-start.44 = (bf16[2,512,256]{2,1,0:T(8,128)(2,1)S(1)}, bf16[2,512,256]{2,1,0:T(8,128)(2,1)S(1)}, u32[]{:S(2)}, u32[]{:S(2)}) collective-permute-start(bf16[2,512,256]{2,1,0:T(8,128)(2,1)S(1)} %fusion.30), channel_id=1, source_target_pairs={{2,0},{4,2},{6,4},{7,6},{5,7},{3,5},{1,3},{0,1},{10,8},{12,10},{14... | collective-permute-start | bytes 1572872 | tf_op jit(solution)/shard_map/ppermute | solution.py:52
  497.0 22.3 %collective-permute-start.30 = (bf16[2,512,256]{2,1,0:T(8,128)(2,1)S(1)}, bf16[2,512,256]{2,1,0:T(8,128)(2,1)S(1)}, u32[]{:S(2)}, u32[]{:S(2)}) collective-permute-start(bf16[2,512,256]{2,1,0:T(8,128)(2,1)S(1)} %fusion.37), channel_id=1, source_target_pairs={{0,2},{2,4},{4,6},{6,7},{7,5},{5,3},{3,1},{1,0},{8,10},{10,12},{12... | collective-permute-start | bytes 1572872 | tf_op jit(solution)/shard_map/ppermute | solution.py:52
  505.7 22.4 %collective-permute-start.3 = (bf16[2,512,256]{2,1,0:T(8,128)(2,1)S(1)}, bf16[2,512,256]{2,1,0:T(8,128)(2,1)S(1)}, u32[]{:S(2)}, u32[]{:S(2)}) collective-permute-start(bf16[2,512,256]{2,1,0:T(8,128)(2,1)S(1)} %fusion.50), channel_id=1, source_target_pairs={{0,2},{2,4},{4,6},{6,7},{7,5},{5,3},{3,1},{1,0},{8,10},{10,12},{12... | collective-permute-start | bytes 1572872 | tf_op jit(solution)/shard_map/ppermute | solution.py:52
  507.5 22.3 %collective-permute-start.17 = (bf16[2,512,256]{2,1,0:T(8,128)(2,1)S(1)}, bf16[2,512,256]{2,1,0:T(8,128)(2,1)S(1)}, u32[]{:S(2)}, u32[]{:S(2)}) collective-permute-start(bf16[2,512,256]{2,1,0:T(8,128)(2,1)S(1)} %fusion.43), channel_id=1, source_target_pairs={{2,0},{4,2},{6,4},{7,6},{5,7},{3,5},{1,3},{0,1},{10,8},{12,10},{14... | collective-permute-start | bytes 1572872 | tf_op jit(solution)/shard_map/ppermute | solution.py:52
  518.7 22.3 %collective-permute-start.45 = (bf16[2,512,256]{2,1,0:T(8,128)(2,1)S(1)}, bf16[2,512,256]{2,1,0:T(8,128)(2,1)S(1)}, u32[]{:S(2)}, u32[]{:S(2)}) collective-permute-start(bf16[2,512,256]{2,1,0:T(8,128)(2,1)S(1)} %fusion.29), channel_id=1, source_target_pairs={{2,0},{4,2},{6,4},{7,6},{5,7},{3,5},{1,3},{0,1},{10,8},{12,10},{14... | collective-permute-start | bytes 1572872 | tf_op jit(solution)/shard_map/ppermute | solution.py:52
  519.5 22.3 %collective-permute-start.31 = (bf16[2,512,256]{2,1,0:T(8,128)(2,1)S(1)}, bf16[2,512,256]{2,1,0:T(8,128)(2,1)S(1)}, u32[]{:S(2)}, u32[]{:S(2)}) collective-permute-start(bf16[2,512,256]{2,1,0:T(8,128)(2,1)S(1)} %fusion.36), channel_id=1, source_target_pairs={{0,2},{2,4},{4,6},{6,7},{7,5},{5,3},{3,1},{1,0},{8,10},{10,12},{12... | collective-permute-start | bytes 1572872 | tf_op jit(solution)/shard_map/ppermute | solution.py:52
  528.2 22.4 %collective-permute-start.4 = (bf16[2,512,256]{2,1,0:T(8,128)(2,1)S(1)}, bf16[2,512,256]{2,1,0:T(8,128)(2,1)S(1)}, u32[]{:S(2)}, u32[]{:S(2)}) collective-permute-start(bf16[2,512,256]{2,1,0:T(8,128)(2,1)S(1)} %fusion.49), channel_id=1, source_target_pairs={{0,2},{2,4},{4,6},{6,7},{7,5},{5,3},{3,1},{1,0},{8,10},{10,12},{12... | collective-permute-start | bytes 1572872 | tf_op jit(solution)/shard_map/ppermute | solution.py:52
  530.0 22.3 %collective-permute-start.18 = (bf16[2,512,256]{2,1,0:T(8,128)(2,1)S(1)}, bf16[2,512,256]{2,1,0:T(8,128)(2,1)S(1)}, u32[]{:S(2)}, u32[]{:S(2)}) collective-permute-start(bf16[2,512,256]{2,1,0:T(8,128)(2,1)S(1)} %fusion.42), channel_id=1, source_target_pairs={{2,0},{4,2},{6,4},{7,6},{5,7},{3,5},{1,3},{0,1},{10,8},{12,10},{14... | collective-permute-start | bytes 1572872 | tf_op jit(solution)/shard_map/ppermute | solution.py:52
  541.2 22.3 %collective-permute-start.46 = (bf16[2,512,256]{2,1,0:T(8,128)(2,1)S(1)}, bf16[2,512,256]{2,1,0:T(8,128)(2,1)S(1)}, u32[]{:S(2)}, u32[]{:S(2)}) collective-permute-start(bf16[2,512,256]{2,1,0:T(8,128)(2,1)S(1)} %fusion.28), channel_id=1, source_target_pairs={{2,0},{4,2},{6,4},{7,6},{5,7},{3,5},{1,3},{0,1},{10,8},{12,10},{14... | collective-permute-start | bytes 1572872 | tf_op jit(solution)/shard_map/ppermute | solution.py:52
  542.0 22.3 %collective-permute-start.32 = (bf16[2,512,256]{2,1,0:T(8,128)(2,1)S(1)}, bf16[2,512,256]{2,1,0:T(8,128)(2,1)S(1)}, u32[]{:S(2)}, u32[]{:S(2)}) collective-permute-start(bf16[2,512,256]{2,1,0:T(8,128)(2,1)S(1)} %fusion.35), channel_id=1, source_target_pairs={{0,2},{2,4},{4,6},{6,7},{7,5},{5,3},{3,1},{1,0},{8,10},{10,12},{12... | collective-permute-start | bytes 1572872 | tf_op jit(solution)/shard_map/ppermute | solution.py:52
  550.7 22.4 %collective-permute-start.5 = (bf16[2,512,256]{2,1,0:T(8,128)(2,1)S(1)}, bf16[2,512,256]{2,1,0:T(8,128)(2,1)S(1)}, u32[]{:S(2)}, u32[]{:S(2)}) collective-permute-start(bf16[2,512,256]{2,1,0:T(8,128)(2,1)S(1)} %fusion.48), channel_id=1, source_target_pairs={{0,2},{2,4},{4,6},{6,7},{7,5},{5,3},{3,1},{1,0},{8,10},{10,12},{12... | collective-permute-start | bytes 1572872 | tf_op jit(solution)/shard_map/ppermute | solution.py:52
  552.4 22.3 %collective-permute-start.19 = (bf16[2,512,256]{2,1,0:T(8,128)(2,1)S(1)}, bf16[2,512,256]{2,1,0:T(8,128)(2,1)S(1)}, u32[]{:S(2)}, u32[]{:S(2)}) collective-permute-start(bf16[2,512,256]{2,1,0:T(8,128)(2,1)S(1)} %fusion.41), channel_id=1, source_target_pairs={{2,0},{4,2},{6,4},{7,6},{5,7},{3,5},{1,3},{0,1},{10,8},{12,10},{14... | collective-permute-start | bytes 1572872 | tf_op jit(solution)/shard_map/ppermute | solution.py:52
  563.7 22.3 %collective-permute-start.47 = (bf16[2,512,256]{2,1,0:T(8,128)(2,1)S(1)}, bf16[2,512,256]{2,1,0:T(8,128)(2,1)S(1)}, u32[]{:S(2)}, u32[]{:S(2)}) collective-permute-start(bf16[2,512,256]{2,1,0:T(8,128)(2,1)S(1)} %fusion.27), channel_id=1, source_target_pairs={{2,0},{4,2},{6,4},{7,6},{5,7},{3,5},{1,3},{0,1},{10,8},{12,10},{14... | collective-permute-start | bytes 1572872 | tf_op jit(solution)/shard_map/ppermute | solution.py:52
  564.4 22.3 %collective-permute-start.33 = (bf16[2,512,256]{2,1,0:T(8,128)(2,1)S(1)}, bf16[2,512,256]{2,1,0:T(8,128)(2,1)S(1)}, u32[]{:S(2)}, u32[]{:S(2)}) collective-permute-start(bf16[2,512,256]{2,1,0:T(8,128)(2,1)S(1)} %fusion.34), channel_id=1, source_target_pairs={{0,2},{2,4},{4,6},{6,7},{7,5},{5,3},{3,1},{1,0},{8,10},{10,12},{12... | collective-permute-start | bytes 1572872 | tf_op jit(solution)/shard_map/ppermute | solution.py:52
  573.1 22.4 %collective-permute-start.6 = (bf16[2,512,256]{2,1,0:T(8,128)(2,1)S(1)}, bf16[2,512,256]{2,1,0:T(8,128)(2,1)S(1)}, u32[]{:S(2)}, u32[]{:S(2)}) collective-permute-start(bf16[2,512,256]{2,1,0:T(8,128)(2,1)S(1)} %fusion.47), channel_id=1, source_target_pairs={{0,2},{2,4},{4,6},{6,7},{7,5},{5,3},{3,1},{1,0},{8,10},{10,12},{12... | collective-permute-start | bytes 1572872 | tf_op jit(solution)/shard_map/ppermute | solution.py:52
  574.9 22.3 %collective-permute-start.20 = (bf16[2,512,256]{2,1,0:T(8,128)(2,1)S(1)}, bf16[2,512,256]{2,1,0:T(8,128)(2,1)S(1)}, u32[]{:S(2)}, u32[]{:S(2)}) collective-permute-start(bf16[2,512,256]{2,1,0:T(8,128)(2,1)S(1)} %fusion.40), channel_id=1, source_target_pairs={{2,0},{4,2},{6,4},{7,6},{5,7},{3,5},{1,3},{0,1},{10,8},{12,10},{14... | collective-permute-start | bytes 1572872 | tf_op jit(solution)/shard_map/ppermute | solution.py:52
  586.1 22.3 %collective-permute-start.48 = (bf16[2,512,256]{2,1,0:T(8,128)(2,1)S(1)}, bf16[2,512,256]{2,1,0:T(8,128)(2,1)S(1)}, u32[]{:S(2)}, u32[]{:S(2)}) collective-permute-start(bf16[2,512,256]{2,1,0:T(8,128)(2,1)S(1)} %fusion.26), channel_id=1, source_target_pairs={{2,0},{4,2},{6,4},{7,6},{5,7},{3,5},{1,3},{0,1},{10,8},{12,10},{14... | collective-permute-start | bytes 1572872 | tf_op jit(solution)/shard_map/ppermute | solution.py:52
  586.9 23.3 %collective-permute-start.34 = (bf16[2,512,256]{2,1,0:T(8,128)(2,1)S(1)}, bf16[2,512,256]{2,1,0:T(8,128)(2,1)S(1)}, u32[]{:S(2)}, u32[]{:S(2)}) collective-permute-start(bf16[2,512,256]{2,1,0:T(8,128)(2,1)S(1)} %fusion.33), channel_id=1, source_target_pairs={{0,2},{2,4},{4,6},{6,7},{7,5},{5,3},{3,1},{1,0},{8,10},{10,12},{12... | collective-permute-start | bytes 1572872 | tf_op jit(solution)/shard_map/ppermute | solution.py:52
  595.6 22.4 %collective-permute-start.7 = (bf16[2,512,256]{2,1,0:T(8,128)(2,1)S(1)}, bf16[2,512,256]{2,1,0:T(8,128)(2,1)S(1)}, u32[]{:S(2)}, u32[]{:S(2)}) collective-permute-start(bf16[2,512,256]{2,1,0:T(8,128)(2,1)S(1)} %broadcast_select_fusion.27), channel_id=1, source_target_pairs={{0,2},{2,4},{4,6},{6,7},{7,5},{5,3},{3,1},{1,0},{8,10},{10,12},{12... | collective-permute-start | bytes 1572872 | tf_op jit(solution)/shard_map/ppermute | solution.py:52
  598.4 22.3 %collective-permute-start.21 = (bf16[2,512,256]{2,1,0:T(8,128)(2,1)S(1)}, bf16[2,512,256]{2,1,0:T(8,128)(2,1)S(1)}, u32[]{:S(2)}, u32[]{:S(2)}) collective-permute-start(bf16[2,512,256]{2,1,0:T(8,128)(2,1)S(1)} %broadcast_select_fusion.20), channel_id=1, source_target_pairs={{2,0},{4,2},{6,4},{7,6},{5,7},{3,5},{1,3},{0,1},{10,8},{12,10},{14... | collective-permute-start | bytes 1572872 | tf_op jit(solution)/shard_map/ppermute | solution.py:52
  732.3 42.7 %collective-permute-start.13 = (bf16[2,512,256]{2,1,0:T(8,128)(2,1)}, bf16[2,512,256]{2,1,0:T(8,128)(2,1)}, u32[]{:S(2)}, u32[]{:S(2)}) collective-permute-start(bf16[2,512,256]{2,1,0:T(8,128)(2,1)} %broadcast_select_fusion.21), channel_id=1, source_target_pairs={{0,2},{2,4},{4,6},{6,7},{7,5},{5,3},{3,1},{1,0},{8,10},{10,12},{12... | collective-permute-start | bytes 1572872 | tf_op jit(solution)/shard_map/ppermute | solution.py:52
  746.2 22.2 %collective-permute-start.41 = (bf16[2,512,256]{2,1,0:T(8,128)(2,1)S(1)}, bf16[2,512,256]{2,1,0:T(8,128)(2,1)S(1)}, u32[]{:S(2)}, u32[]{:S(2)}) collective-permute-start(bf16[2,512,256]{2,1,0:T(8,128)(2,1)S(1)} %broadcast_select_fusion.7), channel_id=1, source_target_pairs={{0,2},{2,4},{4,6},{6,7},{7,5},{5,3},{3,1},{1,0},{8,10},{10,12},{12... | collective-permute-start | bytes 1572872 | tf_op jit(solution)/shard_map/ppermute | solution.py:52
  (41 other events, 1197.8 us)
Sparse Core Ops, SparseCore 0:
  133.8 104.9 all-gather.4
  250.5 104.7 all-gather.2

commit v4 on v2

--- a/solution.py
+++ b/solution.py
@@ -10,11 +10,52 @@
 STEPS = 2
 BLOCK_START = 1022
 PIECES = 2
+RING_CHUNKS = 16
 
 
-def spread(value, axis, source):
-    kept = jnp.where(lax.axis_index(axis) == source, value, 0).astype(value.dtype)
-    return lax.psum(kept, axis)
+def ring_order(count):
+    evens = list(range(0, count, 2))
+    odds = list(range(1, count, 2))[::-1]
+    return evens + odds
+
+
+def broadcast(value, owners, chunks):
+    count = lax.axis_size("row")
+    order = ring_order(count)
+    place = [0] * count
+    for position, member in enumerate(order):
+        place[member] = position
+    place_of = jnp.array(place, jnp.int32)
+    mine = place_of[lax.axis_index("row")]
+    owner_place = place_of[owners]
+    forward = [(order[i], order[(i + 1) % count]) for i in range(count)]
+    backward = [(order[(i + 1) % count], order[i]) for i in range(count)]
+    steps = chunks + count - 2
+    lead = (1,) * (value.ndim - 1)
+    halves = []
+    for direction, pairs in ((0, forward), (1, backward)):
+        if direction == 0:
+            distance = (mine - owner_place) % count
+        else:
+            distance = (owner_place - mine) % count
+        half = value.shape[2] // 2
+        part = value[:, :, direction * half:(direction + 1) * half]
+        own = part.reshape(*part.shape[:2], chunks, half // chunks, *part.shape[3:])
+        is_owner = (distance == 0).reshape(-1, *lead)
+        held = jnp.zeros_like(own[:, :, 0])
+        arrived = []
+        for step in range(steps):
+            send = jnp.where(is_owner, own[:, :, min(step, chunks - 1)], held)
+            held = lax.ppermute(send, "row", pairs)
+            arrived.append(held)
+        stacked = jnp.stack(arrived, axis=2)
+        picked = []
+        for p in range(value.shape[0]):
+            start = jnp.maximum(distance[p] - 1, 0)
+            picked.append(lax.dynamic_slice_in_dim(stacked[p], start, chunks, 1))
+        picked = jnp.where(is_owner[..., None], own, jnp.stack(picked))
+        halves.append(picked.reshape(*picked.shape[:2], -1, *picked.shape[4:]))
+    return jnp.concatenate(halves, axis=2)
 
 
 def to_bf16(value):
@@ -35,28 +76,40 @@
     piece = shots_local // PIECES
     groups = freq_count * row_count
     prior_blocks = prior[0].reshape(2, groups, PIECES, piece, block_rows)
+    panels_each = block_rows // PANEL
+    offsets = [panels[p] % panels_each * PANEL for p in range(STEPS)]
+
+    def transform(samples):
+        total = weights[:, 0, None, None] * samples[0] + weights[:, 1, None, None] * samples[1]
+        return lax.reduce_precision(total, exponent_bits=8, mantissa_bits=7)
+
     parts = []
+    panel_samples = [[] for _ in range(STEPS)]
     for index in range(PIECES):
         chunk = traces[:, index * piece:(index + 1) * piece, :]
         by_row = lax.all_to_all(chunk, "row", split_axis=2, concat_axis=1, tiled=True)
-        gathered = lax.all_gather(by_row, "freq", axis=1, tiled=True).astype(jnp.float32)
-        gathered = gathered.reshape(sample_count, groups, piece, block_rows)
-        transformed = weights[:, 0, None, None, None] * gathered[0] + weights[:, 1, None, None, None] * gathered[1]
-        transformed = lax.reduce_precision(transformed, exponent_bits=8, mantissa_bits=7)
-        parts.append(to_bf16(prior_blocks[:, :, index].astype(jnp.float32) + transformed))
+        gathered = lax.all_gather(by_row, "freq", axis=1, tiled=True)
+        for p in range(STEPS):
+            picked = lax.dynamic_slice_in_dim(gathered, offsets[p], PANEL, 2)
+            panel_samples[p].append(picked.reshape(sample_count, groups, piece, PANEL))
+        samples = gathered.astype(jnp.float32).reshape(sample_count, groups * piece, block_rows)
+        blocks = prior_blocks[:, :, index].reshape(2, groups * piece, block_rows)
+        parts.append(to_bf16(blocks.astype(jnp.float32) + transform(samples)).reshape(2, groups, piece, block_rows))
     spectrum = jnp.stack(parts, axis=2).reshape(2, receivers, block_rows)
-    panels_each = block_rows // PANEL
+    own_panels = []
+    for p in range(STEPS):
+        samples = jnp.stack(panel_samples[p], axis=2).reshape(sample_count, receivers, PANEL).astype(jnp.float32)
+        prior_rows = lax.dynamic_slice_in_dim(prior[0], offsets[p], PANEL, 2).astype(jnp.float32)
+        own_panels.append(to_bf16(prior_rows + transform(samples)))
+    owners = jnp.stack([panels[p] // panels_each for p in range(STEPS)])
+    rights = broadcast(jnp.stack(own_panels), owners, RING_CHUNKS)
     lefts = []
+    for p in range(STEPS):
+        left = lax.dynamic_slice_in_dim(spectrum, panels[p] * PANEL, PANEL, 1)
+        lefts += [left[0], left[1]]
     reals = []
     imags = []
-    for panel_step in range(STEPS):
-        chosen = panels[panel_step]
-        owner = chosen // panels_each
-        offset = chosen % panels_each * PANEL
-        own_rows = lax.dynamic_slice_in_dim(spectrum, offset, PANEL, 2)
-        right = spread(own_rows, "row", owner)
-        left = lax.dynamic_slice_in_dim(spectrum, chosen * PANEL, PANEL, 1)
-        lefts += [left[0], left[1]]
+    for right in rights:
         reals += [right[0], -right[1]]
         imags += [right[1], right[0]]
     left_all = jnp.concatenate(lefts, axis=0)

time: 1060 us -> 966 us (0.911)
  waiting for transfers between devices: 588 us -> 244 us
  other arithmetic: 106 us -> 210 us
  local copies, waits for them, and re-layouts: 100 us -> 188 us
  starting transfers between devices: 0.3 us -> 47.4 us
    psum x1 -> x0, waiting for transfers between devices: 508 us -> none  [spread(): return lax.psum(kept, axis)]
    ppermute x0 -> x44, waiting for transfers between devices: none -> 151 us  [broadcast(): held = lax.ppermute(send, 'row', pairs)]
    select_n x1 -> x47, other arithmetic: 12.4 us -> 60.5 us  [the longest x44 49.7 us: broadcast(): send = jnp.where(is_owner, own[:, :, min(step, chunks - 1)], held)]
    ppermute x0 -> x44, starting transfers between devices: none -> 47.4 us  [broadcast(): held = lax.ppermute(send, 'row', pairs)]
    slice x4 -> x9, local copies, waits for them, and re-layouts: 36 us -> 75.9 us  [the longest x4 54.5 us: transform(): samples[0]]
    unnamed x10 -> x80, local copies, waits for them, and re-layouts: 25.8 us -> 61.9 us
    dynamic_slice x0 -> x8, local copies, waits for them, and re-layouts: none -> 22 us  [the longest x1 11.1 us: body(): picked = lax.dynamic_slice_in_dim(gathered, offsets[p], PANEL, 2)]
    convert_element_type x1 -> x2, other arithmetic: 43.8 us -> 64.2 us  [to_bf16(): lax.reduce_precision(value, exponent_bits=8, mantissa_bits=7)]
  transfers between devices with their start and end apart: 3 -> 46, of which waited for: 2 -> 26; matrix products, arithmetic and copies ran while one was open for 4% -> 24% of each run, Pallas kernels for 0% -> 0%
where the time goes in v4:
time: 966 us; the launch traced here: 955 us
  waiting for transfers between devices  244 us (25%)
  other arithmetic  210 us (22%)
  blocking collectives  197 us (20%)
  local copies, waits for them, and re-layouts  188 us (19%)
  starting transfers between devices  47.4 us (5%)
  matrix products  45.6 us (5%)
  between operations  23.6 us (2%)
    all_to_all x2, blocking collectives, body(): lax.all_to_all(chunk, 'row', split_axis=2, concat_axis=1, tiled=True)  197 us
    ppermute x44, waiting for transfers between devices, broadcast(): held = lax.ppermute(send, 'row', pairs)  151 us
    all_gather x2, waiting for transfers between devices, body(): gathered = lax.all_gather(by_row, 'freq', axis=1, tiled=True)  92.5 us
    convert_element_type x2, other arithmetic, to_bf16(): lax.reduce_precision(value, exponent_bits=8, mantissa_bits=7)  64.2 us
    unnamed x80, local copies, waits for them, and re-layouts  61.9 us
    slice x4, local copies, waits for them, and re-layouts, transform(): samples[0]  54.5 us
    select_n x44, other arithmetic, broadcast(): send = jnp.where(is_owner, own[:, :, min(step, chunks - 1)], held)  49.7 us
    ppermute x44, starting transfers between devices, broadcast(): held = lax.ppermute(send, 'row', pairs)  47.4 us
  transfers between devices with their start and end apart: 46, of which 26 were waited for; matrix products, arithmetic and copies ran while one was open for 24% of the time, Pallas kernels for 0%

profile of v4, /device:TPU:0, one launch (start us, length us, event | category | flops | bytes accessed | tf_op | source)
XLA Modules:
  0.0 955.4 jit_solution(1270892214763760997)
XLA Ops:
  13.2 11.2 %copy.359 = bf16[2,128,8192]{1,0,2:T(2,128)(2,1)} copy(bf16[2,128,8192]{2,1,0:T(8,128)(2,1)} %get-tuple-element.42) | data formatting | bytes 8388608
  24.4 100.4 %all_to_all.36 = bf16[2,128,8192]{1,0,2:T(2,128)(2,1)S(1)} all-to-all(bf16[2,128,8192]{1,0,2:T(2,128)(2,1)} %copy.359), channel_id=1, replica_groups=mesh['freq'=4,'row'=8] {'row'}, dimensions={2} | all-to-all | bytes 8388608 | tf_op jit(solution)/shard_map/all_to_all | solution.py:90
  133.7 11.4 %copy.360 = bf16[2,128,8192]{1,0,2:T(2,128)(2,1)} copy(bf16[2,128,8192]{2,1,0:T(8,128)(2,1)} %get-tuple-element.43) | data formatting | bytes 8388608
  145.1 96.5 %all_to_all.37 = bf16[2,128,8192]{1,0,2:T(2,128)(2,1)S(1)} all-to-all(bf16[2,128,8192]{1,0,2:T(2,128)(2,1)} %copy.360), channel_id=1, replica_groups=mesh['freq'=4,'row'=8] {'row'}, dimensions={2} | all-to-all | bytes 8388608 | tf_op jit(solution)/shard_map/all_to_all | solution.py:90
  262.9 92.5 %all-gather.5.cloned.1.call-done = bf16[2,4096,1024]{2,1,0:T(8,128)(2,1)} async-done(((bf16[2,1024,1024]{2,1,0:T(8,128)(2,1)}), bf16[2,4096,1024]{2,1,0:T(8,128)(2,1)}) %all-gather.5.cloned.1.call-update) | async-done | bytes 16777232 | tf_op jit(solution)/shard_map/all_gather | solution.py:91
  355.3 11.1 %constant_dynamic-slice_fusion.5 = (bf16[2,4096,256]{2,1,0:T(8,128)(2,1)}, bf16[2,4096,256]{2,1,0:T(8,128)(2,1)S(1)}, bf16[2,4096,256]{2,1,0:T(8,128)(2,1)}, bf16[2,4096,256]{2,1,0:T(8,128)(2,1)}) fusion(bf16[2,4096,1024]{2,1,0:T(8,128)(2,1)} %all-gather.5.cloned.1.call-done, s32[]{:T(128)S(6)} %select_n.252, s32[]{:T(128)S(6)} %select_n.250, ...), kind=kLoop, calls=%fused_computation.178 | loop fusion | bytes 33554440 | tf_op jit(solution)/shard_map/dynamic_slice | solution.py:93
  366.4 9.5 maximum_convert_fusion
  375.9 11.1 %fusion.74 = (f32[1,32,2,128,256]{4,3,2,1,0:T(8,128)}, f32[1,32,2,128,256]{4,3,2,1,0:T(8,128)}) fusion(f32[2,32,2,128,256]{4,3,2,1,0:T(8,128)} %maximum_convert_fusion), kind=kLoop, calls=%fused_computation.216 | loop fusion | bytes 33554432 | tf_op jit(solution)/shard_map/slice | solution.py:83
  387.0 10.8 %maximum_convert_fusion.1 = f32[2,32,2,128,256]{4,3,2,1,0:T(8,128)} fusion(bf16[2,32,1,128,256]{4,3,2,1,0:T(8,128)(2,1)} %bitcast.473, bf16[2,32,1,128,256]{4,3,2,1,0:T(8,128)(2,1)} %bitcast.474), kind=kLoop, calls=%fused_computation.36 | loop fusion | flops 8388608 | bytes 25165824 | tf_op jit(solution)/shard_map/convert_element_type | solution.py:101
  397.8 11.6 %fusion.73 = (f32[1,32,2,128,256]{4,3,2,1,0:T(8,128)}, f32[1,32,2,128,256]{4,3,2,1,0:T(8,128)}) fusion(f32[2,32,2,128,256]{4,3,2,1,0:T(8,128)} %maximum_convert_fusion.1), kind=kLoop, calls=%fused_computation.215 | loop fusion | bytes 33554432 | tf_op jit(solution)/shard_map/slice | solution.py:83
  409.4 20.3 %reduce-precision_convert_fusion.2 = (bf16[1,2,8192,256]{3,2,1,0:T(8,128)(2,1)}, bf16[1,2,8192,256]{3,2,1,0:T(8,128)(2,1)}) fusion(f32[8192,256]{1,0:T(8,128)} %bitcast.468, f32[8192,256]{1,0:T(8,128)} %bitcast.467, bf16[1,2,8192,1024]{3,2,1,0:T(8,128)(2,1)} %param.6, s32[]{:T(128)S(6)} %select_n.252, f32[2]{0:T(128)S(1)} %get-tuple-element.3, ...), kind=kLoop, calls=%fused_computation.31 | loop fusion | flops 67108864 | bytes 67108888 | tf_op jit(solution)/shard_map/convert_element_type | solution.py:62
  429.7 7.1 pad_maximum_fusion.2
  442.2 19.8 %fusion.72 = (f32[1,4096,1024]{2,1,0:T(8,128)}, f32[1,4096,1024]{2,1,0:T(8,128)}) fusion(bf16[2,4096,1024]{2,1,0:T(8,128)(2,1)} %all-gather.5.cloned.1.call-done), kind=kLoop, calls=%fused_computation.214 | loop fusion | bytes 67108864 | tf_op jit(solution)/shard_map/slice | solution.py:83
  462.1 12.0 %fusion.71 = (f32[1,4096,1024]{2,1,0:T(8,128)}, f32[1,4096,1024]{2,1,0:T(8,128)}) fusion(bf16[2,4096,1024]{2,1,0:T(8,128)(2,1)S(1)} %bitcast.409), kind=kLoop, calls=%fused_computation.213 | loop fusion | bytes 67108864 | tf_op jit(solution)/shard_map/slice | solution.py:83
  474.1 43.9 %reduce-precision_convert_fusion.1 = (bf16[2,32,1,128,1024]{4,3,2,1,0:T(8,128)(2,1)}, bf16[2,32,1,128,1024]{4,3,2,1,0:T(8,128)(2,1)}) fusion(bf16[2,32,2,128,1024]{4,3,2,1,0:T(8,128)(2,1)} %bitcast.456, f32[32,128,1024]{2,1,0:T(8,128)} %bitcast.460, f32[2]{0:T(128)S(1)} %get-tuple-element.3, f32[32,128,1024]{2,1,0:T(8,128)} %bitcast.459, ...), kind=kLoop, calls=%fused_computation.4 | loop fusion | flops 134217728 | bytes 134217744 | tf_op jit(solution)/shard_map/convert_element_type | solution.py:62
  518.0 23.0 %pad_maximum_fusion = bf16[2,32,2,128,1024]{4,3,2,1,0:T(8,128)(2,1)} fusion(bf16[2,32,1,128,1024]{4,3,2,1,0:T(8,128)(2,1)} %get-tuple-element.13, bf16[2,32,1,128,1024]{4,3,2,1,0:T(8,128)(2,1)} %get-tuple-element.12), kind=kLoop, calls=%fused_computation.1 | loop fusion | flops 16777216 | bytes 67108864 | tf_op jit(solution)/shard_map/stack | solution.py:98
  549.6 9.5 collective-permute-done.23
  565.2 8.7 collective-permute-done.24
  580.0 7.8 collective-permute-done.25
  643.5 7.3 collective-permute-done.30
  656.9 8.4 collective-permute-done.31
  671.4 9.3 collective-permute-done.32
  687.1 9.3 collective-permute-done.33
  702.6 8.8 collective-permute-done.34
  717.5 7.9 collective-permute-done.35
  794.2 8.1 collective-permute-done.41
  823.9 10.0 %fusion.75 = (bf16[1,2,22,256,256]{4,3,1,0,2:T(8,128)(2,1)}, bf16[1,2,22,256,256]{4,3,1,0,2:T(8,128)(2,1)}) fusion(bf16[2,2,22,256,256]{4,3,1,0,2:T(8,128)(2,1)} %bitcast_dynamic-update-slice_fusion.21), kind=kLoop, calls=%fused_computation.217 | loop fusion | bytes 23068672 | tf_op jit(solution)/shard_map/slice | solution.py:55
  842.3 10.0 %fusion.76 = (bf16[1,2,22,256,256]{4,3,2,1,0:T(8,128)(2,1)}, bf16[1,2,22,256,256]{4,3,2,1,0:T(8,128)(2,1)}) fusion(bf16[2,2,22,256,256]{4,3,2,1,0:T(8,128)(2,1)} %bitcast_dynamic-update-slice_fusion.43), kind=kLoop, calls=%fused_computation.218 | loop fusion | bytes 23068672 | tf_op jit(solution)/shard_map/slice | solution.py:55
  852.3 7.2 maximum_select_fusion.1
  879.6 22.6 %convert_bitcast_fusion.1 = bf16[1,1,1024,8192]{3,2,1,0:T(8,128)(2,1)} fusion(bf16[8192,256]{1,0:T(8,128)(2,1)} %get-tuple-element.24, bf16[8192,256]{1,0:T(8,128)(2,1)} %get-tuple-element.27, bf16[8192,256]{1,0:T(8,128)(2,1)} %get-tuple-element.4, bf16[8192,256]{1,0:T(8,128)(2,1)} %get-tuple-element.26, bf16[256,1024]{1,0:T(8,128)(2,1)S(1)} %get-tuple-element.18, ...), kind=kOutput, calls=%fused_computation.30 | convolution fusion | flops 17263755264 | bytes 35651584 | tf_op jit(solution)/shard_map/dot_general | solution.py:117
  902.2 23.0 %convert_bitcast_fusion = bf16[1,1,1024,8192]{3,2,1,0:T(8,128)(2,1)} fusion(bf16[8192,256]{1,0:T(8,128)(2,1)} %get-tuple-element.27, bf16[8192,256]{1,0:T(8,128)(2,1)} %get-tuple-element.25, bf16[8192,256]{1,0:T(8,128)(2,1)} %get-tuple-element.26, bf16[8192,256]{1,0:T(8,128)(2,1)} %get-tuple-element.5, bf16[256,1024]{1,0:T(8,128)(2,1)S(1)} %get-tuple-element.18, ...), kind=kOutput, calls=%fused_computation.29 | convolution fusion | flops 17263755264 | bytes 35651584 | tf_op jit(solution)/shard_map/dot_general | solution.py:118
  925.2 23.0 %pad_maximum_fusion.1 = bf16[1,2,1024,8192]{3,2,1,0:T(8,128)(2,1)} fusion(bf16[1,1,1024,8192]{3,2,1,0:T(8,128)(2,1)} %convert_bitcast_fusion, bf16[1,1,1024,8192]{3,2,1,0:T(8,128)(2,1)} %convert_bitcast_fusion.1), kind=kLoop, calls=%fused_computation.2 | loop fusion | flops 16777216 | bytes 67108864 | tf_op jit(solution)/shard_map/stack | solution.py:119
  (237 shorter events, 258.9 us)
Async XLA Ops:
  7.2 255.7 %all-gather.3.cloned.1.call-start = ((), (), s32[]{:S(2)}) async-start(), calls=%async_computation.2 | async-start | bytes 20971520 | tf_op jit(solution)/shard_map/all_gather | solution.py:91
  133.7 221.7 %all-gather.5.cloned.1.call-start = ((), (), s32[]{:S(2)}) async-start(), calls=%async_computation.3 | async-start | bytes 20971520 | tf_op jit(solution)/shard_map/all_gather | solution.py:91
  437.8 105.7 %collective-permute-start.22 = (bf16[2,2,256,256]{3,2,1,0:T(8,128)(2,1)}, bf16[2,2,256,256]{3,2,1,0:T(8,128)(2,1)S(1)}, u32[]{:S(2)}, u32[]{:S(2)}) collective-permute-start(bf16[2,2,256,256]{3,2,1,0:T(8,128)(2,1)} %fusion.42), channel_id=1, source_target_pairs={{2,0},{4,2},{6,4},{7,6},{5,7},{3,5},{1,3},{0,1},{10,8},{12,10},{14... | collective-permute-start | bytes 1572872 | tf_op jit(solution)/shard_map/ppermute | solution.py:49
  440.5 106.1 %collective-permute-start = (bf16[2,2,256,256]{3,2,1,0:T(8,128)(2,1)S(1)}, bf16[2,2,256,256]{3,2,1,0:T(8,128)(2,1)S(1)}, u32[]{:S(2)}, u32[]{:S(2)}) collective-permute-start(bf16[2,2,256,256]{3,2,1,0:T(8,128)(2,1)S(1)} %fusion.57), channel_id=1, source_target_pairs={{0,2},{2,4},{4,6},{6,7},{7,5},{5,3},{3,1},{1,0},{8,10},{10,12},{12... | collective-permute-start | bytes 1572872 | tf_op jit(solution)/shard_map/ppermute | solution.py:49
  544.7 14.4 %collective-permute-start.23 = (bf16[2,2,256,256]{3,2,1,0:T(8,128)(2,1)S(1)}, bf16[2,2,256,256]{3,2,1,0:T(8,128)(2,1)S(1)}, u32[]{:S(2)}, u32[]{:S(2)}) collective-permute-start(bf16[2,2,256,256]{3,2,1,0:T(8,128)(2,1)S(1)} %fusion.41), channel_id=1, source_target_pairs={{2,0},{4,2},{6,4},{7,6},{5,7},{3,5},{1,3},{0,1},{10,8},{12,10},{14... | collective-permute-start | bytes 1572872 | tf_op jit(solution)/shard_map/ppermute | solution.py:49
  547.8 13.2 %collective-permute-start.1 = (bf16[2,2,256,256]{3,2,1,0:T(8,128)(2,1)S(1)}, bf16[2,2,256,256]{3,2,1,0:T(8,128)(2,1)S(1)}, u32[]{:S(2)}, u32[]{:S(2)}) collective-permute-start(bf16[2,2,256,256]{3,2,1,0:T(8,128)(2,1)S(1)} %fusion.56), channel_id=1, source_target_pairs={{0,2},{2,4},{4,6},{6,7},{7,5},{5,3},{3,1},{1,0},{8,10},{10,12},{12... | collective-permute-start | bytes 1572872 | tf_op jit(solution)/shard_map/ppermute | solution.py:49
  560.3 13.7 %collective-permute-start.24 = (bf16[2,2,256,256]{3,2,1,0:T(8,128)(2,1)S(1)}, bf16[2,2,256,256]{3,2,1,0:T(8,128)(2,1)S(1)}, u32[]{:S(2)}, u32[]{:S(2)}) collective-permute-start(bf16[2,2,256,256]{3,2,1,0:T(8,128)(2,1)S(1)} %fusion.40), channel_id=1, source_target_pairs={{2,0},{4,2},{6,4},{7,6},{5,7},{3,5},{1,3},{0,1},{10,8},{12,10},{14... | collective-permute-start | bytes 1572872 | tf_op jit(solution)/shard_map/ppermute | solution.py:49
  562.2 13.3 %collective-permute-start.2 = (bf16[2,2,256,256]{3,2,1,0:T(8,128)(2,1)S(1)}, bf16[2,2,256,256]{3,2,1,0:T(8,128)(2,1)S(1)}, u32[]{:S(2)}, u32[]{:S(2)}) collective-permute-start(bf16[2,2,256,256]{3,2,1,0:T(8,128)(2,1)S(1)} %fusion.55), channel_id=1, source_target_pairs={{0,2},{2,4},{4,6},{6,7},{7,5},{5,3},{3,1},{1,0},{8,10},{10,12},{12... | collective-permute-start | bytes 1572872 | tf_op jit(solution)/shard_map/ppermute | solution.py:49
  575.1 12.8 %collective-permute-start.25 = (bf16[2,2,256,256]{3,2,1,0:T(8,128)(2,1)S(1)}, bf16[2,2,256,256]{3,2,1,0:T(8,128)(2,1)S(1)}, u32[]{:S(2)}, u32[]{:S(2)}) collective-permute-start(bf16[2,2,256,256]{3,2,1,0:T(8,128)(2,1)S(1)} %fusion.39), channel_id=1, source_target_pairs={{2,0},{4,2},{6,4},{7,6},{5,7},{3,5},{1,3},{0,1},{10,8},{12,10},{14... | collective-permute-start | bytes 1572872 | tf_op jit(solution)/shard_map/ppermute | solution.py:49
  576.6 12.8 %collective-permute-start.3 = (bf16[2,2,256,256]{3,2,1,0:T(8,128)(2,1)S(1)}, bf16[2,2,256,256]{3,2,1,0:T(8,128)(2,1)S(1)}, u32[]{:S(2)}, u32[]{:S(2)}) collective-permute-start(bf16[2,2,256,256]{3,2,1,0:T(8,128)(2,1)S(1)} %fusion.54), channel_id=1, source_target_pairs={{0,2},{2,4},{4,6},{6,7},{7,5},{5,3},{3,1},{1,0},{8,10},{10,12},{12... | collective-permute-start | bytes 1572872 | tf_op jit(solution)/shard_map/ppermute | solution.py:49
  589.0 11.8 %collective-permute-start.26 = (bf16[2,2,256,256]{3,2,1,0:T(8,128)(2,1)S(1)}, bf16[2,2,256,256]{3,2,1,0:T(8,128)(2,1)S(1)}, u32[]{:S(2)}, u32[]{:S(2)}) collective-permute-start(bf16[2,2,256,256]{3,2,1,0:T(8,128)(2,1)S(1)} %fusion.38), channel_id=1, source_target_pairs={{2,0},{4,2},{6,4},{7,6},{5,7},{3,5},{1,3},{0,1},{10,8},{12,10},{14... | collective-permute-start | bytes 1572872 | tf_op jit(solution)/shard_map/ppermute | solution.py:49
  590.5 11.8 %collective-permute-start.4 = (bf16[2,2,256,256]{3,2,1,0:T(8,128)(2,1)S(1)}, bf16[2,2,256,256]{3,2,1,0:T(8,128)(2,1)S(1)}, u32[]{:S(2)}, u32[]{:S(2)}) collective-permute-start(bf16[2,2,256,256]{3,2,1,0:T(8,128)(2,1)S(1)} %fusion.53), channel_id=1, source_target_pairs={{0,2},{2,4},{4,6},{6,7},{7,5},{5,3},{3,1},{1,0},{8,10},{10,12},{12... | collective-permute-start | bytes 1572872 | tf_op jit(solution)/shard_map/ppermute | solution.py:49
  638.5 12.3 %collective-permute-start.30 = (bf16[2,2,256,256]{3,2,1,0:T(8,128)(2,1)S(1)}, bf16[2,2,256,256]{3,2,1,0:T(8,128)(2,1)S(1)}, u32[]{:S(2)}, u32[]{:S(2)}) collective-permute-start(bf16[2,2,256,256]{3,2,1,0:T(8,128)(2,1)S(1)} %fusion.34), channel_id=1, source_target_pairs={{2,0},{4,2},{6,4},{7,6},{5,7},{3,5},{1,3},{0,1},{10,8},{12,10},{14... | collective-permute-start | bytes 1572872 | tf_op jit(solution)/shard_map/ppermute | solution.py:49
  640.0 12.2 %collective-permute-start.8 = (bf16[2,2,256,256]{3,2,1,0:T(8,128)(2,1)S(1)}, bf16[2,2,256,256]{3,2,1,0:T(8,128)(2,1)S(1)}, u32[]{:S(2)}, u32[]{:S(2)}) collective-permute-start(bf16[2,2,256,256]{3,2,1,0:T(8,128)(2,1)S(1)} %fusion.49), channel_id=1, source_target_pairs={{0,2},{2,4},{4,6},{6,7},{7,5},{5,3},{3,1},{1,0},{8,10},{10,12},{12... | collective-permute-start | bytes 1572872 | tf_op jit(solution)/shard_map/ppermute | solution.py:49
  651.9 13.3 %collective-permute-start.31 = (bf16[2,2,256,256]{3,2,1,0:T(8,128)(2,1)S(1)}, bf16[2,2,256,256]{3,2,1,0:T(8,128)(2,1)S(1)}, u32[]{:S(2)}, u32[]{:S(2)}) collective-permute-start(bf16[2,2,256,256]{3,2,1,0:T(8,128)(2,1)S(1)} %fusion.33), channel_id=1, source_target_pairs={{2,0},{4,2},{6,4},{7,6},{5,7},{3,5},{1,3},{0,1},{10,8},{12,10},{14... | collective-permute-start | bytes 1572872 | tf_op jit(solution)/shard_map/ppermute | solution.py:49
  653.4 13.3 %collective-permute-start.9 = (bf16[2,2,256,256]{3,2,1,0:T(8,128)(2,1)S(1)}, bf16[2,2,256,256]{3,2,1,0:T(8,128)(2,1)S(1)}, u32[]{:S(2)}, u32[]{:S(2)}) collective-permute-start(bf16[2,2,256,256]{3,2,1,0:T(8,128)(2,1)S(1)} %fusion.48), channel_id=1, source_target_pairs={{0,2},{2,4},{4,6},{6,7},{7,5},{5,3},{3,1},{1,0},{8,10},{10,12},{12... | collective-permute-start | bytes 1572872 | tf_op jit(solution)/shard_map/ppermute | solution.py:49
  666.4 14.2 %collective-permute-start.32 = (bf16[2,2,256,256]{3,2,1,0:T(8,128)(2,1)S(1)}, bf16[2,2,256,256]{3,2,1,0:T(8,128)(2,1)S(1)}, u32[]{:S(2)}, u32[]{:S(2)}) collective-permute-start(bf16[2,2,256,256]{3,2,1,0:T(8,128)(2,1)S(1)} %fusion.32), channel_id=1, source_target_pairs={{2,0},{4,2},{6,4},{7,6},{5,7},{3,5},{1,3},{0,1},{10,8},{12,10},{14... | collective-permute-start | bytes 1572872 | tf_op jit(solution)/shard_map/ppermute | solution.py:49
  667.9 14.5 %collective-permute-start.10 = (bf16[2,2,256,256]{3,2,1,0:T(8,128)(2,1)S(1)}, bf16[2,2,256,256]{3,2,1,0:T(8,128)(2,1)S(1)}, u32[]{:S(2)}, u32[]{:S(2)}) collective-permute-start(bf16[2,2,256,256]{3,2,1,0:T(8,128)(2,1)S(1)} %fusion.47), channel_id=1, source_target_pairs={{0,2},{2,4},{4,6},{6,7},{7,5},{5,3},{3,1},{1,0},{8,10},{10,12},{12... | collective-permute-start | bytes 1572872 | tf_op jit(solution)/shard_map/ppermute | solution.py:49
  681.8 14.6 %collective-permute-start.33 = (bf16[2,2,256,256]{3,2,1,0:T(8,128)(2,1)S(1)}, bf16[2,2,256,256]{3,2,1,0:T(8,128)(2,1)S(1)}, u32[]{:S(2)}, u32[]{:S(2)}) collective-permute-start(bf16[2,2,256,256]{3,2,1,0:T(8,128)(2,1)S(1)} %fusion.31), channel_id=1, source_target_pairs={{2,0},{4,2},{6,4},{7,6},{5,7},{3,5},{1,3},{0,1},{10,8},{12,10},{14... | collective-permute-start | bytes 1572872 | tf_op jit(solution)/shard_map/ppermute | solution.py:49
  683.6 14.3 %collective-permute-start.11 = (bf16[2,2,256,256]{3,2,1,0:T(8,128)(2,1)S(1)}, bf16[2,2,256,256]{3,2,1,0:T(8,128)(2,1)S(1)}, u32[]{:S(2)}, u32[]{:S(2)}) collective-permute-start(bf16[2,2,256,256]{3,2,1,0:T(8,128)(2,1)S(1)} %fusion.46), channel_id=1, source_target_pairs={{0,2},{2,4},{4,6},{6,7},{7,5},{5,3},{3,1},{1,0},{8,10},{10,12},{12... | collective-permute-start | bytes 1572872 | tf_op jit(solution)/shard_map/ppermute | solution.py:49
  697.6 13.7 %collective-permute-start.34 = (bf16[2,2,256,256]{3,2,1,0:T(8,128)(2,1)S(1)}, bf16[2,2,256,256]{3,2,1,0:T(8,128)(2,1)S(1)}, u32[]{:S(2)}, u32[]{:S(2)}) collective-permute-start(bf16[2,2,256,256]{3,2,1,0:T(8,128)(2,1)S(1)} %fusion.30), channel_id=1, source_target_pairs={{2,0},{4,2},{6,4},{7,6},{5,7},{3,5},{1,3},{0,1},{10,8},{12,10},{14... | collective-permute-start | bytes 1572872 | tf_op jit(solution)/shard_map/ppermute | solution.py:49
  699.1 13.7 %collective-permute-start.12 = (bf16[2,2,256,256]{3,2,1,0:T(8,128)(2,1)S(1)}, bf16[2,2,256,256]{3,2,1,0:T(8,128)(2,1)S(1)}, u32[]{:S(2)}, u32[]{:S(2)}) collective-permute-start(bf16[2,2,256,256]{3,2,1,0:T(8,128)(2,1)S(1)} %fusion.45), channel_id=1, source_target_pairs={{0,2},{2,4},{4,6},{6,7},{7,5},{5,3},{3,1},{1,0},{8,10},{10,12},{12... | collective-permute-start | bytes 1572872 | tf_op jit(solution)/shard_map/ppermute | solution.py:49
  712.5 12.9 %collective-permute-start.35 = (bf16[2,2,256,256]{3,2,1,0:T(8,128)(2,1)S(1)}, bf16[2,2,256,256]{3,2,1,0:T(8,128)(2,1)S(1)}, u32[]{:S(2)}, u32[]{:S(2)}) collective-permute-start(bf16[2,2,256,256]{3,2,1,0:T(8,128)(2,1)S(1)} %fusion.29), channel_id=1, source_target_pairs={{2,0},{4,2},{6,4},{7,6},{5,7},{3,5},{1,3},{0,1},{10,8},{12,10},{14... | collective-permute-start | bytes 1572872 | tf_op jit(solution)/shard_map/ppermute | solution.py:49
  714.0 12.9 %collective-permute-start.13 = (bf16[2,2,256,256]{3,2,1,0:T(8,128)(2,1)S(1)}, bf16[2,2,256,256]{3,2,1,0:T(8,128)(2,1)S(1)}, u32[]{:S(2)}, u32[]{:S(2)}) collective-permute-start(bf16[2,2,256,256]{3,2,1,0:T(8,128)(2,1)S(1)} %fusion.44), channel_id=1, source_target_pairs={{0,2},{2,4},{4,6},{6,7},{7,5},{5,3},{3,1},{1,0},{8,10},{10,12},{12... | collective-permute-start | bytes 1572872 | tf_op jit(solution)/shard_map/ppermute | solution.py:49
  726.6 12.0 %collective-permute-start.36 = (bf16[2,2,256,256]{3,2,1,0:T(8,128)(2,1)S(1)}, bf16[2,2,256,256]{3,2,1,0:T(8,128)(2,1)S(1)}, u32[]{:S(2)}, u32[]{:S(2)}) collective-permute-start(bf16[2,2,256,256]{3,2,1,0:T(8,128)(2,1)S(1)} %fusion.28), channel_id=1, source_target_pairs={{2,0},{4,2},{6,4},{7,6},{5,7},{3,5},{1,3},{0,1},{10,8},{12,10},{14... | collective-permute-start | bytes 1572872 | tf_op jit(solution)/shard_map/ppermute | solution.py:49
  728.1 12.0 %collective-permute-start.14 = (bf16[2,2,256,256]{3,2,1,0:T(8,128)(2,1)S(1)}, bf16[2,2,256,256]{3,2,1,0:T(8,128)(2,1)S(1)}, u32[]{:S(2)}, u32[]{:S(2)}) collective-permute-start(bf16[2,2,256,256]{3,2,1,0:T(8,128)(2,1)S(1)} %fusion.43), channel_id=1, source_target_pairs={{0,2},{2,4},{4,6},{6,7},{7,5},{5,3},{3,1},{1,0},{8,10},{10,12},{12... | collective-permute-start | bytes 1572872 | tf_op jit(solution)/shard_map/ppermute | solution.py:49
  741.2 11.2 %collective-permute-start.15 = (bf16[2,2,256,256]{3,2,1,0:T(8,128)(2,1)S(1)}, bf16[2,2,256,256]{3,2,1,0:T(8,128)(2,1)S(1)}, u32[]{:S(2)}, u32[]{:S(2)}) collective-permute-start(bf16[2,2,256,256]{3,2,1,0:T(8,128)(2,1)S(1)} %broadcast_select_fusion.13), channel_id=1, source_target_pairs={{0,2},{2,4},{4,6},{6,7},{7,5},{5,3},{3,1},{1,0},{8,10},{10,12},{12... | collective-permute-start | bytes 1572872 | tf_op jit(solution)/shard_map/ppermute | solution.py:49
  775.8 12.2 %collective-permute-start.40 = (bf16[2,2,256,256]{3,2,1,0:T(8,128)(2,1)S(1)}, bf16[2,2,256,256]{3,2,1,0:T(8,128)(2,1)S(1)}, u32[]{:S(2)}, u32[]{:S(2)}) collective-permute-start(bf16[2,2,256,256]{3,2,1,0:T(8,128)(2,1)S(1)} %broadcast_select_fusion.3), channel_id=1, source_target_pairs={{2,0},{4,2},{6,4},{7,6},{5,7},{3,5},{1,3},{0,1},{10,8},{12,10},{14... | collective-permute-start | bytes 1572872 | tf_op jit(solution)/shard_map/ppermute | solution.py:49
  777.7 11.8 %collective-permute-start.18 = (bf16[2,2,256,256]{3,2,1,0:T(8,128)(2,1)S(1)}, bf16[2,2,256,256]{3,2,1,0:T(8,128)(2,1)S(1)}, u32[]{:S(2)}, u32[]{:S(2)}) collective-permute-start(bf16[2,2,256,256]{3,2,1,0:T(8,128)(2,1)S(1)} %broadcast_select_fusion.10), channel_id=1, source_target_pairs={{0,2},{2,4},{4,6},{6,7},{7,5},{5,3},{3,1},{1,0},{8,10},{10,12},{12... | collective-permute-start | bytes 1572872 | tf_op jit(solution)/shard_map/ppermute | solution.py:49
  789.2 13.1 %collective-permute-start.41 = (bf16[2,2,256,256]{3,2,1,0:T(8,128)(2,1)S(1)}, bf16[2,2,256,256]{3,2,1,0:T(8,128)(2,1)S(1)}, u32[]{:S(2)}, u32[]{:S(2)}) collective-permute-start(bf16[2,2,256,256]{3,2,1,0:T(8,128)(2,1)S(1)} %broadcast_select_fusion.2), channel_id=1, source_target_pairs={{2,0},{4,2},{6,4},{7,6},{5,7},{3,5},{1,3},{0,1},{10,8},{12,10},{14... | collective-permute-start | bytes 1572872 | tf_op jit(solution)/shard_map/ppermute | solution.py:49
  790.7 13.1 %collective-permute-start.19 = (bf16[2,2,256,256]{3,2,1,0:T(8,128)(2,1)S(1)}, bf16[2,2,256,256]{3,2,1,0:T(8,128)(2,1)S(1)}, u32[]{:S(2)}, u32[]{:S(2)}) collective-permute-start(bf16[2,2,256,256]{3,2,1,0:T(8,128)(2,1)S(1)} %broadcast_select_fusion.9), channel_id=1, source_target_pairs={{0,2},{2,4},{4,6},{6,7},{7,5},{5,3},{3,1},{1,0},{8,10},{10,12},{12... | collective-permute-start | bytes 1572872 | tf_op jit(solution)/shard_map/ppermute | solution.py:49
  815.3 26.1 %collective-permute-start.21 = (bf16[2,2,256,256]{3,2,1,0:T(8,128)(2,1)S(1)}, bf16[2,2,256,256]{3,2,1,0:T(8,128)(2,1)S(1)}, u32[]{:S(2)}, u32[]{:S(2)}) collective-permute-start(bf16[2,2,256,256]{3,2,1,0:T(8,128)(2,1)S(1)} %broadcast_select_fusion.7), channel_id=1, source_target_pairs={{0,2},{2,4},{4,6},{6,7},{7,5},{5,3},{3,1},{1,0},{8,10},{10,12},{12... | collective-permute-start | bytes 1572872 | tf_op jit(solution)/shard_map/ppermute | solution.py:49
  (32 other events, 403.2 us)
Sparse Core Ops, SparseCore 0:
  133.8 104.9 all-gather.2
  250.5 104.7 all-gather.4

commit v5 on v4

--- a/solution.py
+++ b/solution.py
@@ -9,8 +9,8 @@
 PANEL = 256
 STEPS = 2
 BLOCK_START = 1022
-PIECES = 2
-RING_CHUNKS = 16
+PIECES = 4
+RING_CHUNKS = 8
 
 
 def ring_order(count):
@@ -76,47 +76,38 @@
     piece = shots_local // PIECES
     groups = freq_count * row_count
     prior_blocks = prior[0].reshape(2, groups, PIECES, piece, block_rows)
-    panels_each = block_rows // PANEL
-    offsets = [panels[p] % panels_each * PANEL for p in range(STEPS)]
-
-    def transform(samples):
-        total = weights[:, 0, None, None] * samples[0] + weights[:, 1, None, None] * samples[1]
-        return lax.reduce_precision(total, exponent_bits=8, mantissa_bits=7)
-
-    parts = []
-    panel_samples = [[] for _ in range(STEPS)]
+    samples = []
     for index in range(PIECES):
         chunk = traces[:, index * piece:(index + 1) * piece, :]
         by_row = lax.all_to_all(chunk, "row", split_axis=2, concat_axis=1, tiled=True)
         gathered = lax.all_gather(by_row, "freq", axis=1, tiled=True)
-        for p in range(STEPS):
-            picked = lax.dynamic_slice_in_dim(gathered, offsets[p], PANEL, 2)
-            panel_samples[p].append(picked.reshape(sample_count, groups, piece, PANEL))
-        samples = gathered.astype(jnp.float32).reshape(sample_count, groups * piece, block_rows)
-        blocks = prior_blocks[:, :, index].reshape(2, groups * piece, block_rows)
-        parts.append(to_bf16(blocks.astype(jnp.float32) + transform(samples)).reshape(2, groups, piece, block_rows))
-    spectrum = jnp.stack(parts, axis=2).reshape(2, receivers, block_rows)
+        samples.append(gathered.reshape(sample_count, groups, piece, block_rows))
+    samples = jnp.stack(samples, axis=2).reshape(sample_count, receivers, block_rows).astype(jnp.float32)
+    transformed = weights[:, 0, None, None] * samples[0] + weights[:, 1, None, None] * samples[1]
+    transformed = lax.reduce_precision(transformed, exponent_bits=8, mantissa_bits=7)
+    spectrum = to_bf16(prior[0].astype(jnp.float32) + transformed)
+    panels_each = block_rows // PANEL
     own_panels = []
-    for p in range(STEPS):
-        samples = jnp.stack(panel_samples[p], axis=2).reshape(sample_count, receivers, PANEL).astype(jnp.float32)
-        prior_rows = lax.dynamic_slice_in_dim(prior[0], offsets[p], PANEL, 2).astype(jnp.float32)
-        own_panels.append(to_bf16(prior_rows + transform(samples)))
+    lefts = []
+    for panel_step in range(STEPS):
+        chosen = panels[panel_step]
+        offset = chosen % panels_each * PANEL
+        own_panels.append(lax.dynamic_slice_in_dim(spectrum, offset, PANEL, 2))
+        left = lax.dynamic_slice_in_dim(spectrum, chosen * PANEL, PANEL, 1)
+        lefts += [left[0], left[1]]
     owners = jnp.stack([panels[p] // panels_each for p in range(STEPS)])
     rights = broadcast(jnp.stack(own_panels), owners, RING_CHUNKS)
-    lefts = []
-    for p in range(STEPS):
-        left = lax.dynamic_slice_in_dim(spectrum, panels[p] * PANEL, PANEL, 1)
-        lefts += [left[0], left[1]]
     reals = []
     imags = []
     for right in rights:
         reals += [right[0], -right[1]]
         imags += [right[1], right[0]]
     left_all = jnp.concatenate(lefts, axis=0)
-    dims = (((0,), (1,)), ((), ()))
-    real_sum = lax.dot_general(left_all, jnp.concatenate(reals, axis=1), dims, preferred_element_type=jnp.float32)
-    imag_sum = lax.dot_general(left_all, jnp.concatenate(imags, axis=1), dims, preferred_element_type=jnp.float32)
-    return (jnp.stack([real_sum, imag_sum])[None].astype(jnp.bfloat16), spectrum[None])
+    left_pair = jnp.stack([left_all, left_all])
+    right_pair = jnp.stack([jnp.concatenate(reals, axis=1), jnp.concatenate(imags, axis=1)])
+    dims = (((1,), (2,)), ((0,), (0,)))
+    sums = lax.dot_general(left_pair, right_pair, dims, preferred_element_type=jnp.float32)
+    return (sums[None].astype(jnp.bfloat16), spectrum[None])
 
 
 def solution(mesh):

time: 966 us -> 1210 us (1.25)
  local copies, waits for them, and re-layouts: 188 us -> 478 us
  other arithmetic: 210 us -> 183 us
  starting transfers between devices: 47.4 us -> 29.9 us
    unnamed x80 -> x96, local copies, waits for them, and re-layouts: 61.9 us -> 198 us
    all_gather x2 -> x4, waiting for transfers between devices: 92.5 us -> 8.55 us  [body(): gathered = lax.all_gather(by_row, 'freq', axis=1, tiled=True)]
    ppermute x44 -> x28, waiting for transfers between devices: 151 us -> 224 us  [broadcast(): held = lax.ppermute(send, 'row', pairs)]
    mul x0 -> x2, local copies, waits for them, and re-layouts: none -> 62.2 us  [the longest x1 31.1 us: body(): weights[:, 1, None, None] * samples[1]]
    slice x6 -> x5, local copies, waits for them, and re-layouts: 55.3 us -> 91.3 us  [the longest x2 67 us: body(): samples[0]]
    select_n x44 -> x28, other arithmetic: 49.7 us -> 19.3 us  [broadcast(): send = jnp.where(is_owner, own[:, :, min(step, chunks - 1)], held)]
    all_to_all x4, local copies, waits for them, and re-layouts: 17.6 us -> 42.6 us  [body(): lax.all_to_all(chunk, 'row', split_axis=2, concat_axis=1, tiled=True)]
    dynamic_slice x1 -> x3, local copies, waits for them, and re-layouts: 11.1 us -> 35.7 us  [body(): own_panels.append(lax.dynamic_slice_in_dim(spectrum, offset, PANEL, 2))]
  transfers between devices with their start and end apart: 46 -> 32, of which waited for: 26 -> 20; matrix products, arithmetic and copies ran while one was open for 24% -> 24% of each run, Pallas kernels for 0% -> 0%
where the time goes in v5:
time: 1210 us; the launch traced here: 1200 us
  local copies, waits for them, and re-layouts  478 us (40%)
  waiting for transfers between devices  233 us (19%)
  blocking collectives  209 us (17%)
  other arithmetic  183 us (15%)
  matrix products  45.1 us (4%)
  starting transfers between devices  29.9 us (2%)
  between operations  22.6 us (2%)
    ppermute x28, waiting for transfers between devices, broadcast(): held = lax.ppermute(send, 'row', pairs)  224 us
    all_to_all x4, blocking collectives, body(): lax.all_to_all(chunk, 'row', split_axis=2, concat_axis=1, tiled=True)  209 us
    unnamed x96, local copies, waits for them, and re-layouts  198 us
    convert_element_type x2, other arithmetic, to_bf16(): lax.reduce_precision(value, exponent_bits=8, mantissa_bits=7)  85.5 us
    slice x2, local copies, waits for them, and re-layouts, body(): samples[0]  67 us
    dot_general x1, matrix products, body(): lax.dot_general(left_pair, right_pair, dims, preferred_element_type=jnp.f...  45.1 us
    all_to_all x4, local copies, waits for them, and re-layouts, body(): lax.all_to_all(chunk, 'row', split_axis=2, concat_axis=1, tiled=True)  42.6 us
    dynamic_slice x3, local copies, waits for them, and re-layouts, body(): own_panels.append(lax.dynamic_slice_in_dim(spectrum, offset, PANEL, 2))  35.7 us
  transfers between devices with their start and end apart: 32, of which 20 were waited for; matrix products, arithmetic and copies ran while one was open for 24% of the time, Pallas kernels for 0%

profile of v5, /device:TPU:0, one launch (start us, length us, event | category | flops | bytes accessed | tf_op | source)
XLA Modules:
  0.0 1200.9 jit_solution(5584007763937225728)
XLA Ops:
  26.2 55.4 %all_to_all.72 = bf16[8,2,65536]{2,1,0:T(2,128)(2,1)} all-to-all(bf16[8,2,65536]{2,1,0:T(2,128)(2,1)S(1)} %reshape.366), channel_id=1, replica_groups=mesh['freq'=4,'row'=8] {'row'}, dimensions={0} | all-to-all | bytes 4194304 | tf_op jit(solution)/shard_map/all_to_all | solution.py:82
  113.3 51.5 %all_to_all.73 = bf16[8,2,65536]{2,1,0:T(2,128)(2,1)} all-to-all(bf16[8,2,65536]{2,1,0:T(2,128)(2,1)S(1)} %reshape.362), channel_id=1, replica_groups=mesh['freq'=4,'row'=8] {'row'}, dimensions={0} | all-to-all | bytes 4194304 | tf_op jit(solution)/shard_map/all_to_all | solution.py:82
  196.4 51.3 %all_to_all.74 = bf16[8,2,65536]{2,1,0:T(2,128)(2,1)} all-to-all(bf16[8,2,65536]{2,1,0:T(2,128)(2,1)S(1)} %reshape.364), channel_id=1, replica_groups=mesh['freq'=4,'row'=8] {'row'}, dimensions={0} | all-to-all | bytes 4194304 | tf_op jit(solution)/shard_map/all_to_all | solution.py:82
  279.4 51.3 %all_to_all.75 = bf16[8,2,65536]{2,1,0:T(2,128)(2,1)} all-to-all(bf16[8,2,65536]{2,1,0:T(2,128)(2,1)S(1)} %reshape.360), channel_id=1, replica_groups=mesh['freq'=4,'row'=8] {'row'}, dimensions={0} | all-to-all | bytes 4194304 | tf_op jit(solution)/shard_map/all_to_all | solution.py:82
  355.4 40.4 %copy.234 = bf16[1,2,8192,1024]{2,3,1,0:T(8,128)(2,1)} copy(bf16[1,2,8192,1024]{3,2,1,0:T(8,128)(2,1)} %param.6) | data formatting | bytes 67108864 | tf_op args[1]
  406.1 32.0 %maximum_convert_fusion = f32[2,32,4,64,1024]{4,3,1,0,2:T(8,128)} fusion(bf16[2,32,1,64,1024]{4,3,1,0,2:T(8,128)(2,1)} %bitcast.342, bf16[2,32,1,64,1024]{4,3,1,0,2:T(8,128)(2,1)} %bitcast.340, bf16[2,32,1,64,1024]{4,3,1,0,2:T(8,128)(2,1)} %bitcast.341, bf16[2,32,1,64,1024]{4,3,1,0,2:T(8,128)(2,1)} %bitcast.339), kind=kLoop, calls=%fused_computation.8 | loop fusion | flops 67108864 | bytes 100663296 | tf_op jit(solution)/shard_map/convert_element_type | solution.py:85
  438.1 43.7 %fusion.48 = (f32[1,32,4,64,1024]{4,3,1,0,2:T(8,128)}, f32[1,32,4,64,1024]{4,3,1,0,2:T(8,128)}) fusion(f32[2,32,4,64,1024]{4,3,1,0,2:T(8,128)} %maximum_convert_fusion), kind=kLoop, calls=%fused_computation.154 | loop fusion | bytes 134217728 | tf_op jit(solution)/shard_map/slice | solution.py:86
  481.8 23.4 %copy.247 = f32[1,32,4,64,1024]{4,3,2,1,0:T(8,128)} copy(f32[1,32,4,64,1024]{4,3,1,0,2:T(8,128)} %get-tuple-element.24) | data formatting | bytes 67108864 | tf_op jit(solution)/shard_map/slice | solution.py:86
  505.1 31.1 %copy.248 = f32[8192,1024]{0,1:T(8,128)} copy(f32[8192,1024]{1,0:T(8,128)} %bitcast.291) | data formatting | bytes 67108864 | tf_op jit(solution)/shard_map/mul | solution.py:86
  536.3 23.5 %copy.249 = f32[1,32,4,64,1024]{4,3,2,1,0:T(8,128)} copy(f32[1,32,4,64,1024]{4,3,1,0,2:T(8,128)} %get-tuple-element.25) | data formatting | bytes 67108864 | tf_op jit(solution)/shard_map/slice | solution.py:86
  559.8 31.1 %copy.250 = f32[8192,1024]{0,1:T(8,128)} copy(f32[8192,1024]{1,0:T(8,128)} %bitcast.292) | data formatting | bytes 67108864 | tf_op jit(solution)/shard_map/mul | solution.py:86
  590.9 42.8 %fusion.2 = bf16[2,8192,1024]{1,2,0:T(8,128)(2,1)} fusion(bf16[1,2,8192,1024]{2,3,1,0:T(8,128)(2,1)} %copy.234, f32[8192,1024]{0,1:T(8,128)} %copy.250, f32[2]{0:T(128)S(1)} %get-tuple-element.15, f32[8192,1024]{0,1:T(8,128)} %copy.248, f32[2]{0:T(128)S(1)} %get-tuple-element.14), kind=kLoop, calls=%fused_computation.5 | loop fusion | flops 134217728 | bytes 134217744 | tf_op jit(solution)/shard_map/convert_element_type | solution.py:62
  633.7 11.7 constant_dynamic-slice_fusion.5
  645.4 12.0 copy.252
  657.4 12.0 copy.251
  678.4 23.1 %collective-permute-done.14 = bf16[2,2,512,256]{3,2,1,0:T(8,128)(2,1)S(1)} collective-permute-done((bf16[2,2,512,256]{3,2,1,0:T(8,128)(2,1)S(1)}, bf16[2,2,512,256]{3,2,1,0:T(8,128)(2,1)S(1)}, u32[]{:S(2)}, u32[]{:S(2)}) %collective-permute-start.14) | collective-permute-done | bytes 1048608 | tf_op jit(solution)/shard_map/ppermute | solution.py:49
  704.0 22.2 %collective-permute-done.15 = bf16[2,2,512,256]{3,2,1,0:T(8,128)(2,1)S(1)} collective-permute-done((bf16[2,2,512,256]{3,2,1,0:T(8,128)(2,1)S(1)}, bf16[2,2,512,256]{3,2,1,0:T(8,128)(2,1)S(1)}, u32[]{:S(2)}, u32[]{:S(2)}) %collective-permute-start.15) | collective-permute-done | bytes 1048608 | tf_op jit(solution)/shard_map/ppermute | solution.py:49
  728.7 21.3 %collective-permute-done.16 = bf16[2,2,512,256]{3,2,1,0:T(8,128)(2,1)S(1)} collective-permute-done((bf16[2,2,512,256]{3,2,1,0:T(8,128)(2,1)S(1)}, bf16[2,2,512,256]{3,2,1,0:T(8,128)(2,1)S(1)}, u32[]{:S(2)}, u32[]{:S(2)}) %collective-permute-start.16) | collective-permute-done | bytes 1048608 | tf_op jit(solution)/shard_map/ppermute | solution.py:49
  758.9 15.2 %collective-permute-done.17 = bf16[2,2,512,256]{3,2,1,0:T(8,128)(2,1)S(1)} collective-permute-done((bf16[2,2,512,256]{3,2,1,0:T(8,128)(2,1)}, bf16[2,2,512,256]{3,2,1,0:T(8,128)(2,1)S(1)}, u32[]{:S(2)}, u32[]{:S(2)}) %collective-permute-start.17) | collective-permute-done | bytes 1048608 | tf_op jit(solution)/shard_map/ppermute | solution.py:49
  781.3 42.8 %fusion.4 = bf16[1,2,8192,1024]{2,3,1,0:T(8,128)(2,1)} fusion(bf16[1,2,8192,1024]{2,3,1,0:T(8,128)(2,1)} %copy.234, f32[8192,1024]{0,1:T(8,128)} %copy.250, f32[2]{0:T(128)S(1)} %get-tuple-element.15, f32[8192,1024]{0,1:T(8,128)} %copy.248, f32[2]{0:T(128)S(1)} %get-tuple-element.14), kind=kLoop, calls=%fused_computation.7 | loop fusion | flops 134217728 | bytes 134217744 | tf_op jit(solution)/shard_map/convert_element_type | solution.py:62
  831.1 41.9 %copy.286 = bf16[1,2,8192,1024]{3,2,1,0:T(8,128)(2,1)} copy(bf16[1,2,8192,1024]{2,3,1,0:T(8,128)(2,1)} %fusion.4) | data formatting | bytes 67108864
  887.7 14.2 %collective-permute-done.19 = bf16[2,2,512,256]{3,2,1,0:T(8,128)(2,1)S(1)} collective-permute-done((bf16[2,2,512,256]{3,2,1,0:T(8,128)(2,1)S(1)}, bf16[2,2,512,256]{3,2,1,0:T(8,128)(2,1)S(1)}, u32[]{:S(2)}, u32[]{:S(2)}) %collective-permute-start.19) | collective-permute-done | bytes 1048608 | tf_op jit(solution)/shard_map/ppermute | solution.py:49
  910.1 15.2 %collective-permute-done.20 = bf16[2,2,512,256]{3,2,1,0:T(8,128)(2,1)S(1)} collective-permute-done((bf16[2,2,512,256]{3,2,1,0:T(8,128)(2,1)S(1)}, bf16[2,2,512,256]{3,2,1,0:T(8,128)(2,1)S(1)}, u32[]{:S(2)}, u32[]{:S(2)}) %collective-permute-start.20) | collective-permute-done | bytes 1048608 | tf_op jit(solution)/shard_map/ppermute | solution.py:49
  935.6 13.0 %collective-permute-done.21 = bf16[2,2,512,256]{3,2,1,0:T(8,128)(2,1)S(1)} collective-permute-done((bf16[2,2,512,256]{3,2,1,0:T(8,128)(2,1)S(1)}, bf16[2,2,512,256]{3,2,1,0:T(8,128)(2,1)S(1)}, u32[]{:S(2)}, u32[]{:S(2)}) %collective-permute-start.21) | collective-permute-done | bytes 1048608 | tf_op jit(solution)/shard_map/ppermute | solution.py:49
  956.7 15.2 %collective-permute-done.22 = bf16[2,2,512,256]{3,2,1,0:T(8,128)(2,1)S(1)} collective-permute-done((bf16[2,2,512,256]{3,2,1,0:T(8,128)(2,1)S(1)}, bf16[2,2,512,256]{3,2,1,0:T(8,128)(2,1)S(1)}, u32[]{:S(2)}, u32[]{:S(2)}) %collective-permute-start.22) | collective-permute-done | bytes 1048608 | tf_op jit(solution)/shard_map/ppermute | solution.py:49
  981.1 14.2 %collective-permute-done.23 = bf16[2,2,512,256]{3,2,1,0:T(8,128)(2,1)S(1)} collective-permute-done((bf16[2,2,512,256]{3,2,1,0:T(8,128)(2,1)S(1)}, bf16[2,2,512,256]{3,2,1,0:T(8,128)(2,1)S(1)}, u32[]{:S(2)}, u32[]{:S(2)}) %collective-permute-start.23) | collective-permute-done | bytes 1048608 | tf_op jit(solution)/shard_map/ppermute | solution.py:49
  1003.4 15.2 %collective-permute-done.24 = bf16[2,2,512,256]{3,2,1,0:T(8,128)(2,1)S(1)} collective-permute-done((bf16[2,2,512,256]{3,2,1,0:T(8,128)(2,1)S(1)}, bf16[2,2,512,256]{3,2,1,0:T(8,128)(2,1)S(1)}, u32[]{:S(2)}, u32[]{:S(2)}) %collective-permute-start.24) | collective-permute-done | bytes 1048608 | tf_op jit(solution)/shard_map/ppermute | solution.py:49
  1027.7 14.2 %collective-permute-done.25 = bf16[2,2,512,256]{3,2,1,0:T(8,128)(2,1)S(1)} collective-permute-done((bf16[2,2,512,256]{3,2,1,0:T(8,128)(2,1)S(1)}, bf16[2,2,512,256]{3,2,1,0:T(8,128)(2,1)S(1)}, u32[]{:S(2)}, u32[]{:S(2)}) %collective-permute-start.25) | collective-permute-done | bytes 1048608 | tf_op jit(solution)/shard_map/ppermute | solution.py:49
  1050.0 14.1 %collective-permute-done.26 = bf16[2,2,512,256]{3,2,1,0:T(8,128)(2,1)S(1)} collective-permute-done((bf16[2,2,512,256]{3,2,1,0:T(8,128)(2,1)S(1)}, bf16[2,2,512,256]{3,2,1,0:T(8,128)(2,1)S(1)}, u32[]{:S(2)}, u32[]{:S(2)}) %collective-permute-start.26) | collective-permute-done | bytes 1048608 | tf_op jit(solution)/shard_map/ppermute | solution.py:49
  1091.4 11.9 fusion.49
  1130.5 18.8 %maximum_bitcast_fusion = (bf16[1,8192,1024]{2,1,0:T(8,128)(2,1)}, bf16[1,8192,1024]{2,1,0:T(8,128)(2,1)}) fusion(bf16[8192,256]{1,0:T(8,128)(2,1)} %get-tuple-element.32, bf16[8192,256]{1,0:T(8,128)(2,1)S(1)} %copy-done.5, bf16[8192,256]{1,0:T(8,128)(2,1)} %get-tuple-element.16, bf16[8192,256]{1,0:T(8,128)(2,1)S(1)} %get-tuple-element.34, ...), kind=kLoop, calls=%fused_computation.22 | loop fusion | flops 134217728 | bytes 58720256 | tf_op jit(solution)/shard_map/stack | solution.py:107
  1149.3 45.1 %convert_bitcast_fusion.1 = bf16[1,2,1024,8192]{3,2,1,0:T(8,128)(2,1)} fusion(bf16[1,8192,1024]{2,1,0:T(8,128)(2,1)} %get-tuple-element.43, bf16[1,8192,1024]{2,1,0:T(8,128)(2,1)} %get-tuple-element.42, bf16[1,1024,1024]{1,2,0:T(8,128)(2,1)S(1)} %copy-done.17), kind=kOutput, calls=%fused_computation.13 | convolution fusion | flops 34395389952 | bytes 69206016 | tf_op jit(solution)/shard_map/dot_general | solution.py:109
  (212 shorter events, 307.5 us)
Async XLA Ops:
  7.2 390.4 %all-gather.5.cloned.1.call-start = ((), (), s32[]{:S(2)}) async-start(), calls=%async_computation.4 | async-start | bytes 10485760 | tf_op jit(solution)/shard_map/all_gather | solution.py:83
  99.8 297.7 %all-gather.9.cloned.1.call-start = ((), (), s32[]{:S(2)}) async-start(), calls=%async_computation.6 | async-start | bytes 10485760 | tf_op jit(solution)/shard_map/all_gather | solution.py:83
  183.0 214.6 %all-gather.7.cloned.1.call-start = ((), (), s32[]{:S(2)}) async-start(), calls=%async_computation.5 | async-start | bytes 10485760 | tf_op jit(solution)/shard_map/all_gather | solution.py:83
  266.0 140.1 %all-gather.11.cloned.1.call-start = ((), (), s32[]{:S(2)}) async-start(), calls=%async_computation.7 | async-start | bytes 10485760 | tf_op jit(solution)/shard_map/all_gather | solution.py:83
  675.9 25.6 %collective-permute-start.14 = (bf16[2,2,512,256]{3,2,1,0:T(8,128)(2,1)S(1)}, bf16[2,2,512,256]{3,2,1,0:T(8,128)(2,1)S(1)}, u32[]{:S(2)}, u32[]{:S(2)}) collective-permute-start(bf16[2,2,512,256]{3,2,1,0:T(8,128)(2,1)S(1)} %fusion.28), channel_id=1, source_target_pairs={{2,0},{4,2},{6,4},{7,6},{5,7},{3,5},{1,3},{0,1},{10,8},{12,10},{14... | collective-permute-start | bytes 3145736 | tf_op jit(solution)/shard_map/ppermute | solution.py:49
  677.8 25.4 %collective-permute-start = (bf16[2,2,512,256]{3,2,1,0:T(8,128)(2,1)S(1)}, bf16[2,2,512,256]{3,2,1,0:T(8,128)(2,1)S(1)}, u32[]{:S(2)}, u32[]{:S(2)}) collective-permute-start(bf16[2,2,512,256]{3,2,1,0:T(8,128)(2,1)S(1)} %fusion.35), channel_id=1, source_target_pairs={{0,2},{2,4},{4,6},{6,7},{7,5},{5,3},{3,1},{1,0},{8,10},{10,12},{12... | collective-permute-start | bytes 3145736 | tf_op jit(solution)/shard_map/ppermute | solution.py:49
  701.6 24.6 %collective-permute-start.15 = (bf16[2,2,512,256]{3,2,1,0:T(8,128)(2,1)S(1)}, bf16[2,2,512,256]{3,2,1,0:T(8,128)(2,1)S(1)}, u32[]{:S(2)}, u32[]{:S(2)}) collective-permute-start(bf16[2,2,512,256]{3,2,1,0:T(8,128)(2,1)S(1)} %fusion.27), channel_id=1, source_target_pairs={{2,0},{4,2},{6,4},{7,6},{5,7},{3,5},{1,3},{0,1},{10,8},{12,10},{14... | collective-permute-start | bytes 3145736 | tf_op jit(solution)/shard_map/ppermute | solution.py:49
  703.3 24.6 %collective-permute-start.1 = (bf16[2,2,512,256]{3,2,1,0:T(8,128)(2,1)S(1)}, bf16[2,2,512,256]{3,2,1,0:T(8,128)(2,1)S(1)}, u32[]{:S(2)}, u32[]{:S(2)}) collective-permute-start(bf16[2,2,512,256]{3,2,1,0:T(8,128)(2,1)S(1)} %fusion.34), channel_id=1, source_target_pairs={{0,2},{2,4},{4,6},{6,7},{7,5},{5,3},{3,1},{1,0},{8,10},{10,12},{12... | collective-permute-start | bytes 3145736 | tf_op jit(solution)/shard_map/ppermute | solution.py:49
  726.4 23.6 %collective-permute-start.16 = (bf16[2,2,512,256]{3,2,1,0:T(8,128)(2,1)S(1)}, bf16[2,2,512,256]{3,2,1,0:T(8,128)(2,1)S(1)}, u32[]{:S(2)}, u32[]{:S(2)}) collective-permute-start(bf16[2,2,512,256]{3,2,1,0:T(8,128)(2,1)S(1)} %fusion.26), channel_id=1, source_target_pairs={{2,0},{4,2},{6,4},{7,6},{5,7},{3,5},{1,3},{0,1},{10,8},{12,10},{14... | collective-permute-start | bytes 3145736 | tf_op jit(solution)/shard_map/ppermute | solution.py:49
  728.1 24.6 %collective-permute-start.2 = (bf16[2,2,512,256]{3,2,1,0:T(8,128)(2,1)S(1)}, bf16[2,2,512,256]{3,2,1,0:T(8,128)(2,1)S(1)}, u32[]{:S(2)}, u32[]{:S(2)}) collective-permute-start(bf16[2,2,512,256]{3,2,1,0:T(8,128)(2,1)S(1)} %fusion.33), channel_id=1, source_target_pairs={{0,2},{2,4},{4,6},{6,7},{7,5},{5,3},{3,1},{1,0},{8,10},{10,12},{12... | collective-permute-start | bytes 3145736 | tf_op jit(solution)/shard_map/ppermute | solution.py:49
  751.2 22.9 %collective-permute-start.17 = (bf16[2,2,512,256]{3,2,1,0:T(8,128)(2,1)}, bf16[2,2,512,256]{3,2,1,0:T(8,128)(2,1)S(1)}, u32[]{:S(2)}, u32[]{:S(2)}) collective-permute-start(bf16[2,2,512,256]{3,2,1,0:T(8,128)(2,1)} %fusion.25), channel_id=1, source_target_pairs={{2,0},{4,2},{6,4},{7,6},{5,7},{3,5},{1,3},{0,1},{10,8},{12,10},{14... | collective-permute-start | bytes 3145736 | tf_op jit(solution)/shard_map/ppermute | solution.py:49
  754.1 23.9 %collective-permute-start.3 = (bf16[2,2,512,256]{3,2,1,0:T(8,128)(2,1)}, bf16[2,2,512,256]{3,2,1,0:T(8,128)(2,1)}, u32[]{:S(2)}, u32[]{:S(2)}) collective-permute-start(bf16[2,2,512,256]{3,2,1,0:T(8,128)(2,1)} %fusion.32), channel_id=1, source_target_pairs={{0,2},{2,4},{4,6},{6,7},{7,5},{5,3},{3,1},{1,0},{8,10},{10,12},{12... | collective-permute-start | bytes 3145736 | tf_op jit(solution)/shard_map/ppermute | solution.py:49
  776.5 99.8 %collective-permute-start.18 = (bf16[2,2,512,256]{3,2,1,0:T(8,128)(2,1)}, bf16[2,2,512,256]{3,2,1,0:T(8,128)(2,1)}, u32[]{:S(2)}, u32[]{:S(2)}) collective-permute-start(bf16[2,2,512,256]{3,2,1,0:T(8,128)(2,1)} %fusion.24), channel_id=1, source_target_pairs={{2,0},{4,2},{6,4},{7,6},{5,7},{3,5},{1,3},{0,1},{10,8},{12,10},{14... | collective-permute-start | bytes 3145736 | tf_op jit(solution)/shard_map/ppermute | solution.py:49
  780.7 43.3 %collective-permute-start.4 = (bf16[2,2,512,256]{3,2,1,0:T(8,128)(2,1)}, bf16[2,2,512,256]{3,2,1,0:T(8,128)(2,1)}, u32[]{:S(2)}, u32[]{:S(2)}) collective-permute-start(bf16[2,2,512,256]{3,2,1,0:T(8,128)(2,1)} %fusion.31), channel_id=1, source_target_pairs={{0,2},{2,4},{4,6},{6,7},{7,5},{5,3},{3,1},{1,0},{8,10},{10,12},{12... | collective-permute-start | bytes 3145736 | tf_op jit(solution)/shard_map/ppermute | solution.py:49
  826.7 56.5 %collective-permute-start.5 = (bf16[2,2,512,256]{3,2,1,0:T(8,128)(2,1)}, bf16[2,2,512,256]{3,2,1,0:T(8,128)(2,1)}, u32[]{:S(2)}, u32[]{:S(2)}) collective-permute-start(bf16[2,2,512,256]{3,2,1,0:T(8,128)(2,1)} %fusion.30), channel_id=1, source_target_pairs={{0,2},{2,4},{4,6},{6,7},{7,5},{5,3},{3,1},{1,0},{8,10},{10,12},{12... | collective-permute-start | bytes 3145736 | tf_op jit(solution)/shard_map/ppermute | solution.py:49
  878.8 23.1 %collective-permute-start.19 = (bf16[2,2,512,256]{3,2,1,0:T(8,128)(2,1)S(1)}, bf16[2,2,512,256]{3,2,1,0:T(8,128)(2,1)S(1)}, u32[]{:S(2)}, u32[]{:S(2)}) collective-permute-start(bf16[2,2,512,256]{3,2,1,0:T(8,128)(2,1)S(1)} %fusion.23), channel_id=1, source_target_pairs={{2,0},{4,2},{6,4},{7,6},{5,7},{3,5},{1,3},{0,1},{10,8},{12,10},{14... | collective-permute-start | bytes 3145736 | tf_op jit(solution)/shard_map/ppermute | solution.py:49
  885.1 23.1 %collective-permute-start.6 = (bf16[2,2,512,256]{3,2,1,0:T(8,128)(2,1)S(1)}, bf16[2,2,512,256]{3,2,1,0:T(8,128)(2,1)S(1)}, u32[]{:S(2)}, u32[]{:S(2)}) collective-permute-start(bf16[2,2,512,256]{3,2,1,0:T(8,128)(2,1)S(1)} %fusion.29), channel_id=1, source_target_pairs={{0,2},{2,4},{4,6},{6,7},{7,5},{5,3},{3,1},{1,0},{8,10},{10,12},{12... | collective-permute-start | bytes 3145736 | tf_op jit(solution)/shard_map/ppermute | solution.py:49
  902.2 23.1 %collective-permute-start.20 = (bf16[2,2,512,256]{3,2,1,0:T(8,128)(2,1)S(1)}, bf16[2,2,512,256]{3,2,1,0:T(8,128)(2,1)S(1)}, u32[]{:S(2)}, u32[]{:S(2)}) collective-permute-start(bf16[2,2,512,256]{3,2,1,0:T(8,128)(2,1)S(1)} %fusion.22), channel_id=1, source_target_pairs={{2,0},{4,2},{6,4},{7,6},{5,7},{3,5},{1,3},{0,1},{10,8},{12,10},{14... | collective-permute-start | bytes 3145736 | tf_op jit(solution)/shard_map/ppermute | solution.py:49
  908.5 23.1 %collective-permute-start.7 = (bf16[2,2,512,256]{3,2,1,0:T(8,128)(2,1)S(1)}, bf16[2,2,512,256]{3,2,1,0:T(8,128)(2,1)S(1)}, u32[]{:S(2)}, u32[]{:S(2)}) collective-permute-start(bf16[2,2,512,256]{3,2,1,0:T(8,128)(2,1)S(1)} %broadcast_select_fusion.13), channel_id=1, source_target_pairs={{0,2},{2,4},{4,6},{6,7},{7,5},{5,3},{3,1},{1,0},{8,10},{10,12},{12... | collective-permute-start | bytes 3145736 | tf_op jit(solution)/shard_map/ppermute | solution.py:49
  925.5 23.1 %collective-permute-start.21 = (bf16[2,2,512,256]{3,2,1,0:T(8,128)(2,1)S(1)}, bf16[2,2,512,256]{3,2,1,0:T(8,128)(2,1)S(1)}, u32[]{:S(2)}, u32[]{:S(2)}) collective-permute-start(bf16[2,2,512,256]{3,2,1,0:T(8,128)(2,1)S(1)} %broadcast_select_fusion.6), channel_id=1, source_target_pairs={{2,0},{4,2},{6,4},{7,6},{5,7},{3,5},{1,3},{0,1},{10,8},{12,10},{14... | collective-permute-start | bytes 3145736 | tf_op jit(solution)/shard_map/ppermute | solution.py:49
  931.8 23.2 %collective-permute-start.8 = (bf16[2,2,512,256]{3,2,1,0:T(8,128)(2,1)S(1)}, bf16[2,2,512,256]{3,2,1,0:T(8,128)(2,1)S(1)}, u32[]{:S(2)}, u32[]{:S(2)}) collective-permute-start(bf16[2,2,512,256]{3,2,1,0:T(8,128)(2,1)S(1)} %broadcast_select_fusion.12), channel_id=1, source_target_pairs={{0,2},{2,4},{4,6},{6,7},{7,5},{5,3},{3,1},{1,0},{8,10},{10,12},{12... | collective-permute-start | bytes 3145736 | tf_op jit(solution)/shard_map/ppermute | solution.py:49
  948.8 23.1 %collective-permute-start.22 = (bf16[2,2,512,256]{3,2,1,0:T(8,128)(2,1)S(1)}, bf16[2,2,512,256]{3,2,1,0:T(8,128)(2,1)S(1)}, u32[]{:S(2)}, u32[]{:S(2)}) collective-permute-start(bf16[2,2,512,256]{3,2,1,0:T(8,128)(2,1)S(1)} %broadcast_select_fusion.5), channel_id=1, source_target_pairs={{2,0},{4,2},{6,4},{7,6},{5,7},{3,5},{1,3},{0,1},{10,8},{12,10},{14... | collective-permute-start | bytes 3145736 | tf_op jit(solution)/shard_map/ppermute | solution.py:49
  955.1 23.2 %collective-permute-start.9 = (bf16[2,2,512,256]{3,2,1,0:T(8,128)(2,1)S(1)}, bf16[2,2,512,256]{3,2,1,0:T(8,128)(2,1)S(1)}, u32[]{:S(2)}, u32[]{:S(2)}) collective-permute-start(bf16[2,2,512,256]{3,2,1,0:T(8,128)(2,1)S(1)} %broadcast_select_fusion.11), channel_id=1, source_target_pairs={{0,2},{2,4},{4,6},{6,7},{7,5},{5,3},{3,1},{1,0},{8,10},{10,12},{12... | collective-permute-start | bytes 3145736 | tf_op jit(solution)/shard_map/ppermute | solution.py:49
  972.1 23.2 %collective-permute-start.23 = (bf16[2,2,512,256]{3,2,1,0:T(8,128)(2,1)S(1)}, bf16[2,2,512,256]{3,2,1,0:T(8,128)(2,1)S(1)}, u32[]{:S(2)}, u32[]{:S(2)}) collective-permute-start(bf16[2,2,512,256]{3,2,1,0:T(8,128)(2,1)S(1)} %broadcast_select_fusion.4), channel_id=1, source_target_pairs={{2,0},{4,2},{6,4},{7,6},{5,7},{3,5},{1,3},{0,1},{10,8},{12,10},{14... | collective-permute-start | bytes 3145736 | tf_op jit(solution)/shard_map/ppermute | solution.py:49
  978.5 23.2 %collective-permute-start.10 = (bf16[2,2,512,256]{3,2,1,0:T(8,128)(2,1)S(1)}, bf16[2,2,512,256]{3,2,1,0:T(8,128)(2,1)S(1)}, u32[]{:S(2)}, u32[]{:S(2)}) collective-permute-start(bf16[2,2,512,256]{3,2,1,0:T(8,128)(2,1)S(1)} %broadcast_select_fusion.10), channel_id=1, source_target_pairs={{0,2},{2,4},{4,6},{6,7},{7,5},{5,3},{3,1},{1,0},{8,10},{10,12},{12... | collective-permute-start | bytes 3145736 | tf_op jit(solution)/shard_map/ppermute | solution.py:49
  995.5 23.1 %collective-permute-start.24 = (bf16[2,2,512,256]{3,2,1,0:T(8,128)(2,1)S(1)}, bf16[2,2,512,256]{3,2,1,0:T(8,128)(2,1)S(1)}, u32[]{:S(2)}, u32[]{:S(2)}) collective-permute-start(bf16[2,2,512,256]{3,2,1,0:T(8,128)(2,1)S(1)} %broadcast_select_fusion.3), channel_id=1, source_target_pairs={{2,0},{4,2},{6,4},{7,6},{5,7},{3,5},{1,3},{0,1},{10,8},{12,10},{14... | collective-permute-start | bytes 3145736 | tf_op jit(solution)/shard_map/ppermute | solution.py:49
  1001.8 23.1 %collective-permute-start.11 = (bf16[2,2,512,256]{3,2,1,0:T(8,128)(2,1)S(1)}, bf16[2,2,512,256]{3,2,1,0:T(8,128)(2,1)S(1)}, u32[]{:S(2)}, u32[]{:S(2)}) collective-permute-start(bf16[2,2,512,256]{3,2,1,0:T(8,128)(2,1)S(1)} %broadcast_select_fusion.9), channel_id=1, source_target_pairs={{0,2},{2,4},{4,6},{6,7},{7,5},{5,3},{3,1},{1,0},{8,10},{10,12},{12... | collective-permute-start | bytes 3145736 | tf_op jit(solution)/shard_map/ppermute | solution.py:49
  1018.8 23.2 %collective-permute-start.25 = (bf16[2,2,512,256]{3,2,1,0:T(8,128)(2,1)S(1)}, bf16[2,2,512,256]{3,2,1,0:T(8,128)(2,1)S(1)}, u32[]{:S(2)}, u32[]{:S(2)}) collective-permute-start(bf16[2,2,512,256]{3,2,1,0:T(8,128)(2,1)S(1)} %broadcast_select_fusion.2), channel_id=1, source_target_pairs={{2,0},{4,2},{6,4},{7,6},{5,7},{3,5},{1,3},{0,1},{10,8},{12,10},{14... | collective-permute-start | bytes 3145736 | tf_op jit(solution)/shard_map/ppermute | solution.py:49
  1025.1 23.1 %collective-permute-start.12 = (bf16[2,2,512,256]{3,2,1,0:T(8,128)(2,1)S(1)}, bf16[2,2,512,256]{3,2,1,0:T(8,128)(2,1)S(1)}, u32[]{:S(2)}, u32[]{:S(2)}) collective-permute-start(bf16[2,2,512,256]{3,2,1,0:T(8,128)(2,1)S(1)} %broadcast_select_fusion.8), channel_id=1, source_target_pairs={{0,2},{2,4},{4,6},{6,7},{7,5},{5,3},{3,1},{1,0},{8,10},{10,12},{12... | collective-permute-start | bytes 3145736 | tf_op jit(solution)/shard_map/ppermute | solution.py:49
  1042.1 22.0 %collective-permute-start.26 = (bf16[2,2,512,256]{3,2,1,0:T(8,128)(2,1)S(1)}, bf16[2,2,512,256]{3,2,1,0:T(8,128)(2,1)S(1)}, u32[]{:S(2)}, u32[]{:S(2)}) collective-permute-start(bf16[2,2,512,256]{3,2,1,0:T(8,128)(2,1)S(1)} %broadcast_select_fusion.1), channel_id=1, source_target_pairs={{2,0},{4,2},{6,4},{7,6},{5,7},{3,5},{1,3},{0,1},{10,8},{12,10},{14... | collective-permute-start | bytes 3145736 | tf_op jit(solution)/shard_map/ppermute | solution.py:49
  1048.4 18.5 %collective-permute-start.13 = (bf16[2,2,512,256]{3,2,1,0:T(8,128)(2,1)S(1)}, bf16[2,2,512,256]{3,2,1,0:T(8,128)(2,1)S(1)}, u32[]{:S(2)}, u32[]{:S(2)}) collective-permute-start(bf16[2,2,512,256]{3,2,1,0:T(8,128)(2,1)S(1)} %broadcast_select_fusion.7), channel_id=1, source_target_pairs={{0,2},{2,4},{4,6},{6,7},{7,5},{5,3},{3,1},{1,0},{8,10},{10,12},{12... | collective-permute-start | bytes 3145736 | tf_op jit(solution)/shard_map/ppermute | solution.py:49
  1065.3 23.8 %collective-permute-start.27 = (bf16[2,2,512,256]{3,2,1,0:T(8,128)(2,1)}, bf16[2,2,512,256]{3,2,1,0:T(8,128)(2,1)}, u32[]{:S(2)}, u32[]{:S(2)}) collective-permute-start(bf16[2,2,512,256]{3,2,1,0:T(8,128)(2,1)} %broadcast_select_fusion), channel_id=1, source_target_pairs={{2,0},{4,2},{6,4},{7,6},{5,7},{3,5},{1,3},{0,1},{10,8},{12,10},{14... | collective-permute-start | bytes 3145736 | tf_op jit(solution)/shard_map/ppermute | solution.py:49
  (28 other events, 939.6 us)
Sparse Core Ops, SparseCore 0:
  99.9 57.3 all-gather.4
  183.1 57.2 all-gather.8
  266.1 57.2 all-gather.6
  348.8 57.2 all-gather.10

commit v6 on v5

--- a/solution.py
+++ b/solution.py
@@ -9,7 +9,7 @@
 PANEL = 256
 STEPS = 2
 BLOCK_START = 1022
-PIECES = 4
+PIECES = 2
 RING_CHUNKS = 8
 
 
@@ -76,16 +76,18 @@
     piece = shots_local // PIECES
     groups = freq_count * row_count
     prior_blocks = prior[0].reshape(2, groups, PIECES, piece, block_rows)
-    samples = []
+    parts = []
     for index in range(PIECES):
         chunk = traces[:, index * piece:(index + 1) * piece, :]
         by_row = lax.all_to_all(chunk, "row", split_axis=2, concat_axis=1, tiled=True)
         gathered = lax.all_gather(by_row, "freq", axis=1, tiled=True)
-        samples.append(gathered.reshape(sample_count, groups, piece, block_rows))
-    samples = jnp.stack(samples, axis=2).reshape(sample_count, receivers, block_rows).astype(jnp.float32)
-    transformed = weights[:, 0, None, None] * samples[0] + weights[:, 1, None, None] * samples[1]
-    transformed = lax.reduce_precision(transformed, exponent_bits=8, mantissa_bits=7)
-    spectrum = to_bf16(prior[0].astype(jnp.float32) + transformed)
+        gathered = gathered.reshape(sample_count, groups, piece, block_rows)
+        first = gathered[0].astype(jnp.float32)
+        second = gathered[1].astype(jnp.float32)
+        transformed = weights[:, 0, None, None, None] * first + weights[:, 1, None, None, None] * second
+        transformed = lax.reduce_precision(transformed, exponent_bits=8, mantissa_bits=7)
+        parts.append(to_bf16(prior_blocks[:, :, index].astype(jnp.float32) + transformed))
+    spectrum = jnp.stack(parts, axis=2).reshape(2, receivers, block_rows)
     panels_each = block_rows // PANEL
     own_panels = []
     lefts = []
@@ -103,11 +105,10 @@
         reals += [right[0], -right[1]]
         imags += [right[1], right[0]]
     left_all = jnp.concatenate(lefts, axis=0)
-    left_pair = jnp.stack([left_all, left_all])
-    right_pair = jnp.stack([jnp.concatenate(reals, axis=1), jnp.concatenate(imags, axis=1)])
-    dims = (((1,), (2,)), ((0,), (0,)))
-    sums = lax.dot_general(left_pair, right_pair, dims, preferred_element_type=jnp.float32)
-    return (sums[None].astype(jnp.bfloat16), spectrum[None])
+    dims = (((0,), (1,)), ((), ()))
+    real_sum = lax.dot_general(left_all, jnp.concatenate(reals, axis=1), dims, preferred_element_type=jnp.float32)
+    imag_sum = lax.dot_general(left_all, jnp.concatenate(imags, axis=1), dims, preferred_element_type=jnp.float32)
+    return (jnp.stack([real_sum, imag_sum])[None].astype(jnp.bfloat16), spectrum[None])
 
 
 def solution(mesh):

time: 1210 us -> 932 us (0.77)
  local copies, waits for them, and re-layouts: 478 us -> 142 us
  waiting for transfers between devices: 233 us -> 316 us
  other arithmetic: 183 us -> 169 us
    unnamed x96 -> x88, local copies, waits for them, and re-layouts: 198 us -> 45.8 us
    slice x4 -> x3, local copies, waits for them, and re-layouts: 90.7 us -> 25.3 us  [the longest x2 25.2 us: body(): first = gathered[0].astype(jnp.float32)]
    mul x2 -> x0, local copies, waits for them, and re-layouts: 62.2 us -> none  [the longest x1 31.1 us: body(): weights[:, 1, None, None] * samples[1]]
    all_gather x4 -> x2, waiting for transfers between devices: 8.55 us -> 59.7 us  [body(): gathered = lax.all_gather(by_row, 'freq', axis=1, tiled=True)]
    convert_element_type x2 -> x1, other arithmetic: 85.5 us -> 44 us  [to_bf16(): lax.reduce_precision(value, exponent_bits=8, mantissa_bits=7)]
    dynamic_slice x3 -> x0, local copies, waits for them, and re-layouts: 35.7 us -> none  [body(): own_panels.append(lax.dynamic_slice_in_dim(spectrum, offset, PANEL, 2))]
    ppermute x28, waiting for transfers between devices: 224 us -> 257 us  [broadcast(): held = lax.ppermute(send, 'row', pairs)]
    all_to_all x4, local copies, waits for them, and re-layouts: 42.6 us -> 17.7 us  [body(): lax.all_to_all(chunk, 'row', split_axis=2, concat_axis=1, tiled=True)]
  transfers between devices with their start and end apart: 32 -> 30, of which waited for: 20 -> 23; matrix products, arithmetic and copies ran while one was open for 24% -> 12% of each run, Pallas kernels for 0% -> 0%
where the time goes in v6:
time: 932 us; the launch traced here: 922 us
  waiting for transfers between devices  316 us (34%)
  blocking collectives  197 us (21%)
  other arithmetic  169 us (18%)
  local copies, waits for them, and re-layouts  142 us (15%)
  matrix products  45.1 us (5%)
  starting transfers between devices  29.7 us (3%)
  between operations  23.6 us (3%)
    ppermute x28, waiting for transfers between devices, broadcast(): held = lax.ppermute(send, 'row', pairs)  257 us
    all_to_all x2, blocking collectives, body(): lax.all_to_all(chunk, 'row', split_axis=2, concat_axis=1, tiled=True)  197 us
    all_gather x2, waiting for transfers between devices, body(): gathered = lax.all_gather(by_row, 'freq', axis=1, tiled=True)  59.7 us
    unnamed x88, local copies, waits for them, and re-layouts  45.8 us
    convert_element_type x1, other arithmetic, to_bf16(): lax.reduce_precision(value, exponent_bits=8, mantissa_bits=7)  44 us
    ppermute x28, starting transfers between devices, broadcast(): held = lax.ppermute(send, 'row', pairs)  29.7 us
    slice x2, local copies, waits for them, and re-layouts, body(): first = gathered[0].astype(jnp.float32)  25.2 us
    convert_element_type x2, other arithmetic, body(): second = gathered[1].astype(jnp.float32)  23.1 us
  transfers between devices with their start and end apart: 30, of which 23 were waited for; matrix products, arithmetic and copies ran while one was open for 12% of the time, Pallas kernels for 0%

profile of v6, /device:TPU:0, one launch (start us, length us, event | category | flops | bytes accessed | tf_op | source)
XLA Modules:
  0.0 922.1 jit_solution(18300168514622810310)
XLA Ops:
  13.2 11.2 %copy.135 = bf16[2,128,8192]{1,0,2:T(2,128)(2,1)} copy(bf16[2,128,8192]{2,1,0:T(8,128)(2,1)} %get-tuple-element.34) | data formatting | bytes 8388608
  24.4 100.4 %all_to_all.36 = bf16[2,128,8192]{1,0,2:T(2,128)(2,1)S(1)} all-to-all(bf16[2,128,8192]{1,0,2:T(2,128)(2,1)} %copy.135), channel_id=1, replica_groups=mesh['freq'=4,'row'=8] {'row'}, dimensions={2} | all-to-all | bytes 8388608 | tf_op jit(solution)/shard_map/all_to_all | solution.py:82
  133.7 11.4 %copy.136 = bf16[2,128,8192]{1,0,2:T(2,128)(2,1)} copy(bf16[2,128,8192]{2,1,0:T(8,128)(2,1)} %get-tuple-element.35) | data formatting | bytes 8388608
  145.1 96.5 %all_to_all.37 = bf16[2,128,8192]{1,0,2:T(2,128)(2,1)S(1)} all-to-all(bf16[2,128,8192]{1,0,2:T(2,128)(2,1)} %copy.136), channel_id=1, replica_groups=mesh['freq'=4,'row'=8] {'row'}, dimensions={2} | all-to-all | bytes 8388608 | tf_op jit(solution)/shard_map/all_to_all | solution.py:82
  258.7 13.5 %fusion.55 = (bf16[1,4096,1024]{2,1,0:T(8,128)(2,1)}, bf16[1,4096,1024]{2,1,0:T(8,128)(2,1)}) fusion(bf16[2,4096,1024]{2,1,0:T(8,128)(2,1)} %all-gather.3.cloned.1.call-done), kind=kLoop, calls=%fused_computation.159 | loop fusion | bytes 33554432 | tf_op jit(solution)/shard_map/slice | solution.py:85
  272.2 11.7 %convert.24 = f32[32,128,1024]{2,1,0:T(8,128)} convert(bf16[32,128,1024]{2,1,0:T(8,128)(2,1)} %bitcast.274) | non-fusion elementwise | flops 4194304 | bytes 25165824 | tf_op jit(solution)/shard_map/convert_element_type | solution.py:86
  284.0 11.7 %convert.23 = f32[32,128,1024]{2,1,0:T(8,128)} convert(bf16[32,128,1024]{2,1,0:T(8,128)(2,1)} %bitcast.272) | non-fusion elementwise | flops 4194304 | bytes 25165824 | tf_op jit(solution)/shard_map/convert_element_type | solution.py:85
  295.7 59.7 %all-gather.5.cloned.1.call-done = bf16[2,4096,1024]{2,1,0:T(8,128)(2,1)} async-done(((bf16[2,1024,1024]{2,1,0:T(8,128)(2,1)}), bf16[2,4096,1024]{2,1,0:T(8,128)(2,1)}) %all-gather.5.cloned.1.call-update) | async-done | bytes 16777232 | tf_op jit(solution)/shard_map/all_gather | solution.py:83
  355.4 11.7 %fusion.56 = (bf16[1,4096,1024]{2,1,0:T(8,128)(2,1)}, bf16[1,4096,1024]{2,1,0:T(8,128)(2,1)}) fusion(bf16[2,4096,1024]{2,1,0:T(8,128)(2,1)} %all-gather.5.cloned.1.call-done), kind=kLoop, calls=%fused_computation.160 | loop fusion | bytes 33554432 | tf_op jit(solution)/shard_map/slice | solution.py:85
  367.1 11.4 %convert.26 = f32[32,128,1024]{2,1,0:T(8,128)} convert(bf16[32,128,1024]{2,1,0:T(8,128)(2,1)} %bitcast.275) | non-fusion elementwise | flops 4194304 | bytes 25165824 | tf_op jit(solution)/shard_map/convert_element_type | solution.py:86
  378.4 11.3 %convert.25 = f32[32,128,1024]{2,1,0:T(8,128)} convert(bf16[32,128,1024]{2,1,0:T(8,128)(2,1)} %bitcast.273) | non-fusion elementwise | flops 4194304 | bytes 25165824 | tf_op jit(solution)/shard_map/convert_element_type | solution.py:85
  389.8 44.0 %reduce-precision_convert_fusion.1 = (bf16[2,32,1,128,1024]{4,3,2,1,0:T(8,128)(2,1)}, bf16[2,32,1,128,1024]{4,3,2,1,0:T(8,128)(2,1)}) fusion(bf16[2,32,2,128,1024]{4,3,2,1,0:T(8,128)(2,1)} %bitcast.271, f32[32,128,1024]{2,1,0:T(8,128)} %convert.24, f32[2]{0:T(128)S(1)} %get-tuple-element.3, f32[32,128,1024]{2,1,0:T(8,128)} %convert.23, ...), kind=kLoop, calls=%fused_computation.4 | loop fusion | flops 134217728 | bytes 134217744 | tf_op jit(solution)/shard_map/convert_element_type | solution.py:62
  433.8 23.0 %pad_maximum_fusion = bf16[2,32,2,128,1024]{4,3,2,1,0:T(8,128)(2,1)} fusion(bf16[2,32,1,128,1024]{4,3,2,1,0:T(8,128)(2,1)} %get-tuple-element.13, bf16[2,32,1,128,1024]{4,3,2,1,0:T(8,128)(2,1)} %get-tuple-element.12), kind=kLoop, calls=%fused_computation.1 | loop fusion | flops 16777216 | bytes 67108864 | tf_op jit(solution)/shard_map/stack | solution.py:90
  466.9 23.1 %collective-permute-done = bf16[2,2,512,256]{3,2,1,0:T(8,128)(2,1)S(1)} collective-permute-done((bf16[2,2,512,256]{3,2,1,0:T(8,128)(2,1)S(1)}, bf16[2,2,512,256]{3,2,1,0:T(8,128)(2,1)S(1)}, u32[]{:S(2)}, u32[]{:S(2)}) %collective-permute-start) | collective-permute-done | bytes 1048608 | tf_op jit(solution)/shard_map/ppermute | solution.py:49
  492.5 22.2 %collective-permute-done.1 = bf16[2,2,512,256]{3,2,1,0:T(8,128)(2,1)S(1)} collective-permute-done((bf16[2,2,512,256]{3,2,1,0:T(8,128)(2,1)S(1)}, bf16[2,2,512,256]{3,2,1,0:T(8,128)(2,1)S(1)}, u32[]{:S(2)}, u32[]{:S(2)}) %collective-permute-start.1) | collective-permute-done | bytes 1048608 | tf_op jit(solution)/shard_map/ppermute | solution.py:49
  517.3 21.3 %collective-permute-done.2 = bf16[2,2,512,256]{3,2,1,0:T(8,128)(2,1)S(1)} collective-permute-done((bf16[2,2,512,256]{3,2,1,0:T(8,128)(2,1)S(1)}, bf16[2,2,512,256]{3,2,1,0:T(8,128)(2,1)S(1)}, u32[]{:S(2)}, u32[]{:S(2)}) %collective-permute-start.2) | collective-permute-done | bytes 1048608 | tf_op jit(solution)/shard_map/ppermute | solution.py:49
  541.1 20.8 %collective-permute-done.3 = bf16[2,2,512,256]{3,2,1,0:T(8,128)(2,1)S(1)} collective-permute-done((bf16[2,2,512,256]{3,2,1,0:T(8,128)(2,1)S(1)}, bf16[2,2,512,256]{3,2,1,0:T(8,128)(2,1)S(1)}, u32[]{:S(2)}, u32[]{:S(2)}) %collective-permute-start.3) | collective-permute-done | bytes 1048608 | tf_op jit(solution)/shard_map/ppermute | solution.py:49
  565.5 18.5 %collective-permute-done.4 = bf16[2,2,512,256]{3,2,1,0:T(8,128)(2,1)S(1)} collective-permute-done((bf16[2,2,512,256]{3,2,1,0:T(8,128)(2,1)S(1)}, bf16[2,2,512,256]{3,2,1,0:T(8,128)(2,1)S(1)}, u32[]{:S(2)}, u32[]{:S(2)}) %collective-permute-start.4) | collective-permute-done | bytes 1048608 | tf_op jit(solution)/shard_map/ppermute | solution.py:49
  620.7 11.2 %collective-permute-done.6 = bf16[2,2,512,256]{3,2,1,0:T(8,128)(2,1)S(1)} collective-permute-done((bf16[2,2,512,256]{3,2,1,0:T(8,128)(2,1)S(1)}, bf16[2,2,512,256]{3,2,1,0:T(8,128)(2,1)S(1)}, u32[]{:S(2)}, u32[]{:S(2)}) %collective-permute-start.6) | collective-permute-done | bytes 1048608 | tf_op jit(solution)/shard_map/ppermute | solution.py:49
  633.7 8.4 collective-permute-done.20
  644.0 11.2 %collective-permute-done.7 = bf16[2,2,512,256]{3,2,1,0:T(8,128)(2,1)S(1)} collective-permute-done((bf16[2,2,512,256]{3,2,1,0:T(8,128)(2,1)S(1)}, bf16[2,2,512,256]{3,2,1,0:T(8,128)(2,1)S(1)}, u32[]{:S(2)}, u32[]{:S(2)}) %collective-permute-start.7) | collective-permute-done | bytes 1048608 | tf_op jit(solution)/shard_map/ppermute | solution.py:49
  668.5 10.0 %collective-permute-done.8 = bf16[2,2,512,256]{3,2,1,0:T(8,128)(2,1)S(1)} collective-permute-done((bf16[2,2,512,256]{3,2,1,0:T(8,128)(2,1)S(1)}, bf16[2,2,512,256]{3,2,1,0:T(8,128)(2,1)S(1)}, u32[]{:S(2)}, u32[]{:S(2)}) %collective-permute-start.8) | collective-permute-done | bytes 1048608 | tf_op jit(solution)/shard_map/ppermute | solution.py:49
  680.3 8.4 collective-permute-done.22
  690.6 11.2 %collective-permute-done.9 = bf16[2,2,512,256]{3,2,1,0:T(8,128)(2,1)S(1)} collective-permute-done((bf16[2,2,512,256]{3,2,1,0:T(8,128)(2,1)S(1)}, bf16[2,2,512,256]{3,2,1,0:T(8,128)(2,1)S(1)}, u32[]{:S(2)}, u32[]{:S(2)}) %collective-permute-start.9) | collective-permute-done | bytes 1048608 | tf_op jit(solution)/shard_map/ppermute | solution.py:49
  714.0 11.2 %collective-permute-done.10 = bf16[2,2,512,256]{3,2,1,0:T(8,128)(2,1)S(1)} collective-permute-done((bf16[2,2,512,256]{3,2,1,0:T(8,128)(2,1)S(1)}, bf16[2,2,512,256]{3,2,1,0:T(8,128)(2,1)S(1)}, u32[]{:S(2)}, u32[]{:S(2)}) %collective-permute-start.10) | collective-permute-done | bytes 1048608 | tf_op jit(solution)/shard_map/ppermute | solution.py:49
  727.0 8.4 collective-permute-done.24
  737.3 11.2 %collective-permute-done.11 = bf16[2,2,512,256]{3,2,1,0:T(8,128)(2,1)S(1)} collective-permute-done((bf16[2,2,512,256]{3,2,1,0:T(8,128)(2,1)S(1)}, bf16[2,2,512,256]{3,2,1,0:T(8,128)(2,1)S(1)}, u32[]{:S(2)}, u32[]{:S(2)}) %collective-permute-start.11) | collective-permute-done | bytes 1048608 | tf_op jit(solution)/shard_map/ppermute | solution.py:49
  760.6 11.2 %collective-permute-done.12 = bf16[2,2,512,256]{3,2,1,0:T(8,128)(2,1)S(1)} collective-permute-done((bf16[2,2,512,256]{3,2,1,0:T(8,128)(2,1)S(1)}, bf16[2,2,512,256]{3,2,1,0:T(8,128)(2,1)S(1)}, u32[]{:S(2)}, u32[]{:S(2)}) %collective-permute-start.12) | collective-permute-done | bytes 1048608 | tf_op jit(solution)/shard_map/ppermute | solution.py:49
  838.3 8.4 fusion.51
  846.8 22.5 %convert_bitcast_fusion = bf16[1,1,1024,8192]{3,2,1,0:T(8,128)(2,1)} fusion(bf16[8192,256]{1,0:T(8,128)(2,1)} %get-tuple-element.23, bf16[8192,256]{1,0:T(8,128)(2,1)} %get-tuple-element.21, bf16[8192,256]{1,0:T(8,128)(2,1)} %get-tuple-element.22, bf16[8192,256]{1,0:T(8,128)(2,1)} %get-tuple-element.5, bf16[256,1024]{1,0:T(8,128)(2,1)S(1)} %copy-done.22, ...), kind=kOutput, calls=%fused_computation.29 | convolution fusion | flops 17263755264 | bytes 35651584 | tf_op jit(solution)/shard_map/dot_general | solution.py:110
  869.2 22.7 %convert_bitcast_fusion.1 = bf16[1,1,1024,8192]{3,2,1,0:T(8,128)(2,1)} fusion(bf16[8192,256]{1,0:T(8,128)(2,1)} %get-tuple-element.20, bf16[8192,256]{1,0:T(8,128)(2,1)} %get-tuple-element.23, bf16[8192,256]{1,0:T(8,128)(2,1)} %get-tuple-element.4, bf16[8192,256]{1,0:T(8,128)(2,1)} %get-tuple-element.22, bf16[256,1024]{1,0:T(8,128)(2,1)S(1)} %copy-done.22, ...), kind=kOutput, calls=%fused_computation.30 | convolution fusion | flops 17263755264 | bytes 35651584 | tf_op jit(solution)/shard_map/dot_general | solution.py:109
  891.9 23.0 %pad_maximum_fusion.1 = bf16[1,2,1024,8192]{3,2,1,0:T(8,128)(2,1)} fusion(bf16[1,1,1024,8192]{3,2,1,0:T(8,128)(2,1)} %convert_bitcast_fusion, bf16[1,1,1024,8192]{3,2,1,0:T(8,128)(2,1)} %convert_bitcast_fusion.1), kind=kLoop, calls=%fused_computation.2 | loop fusion | flops 16777216 | bytes 67108864 | tf_op jit(solution)/shard_map/stack | solution.py:111
  (196 shorter events, 195.9 us)
Async XLA Ops:
  7.2 251.6 %all-gather.3.cloned.1.call-start = ((), (), s32[]{:S(2)}) async-start(), calls=%async_computation.2 | async-start | bytes 20971520 | tf_op jit(solution)/shard_map/all_gather | solution.py:83
  133.6 221.7 %all-gather.5.cloned.1.call-start = ((), (), s32[]{:S(2)}) async-start(), calls=%async_computation.3 | async-start | bytes 20971520 | tf_op jit(solution)/shard_map/all_gather | solution.py:83
  464.5 99.1 %copy-start.1 = (bf16[2,2,4096,256]{3,2,1,0:T(8,128)(2,1)}, bf16[2,2,4096,256]{3,2,1,0:T(8,128)(2,1)S(1)}, u32[]{:S(2)}) copy-start(bf16[2,2,4096,256]{3,2,1,0:T(8,128)(2,1)S(1)} %get-tuple-element.24) | copy-start | bytes 25165828
  464.5 119.5 %copy-start.2 = (bf16[2,2,4096,256]{3,2,1,0:T(8,128)(2,1)}, bf16[2,2,4096,256]{3,2,1,0:T(8,128)(2,1)S(1)}, u32[]{:S(2)}) copy-start(bf16[2,2,4096,256]{3,2,1,0:T(8,128)(2,1)S(1)} %get-tuple-element.25) | copy-start | bytes 25165828
  464.7 25.4 %collective-permute-start = (bf16[2,2,512,256]{3,2,1,0:T(8,128)(2,1)S(1)}, bf16[2,2,512,256]{3,2,1,0:T(8,128)(2,1)S(1)}, u32[]{:S(2)}, u32[]{:S(2)}) collective-permute-start(bf16[2,2,512,256]{3,2,1,0:T(8,128)(2,1)S(1)} %fusion.41), channel_id=1, source_target_pairs={{0,2},{2,4},{4,6},{6,7},{7,5},{5,3},{3,1},{1,0},{8,10},{10,12},{12... | collective-permute-start | bytes 3145736 | tf_op jit(solution)/shard_map/ppermute | solution.py:49
  466.4 25.4 %collective-permute-start.14 = (bf16[2,2,512,256]{3,2,1,0:T(8,128)(2,1)S(1)}, bf16[2,2,512,256]{3,2,1,0:T(8,128)(2,1)S(1)}, u32[]{:S(2)}, u32[]{:S(2)}) collective-permute-start(bf16[2,2,512,256]{3,2,1,0:T(8,128)(2,1)S(1)} %fusion.34), channel_id=1, source_target_pairs={{2,0},{4,2},{6,4},{7,6},{5,7},{3,5},{1,3},{0,1},{10,8},{12,10},{14... | collective-permute-start | bytes 3145736 | tf_op jit(solution)/shard_map/ppermute | solution.py:49
  490.2 24.6 %collective-permute-start.1 = (bf16[2,2,512,256]{3,2,1,0:T(8,128)(2,1)S(1)}, bf16[2,2,512,256]{3,2,1,0:T(8,128)(2,1)S(1)}, u32[]{:S(2)}, u32[]{:S(2)}) collective-permute-start(bf16[2,2,512,256]{3,2,1,0:T(8,128)(2,1)S(1)} %fusion.40), channel_id=1, source_target_pairs={{0,2},{2,4},{4,6},{6,7},{7,5},{5,3},{3,1},{1,0},{8,10},{10,12},{12... | collective-permute-start | bytes 3145736 | tf_op jit(solution)/shard_map/ppermute | solution.py:49
  491.9 24.6 %collective-permute-start.15 = (bf16[2,2,512,256]{3,2,1,0:T(8,128)(2,1)S(1)}, bf16[2,2,512,256]{3,2,1,0:T(8,128)(2,1)S(1)}, u32[]{:S(2)}, u32[]{:S(2)}) collective-permute-start(bf16[2,2,512,256]{3,2,1,0:T(8,128)(2,1)S(1)} %fusion.33), channel_id=1, source_target_pairs={{2,0},{4,2},{6,4},{7,6},{5,7},{3,5},{1,3},{0,1},{10,8},{12,10},{14... | collective-permute-start | bytes 3145736 | tf_op jit(solution)/shard_map/ppermute | solution.py:49
  515.0 23.6 %collective-permute-start.2 = (bf16[2,2,512,256]{3,2,1,0:T(8,128)(2,1)S(1)}, bf16[2,2,512,256]{3,2,1,0:T(8,128)(2,1)S(1)}, u32[]{:S(2)}, u32[]{:S(2)}) collective-permute-start(bf16[2,2,512,256]{3,2,1,0:T(8,128)(2,1)S(1)} %fusion.39), channel_id=1, source_target_pairs={{0,2},{2,4},{4,6},{6,7},{7,5},{5,3},{3,1},{1,0},{8,10},{10,12},{12... | collective-permute-start | bytes 3145736 | tf_op jit(solution)/shard_map/ppermute | solution.py:49
  516.7 23.6 %collective-permute-start.16 = (bf16[2,2,512,256]{3,2,1,0:T(8,128)(2,1)S(1)}, bf16[2,2,512,256]{3,2,1,0:T(8,128)(2,1)S(1)}, u32[]{:S(2)}, u32[]{:S(2)}) collective-permute-start(bf16[2,2,512,256]{3,2,1,0:T(8,128)(2,1)S(1)} %fusion.32), channel_id=1, source_target_pairs={{2,0},{4,2},{6,4},{7,6},{5,7},{3,5},{1,3},{0,1},{10,8},{12,10},{14... | collective-permute-start | bytes 3145736 | tf_op jit(solution)/shard_map/ppermute | solution.py:49
  538.8 23.1 %collective-permute-start.3 = (bf16[2,2,512,256]{3,2,1,0:T(8,128)(2,1)S(1)}, bf16[2,2,512,256]{3,2,1,0:T(8,128)(2,1)S(1)}, u32[]{:S(2)}, u32[]{:S(2)}) collective-permute-start(bf16[2,2,512,256]{3,2,1,0:T(8,128)(2,1)S(1)} %fusion.38), channel_id=1, source_target_pairs={{0,2},{2,4},{4,6},{6,7},{7,5},{5,3},{3,1},{1,0},{8,10},{10,12},{12... | collective-permute-start | bytes 3145736 | tf_op jit(solution)/shard_map/ppermute | solution.py:49
  540.5 23.1 %collective-permute-start.17 = (bf16[2,2,512,256]{3,2,1,0:T(8,128)(2,1)S(1)}, bf16[2,2,512,256]{3,2,1,0:T(8,128)(2,1)S(1)}, u32[]{:S(2)}, u32[]{:S(2)}) collective-permute-start(bf16[2,2,512,256]{3,2,1,0:T(8,128)(2,1)S(1)} %fusion.31), channel_id=1, source_target_pairs={{2,0},{4,2},{6,4},{7,6},{5,7},{3,5},{1,3},{0,1},{10,8},{12,10},{14... | collective-permute-start | bytes 3145736 | tf_op jit(solution)/shard_map/ppermute | solution.py:49
  562.1 21.9 %collective-permute-start.4 = (bf16[2,2,512,256]{3,2,1,0:T(8,128)(2,1)S(1)}, bf16[2,2,512,256]{3,2,1,0:T(8,128)(2,1)S(1)}, u32[]{:S(2)}, u32[]{:S(2)}) collective-permute-start(bf16[2,2,512,256]{3,2,1,0:T(8,128)(2,1)S(1)} %fusion.37), channel_id=1, source_target_pairs={{0,2},{2,4},{4,6},{6,7},{7,5},{5,3},{3,1},{1,0},{8,10},{10,12},{12... | collective-permute-start | bytes 3145736 | tf_op jit(solution)/shard_map/ppermute | solution.py:49
  565.0 29.1 %collective-permute-start.18 = (bf16[2,2,512,256]{3,2,1,0:T(8,128)(2,1)}, bf16[2,2,512,256]{3,2,1,0:T(8,128)(2,1)S(1)}, u32[]{:S(2)}, u32[]{:S(2)}) collective-permute-start(bf16[2,2,512,256]{3,2,1,0:T(8,128)(2,1)} %fusion.30), channel_id=1, source_target_pairs={{2,0},{4,2},{6,4},{7,6},{5,7},{3,5},{1,3},{0,1},{10,8},{12,10},{14... | collective-permute-start | bytes 3145736 | tf_op jit(solution)/shard_map/ppermute | solution.py:49
  585.3 21.8 %collective-permute-start.5 = (bf16[2,2,512,256]{3,2,1,0:T(8,128)(2,1)}, bf16[2,2,512,256]{3,2,1,0:T(8,128)(2,1)}, u32[]{:S(2)}, u32[]{:S(2)}) collective-permute-start(bf16[2,2,512,256]{3,2,1,0:T(8,128)(2,1)} %fusion.36), channel_id=1, source_target_pairs={{0,2},{2,4},{4,6},{6,7},{7,5},{5,3},{3,1},{1,0},{8,10},{10,12},{12... | collective-permute-start | bytes 3145736 | tf_op jit(solution)/shard_map/ppermute | solution.py:49
  595.6 23.1 %collective-permute-start.19 = (bf16[2,2,512,256]{3,2,1,0:T(8,128)(2,1)S(1)}, bf16[2,2,512,256]{3,2,1,0:T(8,128)(2,1)S(1)}, u32[]{:S(2)}, u32[]{:S(2)}) collective-permute-start(bf16[2,2,512,256]{3,2,1,0:T(8,128)(2,1)S(1)} %fusion.29), channel_id=1, source_target_pairs={{2,0},{4,2},{6,4},{7,6},{5,7},{3,5},{1,3},{0,1},{10,8},{12,10},{14... | collective-permute-start | bytes 3145736 | tf_op jit(solution)/shard_map/ppermute | solution.py:49
  608.8 23.1 %collective-permute-start.6 = (bf16[2,2,512,256]{3,2,1,0:T(8,128)(2,1)S(1)}, bf16[2,2,512,256]{3,2,1,0:T(8,128)(2,1)S(1)}, u32[]{:S(2)}, u32[]{:S(2)}) collective-permute-start(bf16[2,2,512,256]{3,2,1,0:T(8,128)(2,1)S(1)} %fusion.35), channel_id=1, source_target_pairs={{0,2},{2,4},{4,6},{6,7},{7,5},{5,3},{3,1},{1,0},{8,10},{10,12},{12... | collective-permute-start | bytes 3145736 | tf_op jit(solution)/shard_map/ppermute | solution.py:49
  619.0 23.1 %collective-permute-start.20 = (bf16[2,2,512,256]{3,2,1,0:T(8,128)(2,1)S(1)}, bf16[2,2,512,256]{3,2,1,0:T(8,128)(2,1)S(1)}, u32[]{:S(2)}, u32[]{:S(2)}) collective-permute-start(bf16[2,2,512,256]{3,2,1,0:T(8,128)(2,1)S(1)} %fusion.28), channel_id=1, source_target_pairs={{2,0},{4,2},{6,4},{7,6},{5,7},{3,5},{1,3},{0,1},{10,8},{12,10},{14... | collective-permute-start | bytes 3145736 | tf_op jit(solution)/shard_map/ppermute | solution.py:49
  632.1 23.1 %collective-permute-start.7 = (bf16[2,2,512,256]{3,2,1,0:T(8,128)(2,1)S(1)}, bf16[2,2,512,256]{3,2,1,0:T(8,128)(2,1)S(1)}, u32[]{:S(2)}, u32[]{:S(2)}) collective-permute-start(bf16[2,2,512,256]{3,2,1,0:T(8,128)(2,1)S(1)} %broadcast_select_fusion.13), channel_id=1, source_target_pairs={{0,2},{2,4},{4,6},{6,7},{7,5},{5,3},{3,1},{1,0},{8,10},{10,12},{12... | collective-permute-start | bytes 3145736 | tf_op jit(solution)/shard_map/ppermute | solution.py:49
  642.3 23.2 %collective-permute-start.21 = (bf16[2,2,512,256]{3,2,1,0:T(8,128)(2,1)S(1)}, bf16[2,2,512,256]{3,2,1,0:T(8,128)(2,1)S(1)}, u32[]{:S(2)}, u32[]{:S(2)}) collective-permute-start(bf16[2,2,512,256]{3,2,1,0:T(8,128)(2,1)S(1)} %broadcast_select_fusion.6), channel_id=1, source_target_pairs={{2,0},{4,2},{6,4},{7,6},{5,7},{3,5},{1,3},{0,1},{10,8},{12,10},{14... | collective-permute-start | bytes 3145736 | tf_op jit(solution)/shard_map/ppermute | solution.py:49
  655.4 23.2 %collective-permute-start.8 = (bf16[2,2,512,256]{3,2,1,0:T(8,128)(2,1)S(1)}, bf16[2,2,512,256]{3,2,1,0:T(8,128)(2,1)S(1)}, u32[]{:S(2)}, u32[]{:S(2)}) collective-permute-start(bf16[2,2,512,256]{3,2,1,0:T(8,128)(2,1)S(1)} %broadcast_select_fusion.12), channel_id=1, source_target_pairs={{0,2},{2,4},{4,6},{6,7},{7,5},{5,3},{3,1},{1,0},{8,10},{10,12},{12... | collective-permute-start | bytes 3145736 | tf_op jit(solution)/shard_map/ppermute | solution.py:49
  665.6 23.1 %collective-permute-start.22 = (bf16[2,2,512,256]{3,2,1,0:T(8,128)(2,1)S(1)}, bf16[2,2,512,256]{3,2,1,0:T(8,128)(2,1)S(1)}, u32[]{:S(2)}, u32[]{:S(2)}) collective-permute-start(bf16[2,2,512,256]{3,2,1,0:T(8,128)(2,1)S(1)} %broadcast_select_fusion.5), channel_id=1, source_target_pairs={{2,0},{4,2},{6,4},{7,6},{5,7},{3,5},{1,3},{0,1},{10,8},{12,10},{14... | collective-permute-start | bytes 3145736 | tf_op jit(solution)/shard_map/ppermute | solution.py:49
  678.7 23.2 %collective-permute-start.9 = (bf16[2,2,512,256]{3,2,1,0:T(8,128)(2,1)S(1)}, bf16[2,2,512,256]{3,2,1,0:T(8,128)(2,1)S(1)}, u32[]{:S(2)}, u32[]{:S(2)}) collective-permute-start(bf16[2,2,512,256]{3,2,1,0:T(8,128)(2,1)S(1)} %broadcast_select_fusion.11), channel_id=1, source_target_pairs={{0,2},{2,4},{4,6},{6,7},{7,5},{5,3},{3,1},{1,0},{8,10},{10,12},{12... | collective-permute-start | bytes 3145736 | tf_op jit(solution)/shard_map/ppermute | solution.py:49
  688.9 23.1 %collective-permute-start.23 = (bf16[2,2,512,256]{3,2,1,0:T(8,128)(2,1)S(1)}, bf16[2,2,512,256]{3,2,1,0:T(8,128)(2,1)S(1)}, u32[]{:S(2)}, u32[]{:S(2)}) collective-permute-start(bf16[2,2,512,256]{3,2,1,0:T(8,128)(2,1)S(1)} %broadcast_select_fusion.4), channel_id=1, source_target_pairs={{2,0},{4,2},{6,4},{7,6},{5,7},{3,5},{1,3},{0,1},{10,8},{12,10},{14... | collective-permute-start | bytes 3145736 | tf_op jit(solution)/shard_map/ppermute | solution.py:49
  702.1 23.2 %collective-permute-start.10 = (bf16[2,2,512,256]{3,2,1,0:T(8,128)(2,1)S(1)}, bf16[2,2,512,256]{3,2,1,0:T(8,128)(2,1)S(1)}, u32[]{:S(2)}, u32[]{:S(2)}) collective-permute-start(bf16[2,2,512,256]{3,2,1,0:T(8,128)(2,1)S(1)} %broadcast_select_fusion.10), channel_id=1, source_target_pairs={{0,2},{2,4},{4,6},{6,7},{7,5},{5,3},{3,1},{1,0},{8,10},{10,12},{12... | collective-permute-start | bytes 3145736 | tf_op jit(solution)/shard_map/ppermute | solution.py:49
  712.3 23.2 %collective-permute-start.24 = (bf16[2,2,512,256]{3,2,1,0:T(8,128)(2,1)S(1)}, bf16[2,2,512,256]{3,2,1,0:T(8,128)(2,1)S(1)}, u32[]{:S(2)}, u32[]{:S(2)}) collective-permute-start(bf16[2,2,512,256]{3,2,1,0:T(8,128)(2,1)S(1)} %broadcast_select_fusion.3), channel_id=1, source_target_pairs={{2,0},{4,2},{6,4},{7,6},{5,7},{3,5},{1,3},{0,1},{10,8},{12,10},{14... | collective-permute-start | bytes 3145736 | tf_op jit(solution)/shard_map/ppermute | solution.py:49
  725.4 23.2 %collective-permute-start.11 = (bf16[2,2,512,256]{3,2,1,0:T(8,128)(2,1)S(1)}, bf16[2,2,512,256]{3,2,1,0:T(8,128)(2,1)S(1)}, u32[]{:S(2)}, u32[]{:S(2)}) collective-permute-start(bf16[2,2,512,256]{3,2,1,0:T(8,128)(2,1)S(1)} %broadcast_select_fusion.9), channel_id=1, source_target_pairs={{0,2},{2,4},{4,6},{6,7},{7,5},{5,3},{3,1},{1,0},{8,10},{10,12},{12... | collective-permute-start | bytes 3145736 | tf_op jit(solution)/shard_map/ppermute | solution.py:49
  735.6 23.1 %collective-permute-start.25 = (bf16[2,2,512,256]{3,2,1,0:T(8,128)(2,1)S(1)}, bf16[2,2,512,256]{3,2,1,0:T(8,128)(2,1)S(1)}, u32[]{:S(2)}, u32[]{:S(2)}) collective-permute-start(bf16[2,2,512,256]{3,2,1,0:T(8,128)(2,1)S(1)} %broadcast_select_fusion.2), channel_id=1, source_target_pairs={{2,0},{4,2},{6,4},{7,6},{5,7},{3,5},{1,3},{0,1},{10,8},{12,10},{14... | collective-permute-start | bytes 3145736 | tf_op jit(solution)/shard_map/ppermute | solution.py:49
  748.7 23.2 %collective-permute-start.12 = (bf16[2,2,512,256]{3,2,1,0:T(8,128)(2,1)S(1)}, bf16[2,2,512,256]{3,2,1,0:T(8,128)(2,1)S(1)}, u32[]{:S(2)}, u32[]{:S(2)}) collective-permute-start(bf16[2,2,512,256]{3,2,1,0:T(8,128)(2,1)S(1)} %broadcast_select_fusion.8), channel_id=1, source_target_pairs={{0,2},{2,4},{4,6},{6,7},{7,5},{5,3},{3,1},{1,0},{8,10},{10,12},{12... | collective-permute-start | bytes 3145736 | tf_op jit(solution)/shard_map/ppermute | solution.py:49
  758.9 22.1 %collective-permute-start.26 = (bf16[2,2,512,256]{3,2,1,0:T(8,128)(2,1)S(1)}, bf16[2,2,512,256]{3,2,1,0:T(8,128)(2,1)S(1)}, u32[]{:S(2)}, u32[]{:S(2)}) collective-permute-start(bf16[2,2,512,256]{3,2,1,0:T(8,128)(2,1)S(1)} %broadcast_select_fusion.1), channel_id=1, source_target_pairs={{2,0},{4,2},{6,4},{7,6},{5,7},{3,5},{1,3},{0,1},{10,8},{12,10},{14... | collective-permute-start | bytes 3145736 | tf_op jit(solution)/shard_map/ppermute | solution.py:49
  772.0 14.9 %collective-permute-start.13 = (bf16[2,2,512,256]{3,2,1,0:T(8,128)(2,1)S(1)}, bf16[2,2,512,256]{3,2,1,0:T(8,128)(2,1)S(1)}, u32[]{:S(2)}, u32[]{:S(2)}) collective-permute-start(bf16[2,2,512,256]{3,2,1,0:T(8,128)(2,1)S(1)} %broadcast_select_fusion.7), channel_id=1, source_target_pairs={{0,2},{2,4},{4,6},{6,7},{7,5},{5,3},{3,1},{1,0},{8,10},{10,12},{12... | collective-permute-start | bytes 3145736 | tf_op jit(solution)/shard_map/ppermute | solution.py:49
  782.2 23.8 %collective-permute-start.27 = (bf16[2,2,512,256]{3,2,1,0:T(8,128)(2,1)}, bf16[2,2,512,256]{3,2,1,0:T(8,128)(2,1)}, u32[]{:S(2)}, u32[]{:S(2)}) collective-permute-start(bf16[2,2,512,256]{3,2,1,0:T(8,128)(2,1)} %broadcast_select_fusion), channel_id=1, source_target_pairs={{2,0},{4,2},{6,4},{7,6},{5,7},{3,5},{1,3},{0,1},{10,8},{12,10},{14... | collective-permute-start | bytes 3145736 | tf_op jit(solution)/shard_map/ppermute | solution.py:49
  (28 other events, 608.4 us)
Sparse Core Ops, SparseCore 0:
  133.8 104.9 all-gather.2
  250.6 104.7 all-gather.4

commit v7 on v3

--- a/solution.py
+++ b/solution.py
@@ -3,6 +3,8 @@
 import jax
 import jax.numpy as jnp
 from jax import lax
+from jax.experimental import pallas as pl
+from jax.experimental.pallas import tpu as pltpu
 from jax.sharding import PartitionSpec as P
 
 NT_REC = 1024
@@ -63,6 +65,35 @@
     return [jnp.concatenate([halves[0][p], halves[1][p]], axis=1) for p in range(len(values))]
 
 
+def spectrum_kernel(weight_ref, first_ref, second_ref, prior_ref, out_ref):
+    piece = first_ref.shape[1]
+    for half, source_ref in enumerate((first_ref, second_ref)):
+        early = source_ref[0].astype(jnp.float32)
+        late = source_ref[1].astype(jnp.float32)
+        rows = pl.ds(half * piece, piece)
+        for part in range(2):
+            total = weight_ref[2 * part] * early + weight_ref[2 * part + 1] * late
+            total = total.astype(jnp.bfloat16).astype(jnp.float32)
+            out_ref[part, rows, :] = (prior_ref[part, rows, :].astype(jnp.float32) + total).astype(jnp.bfloat16)
+
+
+def make_spectrum(weights, first, second, prior_block, piece):
+    parts, shots, columns = prior_block.shape
+    groups = first.shape[1] // piece
+    half_spec = pl.BlockSpec((parts, piece, columns), lambda g: (0, g, 0))
+    whole_spec = pl.BlockSpec((parts, 2 * piece, columns), lambda g: (0, g, 0))
+    return pl.pallas_call(
+        spectrum_kernel,
+        grid=(groups,),
+        in_specs=[pl.BlockSpec(memory_space=pltpu.SMEM), half_spec, half_spec, whole_spec],
+        out_specs=whole_spec,
+        out_shape=jax.ShapeDtypeStruct(prior_block.shape, jnp.bfloat16),
+        cost_estimate=pl.CostEstimate(
+            flops=8 * parts * shots * columns, transcendentals=0, bytes_accessed=6 * parts * shots * columns
+        ),
+    )(weights.reshape(-1), first, second, prior_block)
+
+
 def to_bf16(value):
     return lax.reduce_precision(value, exponent_bits=8, mantissa_bits=7).astype(jnp.bfloat16)
 
@@ -70,7 +101,6 @@
 def body(traces, prior, bins, panels):
     sample_count, shots_local, receivers = traces.shape
     row_count = lax.axis_size("row")
-    freq_count = lax.axis_size("freq")
     block_rows = receivers // row_count
     sample_index = BLOCK_START + jnp.arange(sample_count, dtype=jnp.int32)
     turn_count = bins[:, None] * sample_index[None, :] % NT_REC
@@ -79,40 +109,34 @@
     own_twiddle = lax.dynamic_index_in_dim(twiddle, lax.axis_index("freq"), 0, keepdims=False)
     weights = own_twiddle.astype(jnp.float32)
     piece = shots_local // PIECES
-    groups = freq_count * row_count
-    prior_blocks = prior[0].reshape(2, groups, PIECES, piece, block_rows)
-    parts = []
+    halves = []
     for index in range(PIECES):
         chunk = traces[:, index * piece:(index + 1) * piece, :]
         by_row = lax.all_to_all(chunk, "row", split_axis=2, concat_axis=1, tiled=True)
-        gathered = lax.all_gather(by_row, "freq", axis=1, tiled=True).astype(jnp.float32)
-        gathered = gathered.reshape(sample_count, groups, piece, block_rows)
-        transformed = weights[:, 0, None, None, None] * gathered[0] + weights[:, 1, None, None, None] * gathered[1]
-        transformed = lax.reduce_precision(transformed, exponent_bits=8, mantissa_bits=7)
-        parts.append(to_bf16(prior_blocks[:, :, index].astype(jnp.float32) + transformed))
-    spectrum = jnp.stack(parts, axis=2).reshape(2, receivers, block_rows)
+        halves.append(lax.all_gather(by_row, "freq", axis=1, tiled=True))
+    spectrum = make_spectrum(weights, halves[0], halves[1], prior[0], piece)
     panels_each = block_rows // PANEL
-    own_panels = []
-    owners = []
     lefts = []
+    rights = []
     for panel_step in range(STEPS):
         chosen = panels[panel_step]
-        owners.append(chosen // panels_each)
         offset = chosen % panels_each * PANEL
-        own_panels.append(lax.dynamic_slice_in_dim(spectrum, offset, PANEL, 2))
-        left = lax.dynamic_slice_in_dim(spectrum, chosen * PANEL, PANEL, 1)
-        lefts += [left[0], left[1]]
-    rights = broadcast(own_panels, owners, RING_CHUNKS)
-    reals = []
-    imags = []
-    for right in rights:
-        reals += [right[0], -right[1]]
-        imags += [right[1], right[0]]
-    left_all = jnp.concatenate(lefts, axis=0)
-    dims = (((0,), (1,)), ((), ()))
-    real_sum = lax.dot_general(left_all, jnp.concatenate(reals, axis=1), dims, preferred_element_type=jnp.float32)
-    imag_sum = lax.dot_general(left_all, jnp.concatenate(imags, axis=1), dims, preferred_element_type=jnp.float32)
-    return (jnp.stack([real_sum, imag_sum])[None].astype(jnp.bfloat16), spectrum[None])
+        own_rows = lax.dynamic_slice_in_dim(spectrum, offset, PANEL, 2)
+        rights.append(own_rows)
+        lefts.append(lax.dynamic_slice_in_dim(spectrum, chosen * PANEL, PANEL, 1))
+    owners = [panels[p] // panels_each for p in range(STEPS)]
+    rights = broadcast(rights, owners, RING_CHUNKS)
+    real_left = []
+    imag_left = []
+    shared = []
+    for left, right in zip(lefts, rights):
+        real_left += [left[0], -left[1]]
+        imag_left += [left[1], left[0]]
+        shared += [right[0], right[1]]
+    left_pair = jnp.stack([jnp.concatenate(real_left, axis=0), jnp.concatenate(imag_left, axis=0)])
+    dims = (((1,), (1,)), ((), ()))
+    sums = lax.dot_general(left_pair, jnp.concatenate(shared, axis=1), dims, preferred_element_type=jnp.float32)
+    return (sums[None].astype(jnp.bfloat16), spectrum[None])
 
 
 def solution(mesh):

time: 877 us -> 813 us (0.927)
  other arithmetic: 147 us -> 57.5 us
  Pallas kernels: 0 us -> 48 us
  local copies, waits for them, and re-layouts: 114 us -> 99.1 us
    pallas_call x0 -> x1, Pallas kernels: none -> 48 us  [make_spectrum(): pl.pallas_call(spectrum_kernel, grid=(groups,), in_specs=[pl.BlockSpec(me...]
    convert_element_type x1 -> x0, other arithmetic: 44 us -> none  [to_bf16(): lax.reduce_precision(value, exponent_bits=8, mantissa_bits=7)]
    another operation x3 -> x2, other arithmetic: 46 us -> 2.42 us  [the longest x1 2.3 us: body(): jnp.stack([jnp.concatenate(real_left, axis=0), jnp.concatenate(imag_left,...]
    slice x3 -> x0, local copies, waits for them, and re-layouts: 34.6 us -> none  [the longest x2 34.5 us: body(): gathered[0]]
    ppermute x56, waiting for transfers between devices: 203 us -> 185 us  [broadcast(): held = lax.ppermute(send, 'row', pairs)]
    all_gather x2, waiting for transfers between devices: 73.1 us -> 90.7 us  [body(): halves.append(lax.all_gather(by_row, 'freq', axis=1, tiled=True))]
    unnamed x84 -> x82, local copies, waits for them, and re-layouts: 38.6 us -> 52.3 us
    all_to_all x4 -> x2, local copies, waits for them, and re-layouts: 17.6 us -> 22.2 us  [body(): lax.all_to_all(chunk, 'row', split_axis=2, concat_axis=1, tiled=True)]
  transfers between devices with their start and end apart: 58 -> 58, of which waited for: 36 -> 29; matrix products, arithmetic and copies ran while one was open for 12% -> 13% of each run, Pallas kernels for 0% -> 0%
where the time goes in v7:
time: 813 us; the launch traced here: 810 us
  waiting for transfers between devices  276 us (34%)
  blocking collectives  198 us (24%)
  local copies, waits for them, and re-layouts  99.1 us (12%)
  starting transfers between devices  59.8 us (7%)
  other arithmetic  57.5 us (7%)
  Pallas kernels  48 us (6%)
  matrix products  45.9 us (6%)
  between operations  25.9 us (3%)
    all_to_all x2, blocking collectives, body(): lax.all_to_all(chunk, 'row', split_axis=2, concat_axis=1, tiled=True)  198 us
    ppermute x56, waiting for transfers between devices, broadcast(): held = lax.ppermute(send, 'row', pairs)  185 us
    all_gather x2, waiting for transfers between devices, body(): halves.append(lax.all_gather(by_row, 'freq', axis=1, tiled=True))  90.7 us
    ppermute x56, starting transfers between devices, broadcast(): held = lax.ppermute(send, 'row', pairs)  59.8 us
    unnamed x82, local copies, waits for them, and re-layouts  52.3 us
    pallas_call x1, Pallas kernels, make_spectrum(): pl.pallas_call(spectrum_kernel, grid=(groups,), in_specs=[pl.BlockSpec(me...  48 us
    dot_general x1, matrix products, body(): lax.dot_general(left_pair, jnp.concatenate(shared, axis=1), dims, preferr...  45.9 us
    select_n x56, other arithmetic, broadcast(): jnp.where(distance[p] == 0, own[p][:, min(step, chunks - 1)], held[p])  35.4 us
  transfers between devices with their start and end apart: 58, of which 29 were waited for; matrix products, arithmetic and copies ran while one was open for 13% of the time, Pallas kernels for 0%

profile of v7, /device:TPU:0, one launch (start us, length us, event | category | flops | bytes accessed | tf_op | source)
XLA Modules:
  0.0 809.5 jit_solution(8951205744969892930)
XLA Ops:
  7.2 6.0 fusion.51
  13.2 11.2 %copy.230 = bf16[2,128,8192]{1,0,2:T(2,128)(2,1)} copy(bf16[2,128,8192]{2,1,0:T(8,128)(2,1)} %get-tuple-element.19) | data formatting | bytes 8388608
  24.4 100.5 %all_to_all.36 = bf16[2,128,8192]{1,0,2:T(2,128)(2,1)} all-to-all(bf16[2,128,8192]{1,0,2:T(2,128)(2,1)} %copy.230), channel_id=1, replica_groups=mesh['freq'=4,'row'=8] {'row'}, dimensions={2} | all-to-all | bytes 8388608 | tf_op jit(solution)/shard_map/all_to_all | solution.py:115
  124.9 11.1 %copy.174 = bf16[2,128,8,1024]{3,1,2,0:T(8,128)(2,1)} copy(bf16[2,128,8,1024]{1,0,3,2:T(2,128)(2,1)} %bitcast.446) | data formatting | bytes 8388608 | tf_op jit(solution)/shard_map/all_to_all | solution.py:115
  136.1 11.4 %copy.231 = bf16[2,128,8192]{1,0,2:T(2,128)(2,1)} copy(bf16[2,128,8192]{2,1,0:T(8,128)(2,1)} %get-tuple-element.18) | data formatting | bytes 8388608
  147.6 97.0 %all_to_all.37 = bf16[2,128,8192]{1,0,2:T(2,128)(2,1)} all-to-all(bf16[2,128,8192]{1,0,2:T(2,128)(2,1)} %copy.231), channel_id=1, replica_groups=mesh['freq'=4,'row'=8] {'row'}, dimensions={2} | all-to-all | bytes 8388608 | tf_op jit(solution)/shard_map/all_to_all | solution.py:115
  244.6 11.1 %copy.176 = bf16[2,128,8,1024]{3,1,2,0:T(8,128)(2,1)} copy(bf16[2,128,8,1024]{1,0,3,2:T(2,128)(2,1)} %bitcast.447) | data formatting | bytes 8388608 | tf_op jit(solution)/shard_map/all_to_all | solution.py:115
  269.9 90.7 %all-gather.5.cloned.1.call-done.second_ref = bf16[2,4096,1024]{2,1,0:T(8,128)(2,1)} async-done(((bf16[2,1024,1024]{2,1,0:T(8,128)(2,1)}), bf16[2,4096,1024]{2,1,0:T(8,128)(2,1)}) %all-gather.5.cloned.1.call-update) | async-done | bytes 16777232 | tf_op jit(solution)/shard_map/all_gather | solution.py:116
  360.6 48.0 %shard_map.68 = bf16[2,8192,1024]{2,1,0:T(8,128)(2,1)} custom-call(f32[4]{0:T(128)} %reshape.182.weight_ref, bf16[2,4096,1024]{2,1,0:T(8,128)(2,1)} %all-gather.3.cloned.1.call-done.first_ref, bf16[2,4096,1024]{2,1,0:T(8,128)(2,1)} %all-gather.5.cloned.1.call-done.second_ref, bf16[2,8192,1024]{2,1,0:T(8,128)(2,1)} %bitcast.443), custom_call_target="tpu_custom_call" | custom-call | flops 134217728 | bytes 100663296 | tf_op jit(solution)/shard_map/pallas_call | solution.py:85
  408.6 6.6 constant_dynamic-slice_fusion
  425.7 4.5 collective-permute-done
  432.7 10.5 %collective-permute-done.42 = bf16[2,512,256]{2,1,0:T(8,128)(2,1)S(1)} collective-permute-done((bf16[2,512,256]{2,1,0:T(8,128)(2,1)S(1)}, bf16[2,512,256]{2,1,0:T(8,128)(2,1)S(1)}, u32[]{:S(2)}, u32[]{:S(2)}) %collective-permute-start.42) | collective-permute-done | bytes 524320 | tf_op jit(solution)/shard_map/ppermute | solution.py:54
  447.3 5.4 collective-permute-done.1
  455.1 10.5 %collective-permute-done.43 = bf16[2,512,256]{2,1,0:T(8,128)(2,1)S(1)} collective-permute-done((bf16[2,512,256]{2,1,0:T(8,128)(2,1)S(1)}, bf16[2,512,256]{2,1,0:T(8,128)(2,1)S(1)}, u32[]{:S(2)}, u32[]{:S(2)}) %collective-permute-start.43) | collective-permute-done | bytes 524320 | tf_op jit(solution)/shard_map/ppermute | solution.py:54
  469.7 5.4 collective-permute-done.2
  477.6 10.5 %collective-permute-done.44 = bf16[2,512,256]{2,1,0:T(8,128)(2,1)S(1)} collective-permute-done((bf16[2,512,256]{2,1,0:T(8,128)(2,1)S(1)}, bf16[2,512,256]{2,1,0:T(8,128)(2,1)S(1)}, u32[]{:S(2)}, u32[]{:S(2)}) %collective-permute-start.44) | collective-permute-done | bytes 524320 | tf_op jit(solution)/shard_map/ppermute | solution.py:54
  492.2 5.4 collective-permute-done.3
  500.1 10.5 %collective-permute-done.45 = bf16[2,512,256]{2,1,0:T(8,128)(2,1)S(1)} collective-permute-done((bf16[2,512,256]{2,1,0:T(8,128)(2,1)S(1)}, bf16[2,512,256]{2,1,0:T(8,128)(2,1)S(1)}, u32[]{:S(2)}, u32[]{:S(2)}) %collective-permute-start.45) | collective-permute-done | bytes 524320 | tf_op jit(solution)/shard_map/ppermute | solution.py:54
  514.6 5.4 collective-permute-done.4
  522.5 10.5 %collective-permute-done.46 = bf16[2,512,256]{2,1,0:T(8,128)(2,1)S(1)} collective-permute-done((bf16[2,512,256]{2,1,0:T(8,128)(2,1)S(1)}, bf16[2,512,256]{2,1,0:T(8,128)(2,1)S(1)}, u32[]{:S(2)}, u32[]{:S(2)}) %collective-permute-start.46) | collective-permute-done | bytes 524320 | tf_op jit(solution)/shard_map/ppermute | solution.py:54
  537.1 5.4 collective-permute-done.5
  545.0 10.5 %collective-permute-done.47 = bf16[2,512,256]{2,1,0:T(8,128)(2,1)S(1)} collective-permute-done((bf16[2,512,256]{2,1,0:T(8,128)(2,1)S(1)}, bf16[2,512,256]{2,1,0:T(8,128)(2,1)S(1)}, u32[]{:S(2)}, u32[]{:S(2)}) %collective-permute-start.47) | collective-permute-done | bytes 524320 | tf_op jit(solution)/shard_map/ppermute | solution.py:54
  559.6 5.4 collective-permute-done.6
  568.5 9.5 %collective-permute-done.48 = bf16[2,512,256]{2,1,0:T(8,128)(2,1)S(1)} collective-permute-done((bf16[2,512,256]{2,1,0:T(8,128)(2,1)S(1)}, bf16[2,512,256]{2,1,0:T(8,128)(2,1)S(1)}, u32[]{:S(2)}, u32[]{:S(2)}) %collective-permute-start.48) | collective-permute-done | bytes 524320 | tf_op jit(solution)/shard_map/ppermute | solution.py:54
  592.0 8.4 %collective-permute-done.49 = bf16[2,512,256]{2,1,0:T(8,128)(2,1)S(1)} collective-permute-done((bf16[2,512,256]{2,1,0:T(8,128)(2,1)S(1)}, bf16[2,512,256]{2,1,0:T(8,128)(2,1)S(1)}, u32[]{:S(2)}, u32[]{:S(2)}) %collective-permute-start.49) | collective-permute-done | bytes 524320 | tf_op jit(solution)/shard_map/ppermute | solution.py:54
  614.4 8.4 %collective-permute-done.50 = bf16[2,512,256]{2,1,0:T(8,128)(2,1)S(1)} collective-permute-done((bf16[2,512,256]{2,1,0:T(8,128)(2,1)S(1)}, bf16[2,512,256]{2,1,0:T(8,128)(2,1)S(1)}, u32[]{:S(2)}, u32[]{:S(2)}) %collective-permute-start.50) | collective-permute-done | bytes 524320 | tf_op jit(solution)/shard_map/ppermute | solution.py:54
  636.9 8.4 %collective-permute-done.51 = bf16[2,512,256]{2,1,0:T(8,128)(2,1)S(1)} collective-permute-done((bf16[2,512,256]{2,1,0:T(8,128)(2,1)S(1)}, bf16[2,512,256]{2,1,0:T(8,128)(2,1)S(1)}, u32[]{:S(2)}, u32[]{:S(2)}) %collective-permute-start.51) | collective-permute-done | bytes 524320 | tf_op jit(solution)/shard_map/ppermute | solution.py:54
  659.4 8.4 %collective-permute-done.52 = bf16[2,512,256]{2,1,0:T(8,128)(2,1)S(1)} collective-permute-done((bf16[2,512,256]{2,1,0:T(8,128)(2,1)S(1)}, bf16[2,512,256]{2,1,0:T(8,128)(2,1)S(1)}, u32[]{:S(2)}, u32[]{:S(2)}) %collective-permute-start.52) | collective-permute-done | bytes 524320 | tf_op jit(solution)/shard_map/ppermute | solution.py:54
  681.9 8.4 %collective-permute-done.53 = bf16[2,512,256]{2,1,0:T(8,128)(2,1)S(1)} collective-permute-done((bf16[2,512,256]{2,1,0:T(8,128)(2,1)S(1)}, bf16[2,512,256]{2,1,0:T(8,128)(2,1)S(1)}, u32[]{:S(2)}, u32[]{:S(2)}) %collective-permute-start.53) | collective-permute-done | bytes 524320 | tf_op jit(solution)/shard_map/ppermute | solution.py:54
  704.3 8.4 %collective-permute-done.54 = bf16[2,512,256]{2,1,0:T(8,128)(2,1)S(1)} collective-permute-done((bf16[2,512,256]{2,1,0:T(8,128)(2,1)S(1)}, bf16[2,512,256]{2,1,0:T(8,128)(2,1)S(1)}, u32[]{:S(2)}, u32[]{:S(2)}) %collective-permute-start.54) | collective-permute-done | bytes 524320 | tf_op jit(solution)/shard_map/ppermute | solution.py:54
  748.1 8.7 %fusion.7 = (bf16[8192,256]{1,0:T(8,128)(2,1)}, bf16[8192,256]{1,0:T(8,128)(2,1)}, bf16[8192,256]{1,0:T(8,128)(2,1)}, bf16[8192,256]{1,0:T(8,128)(2,1)}) fusion(bf16[2,4096,256]{2,1,0:T(8,128)(2,1)} %bitcast.451, bf16[2,4096,256]{2,1,0:T(8,128)(2,1)S(1)} %bitcast.448, bf16[2,4096,256]{2,1,0:T(8,128)(2,1)} %bitcast.450, bf16[2,4096,256]{2,1,0:T(8,128)(2,1)S(1)} %bitcast.449), kind=kLoop, calls=%fused_computation.13 | loop fusion | flops 33554432 | bytes 33554432 | tf_op jit(solution)/shard_map/squeeze | solution.py:135
  756.8 45.9 %convert_bitcast_fusion = bf16[1,2,1024,8192]{3,2,1,0:T(8,128)(2,1)} fusion(bf16[8192,256]{1,0:T(8,128)(2,1)} %get-tuple-element.17, bf16[8192,256]{1,0:T(8,128)(2,1)} %get-tuple-element.16, bf16[8192,256]{1,0:T(8,128)(2,1)} %get-tuple-element.29, bf16[8192,256]{1,0:T(8,128)(2,1)} %get-tuple-element.30, bf16[1,1024,1024]{2,1,0:T(8,128)(2,1)} %get-tuple-element.21, ...), kind=kOutput, calls=%fused_computation | convolution fusion | flops 34445721600 | bytes 54525952 | tf_op jit(solution)/shard_map/dot_general | solution.py:138
  (253 shorter events, 175.2 us)
Async XLA Ops:
  7.2 262.7 %all-gather.3.cloned.1.call-start = ((), (), s32[]{:S(2)}) async-start(), calls=%async_computation.2 | async-start | bytes 20971520 | tf_op jit(solution)/shard_map/all_gather | solution.py:116
  136.1 224.5 %all-gather.5.cloned.1.call-start = ((), (), s32[]{:S(2)}) async-start(), calls=%async_computation.3 | async-start | bytes 20971520 | tf_op jit(solution)/shard_map/all_gather | solution.py:116
  417.7 25.4 %collective-permute-start.42 = (bf16[2,512,256]{2,1,0:T(8,128)(2,1)S(1)}, bf16[2,512,256]{2,1,0:T(8,128)(2,1)S(1)}, u32[]{:S(2)}, u32[]{:S(2)}) collective-permute-start(bf16[2,512,256]{2,1,0:T(8,128)(2,1)S(1)} %fusion.22), channel_id=1, source_target_pairs={{2,0},{4,2},{6,4},{7,6},{5,7},{3,5},{1,3},{0,1},{10,8},{12,10},{14... | collective-permute-start | bytes 1572872 | tf_op jit(solution)/shard_map/ppermute | solution.py:54
  419.3 24.5 %collective-permute-start.28 = (bf16[2,512,256]{2,1,0:T(8,128)(2,1)S(1)}, bf16[2,512,256]{2,1,0:T(8,128)(2,1)S(1)}, u32[]{:S(2)}, u32[]{:S(2)}) collective-permute-start(bf16[2,512,256]{2,1,0:T(8,128)(2,1)S(1)} %fusion.29), channel_id=1, source_target_pairs={{0,2},{2,4},{4,6},{6,7},{7,5},{5,3},{3,1},{1,0},{8,10},{10,12},{12... | collective-permute-start | bytes 1572872 | tf_op jit(solution)/shard_map/ppermute | solution.py:54
  430.4 22.3 %collective-permute-start.1 = (bf16[2,512,256]{2,1,0:T(8,128)(2,1)S(1)}, bf16[2,512,256]{2,1,0:T(8,128)(2,1)S(1)}, u32[]{:S(2)}, u32[]{:S(2)}) collective-permute-start(bf16[2,512,256]{2,1,0:T(8,128)(2,1)S(1)} %fusion.42), channel_id=1, source_target_pairs={{0,2},{2,4},{4,6},{6,7},{7,5},{5,3},{3,1},{1,0},{8,10},{10,12},{12... | collective-permute-start | bytes 1572872 | tf_op jit(solution)/shard_map/ppermute | solution.py:54
  432.1 22.3 %collective-permute-start.15 = (bf16[2,512,256]{2,1,0:T(8,128)(2,1)S(1)}, bf16[2,512,256]{2,1,0:T(8,128)(2,1)S(1)}, u32[]{:S(2)}, u32[]{:S(2)}) collective-permute-start(bf16[2,512,256]{2,1,0:T(8,128)(2,1)S(1)} %fusion.35), channel_id=1, source_target_pairs={{2,0},{4,2},{6,4},{7,6},{5,7},{3,5},{1,3},{0,1},{10,8},{12,10},{14... | collective-permute-start | bytes 1572872 | tf_op jit(solution)/shard_map/ppermute | solution.py:54
  443.2 22.4 %collective-permute-start.43 = (bf16[2,512,256]{2,1,0:T(8,128)(2,1)S(1)}, bf16[2,512,256]{2,1,0:T(8,128)(2,1)S(1)}, u32[]{:S(2)}, u32[]{:S(2)}) collective-permute-start(bf16[2,512,256]{2,1,0:T(8,128)(2,1)S(1)} %fusion.20), channel_id=1, source_target_pairs={{2,0},{4,2},{6,4},{7,6},{5,7},{3,5},{1,3},{0,1},{10,8},{12,10},{14... | collective-permute-start | bytes 1572872 | tf_op jit(solution)/shard_map/ppermute | solution.py:54
  443.9 22.3 %collective-permute-start.29 = (bf16[2,512,256]{2,1,0:T(8,128)(2,1)S(1)}, bf16[2,512,256]{2,1,0:T(8,128)(2,1)S(1)}, u32[]{:S(2)}, u32[]{:S(2)}) collective-permute-start(bf16[2,512,256]{2,1,0:T(8,128)(2,1)S(1)} %fusion.28), channel_id=1, source_target_pairs={{0,2},{2,4},{4,6},{6,7},{7,5},{5,3},{3,1},{1,0},{8,10},{10,12},{12... | collective-permute-start | bytes 1572872 | tf_op jit(solution)/shard_map/ppermute | solution.py:54
  452.8 22.3 %collective-permute-start.2 = (bf16[2,512,256]{2,1,0:T(8,128)(2,1)S(1)}, bf16[2,512,256]{2,1,0:T(8,128)(2,1)S(1)}, u32[]{:S(2)}, u32[]{:S(2)}) collective-permute-start(bf16[2,512,256]{2,1,0:T(8,128)(2,1)S(1)} %fusion.41), channel_id=1, source_target_pairs={{0,2},{2,4},{4,6},{6,7},{7,5},{5,3},{3,1},{1,0},{8,10},{10,12},{12... | collective-permute-start | bytes 1572872 | tf_op jit(solution)/shard_map/ppermute | solution.py:54
  454.5 22.3 %collective-permute-start.16 = (bf16[2,512,256]{2,1,0:T(8,128)(2,1)S(1)}, bf16[2,512,256]{2,1,0:T(8,128)(2,1)S(1)}, u32[]{:S(2)}, u32[]{:S(2)}) collective-permute-start(bf16[2,512,256]{2,1,0:T(8,128)(2,1)S(1)} %fusion.34), channel_id=1, source_target_pairs={{2,0},{4,2},{6,4},{7,6},{5,7},{3,5},{1,3},{0,1},{10,8},{12,10},{14... | collective-permute-start | bytes 1572872 | tf_op jit(solution)/shard_map/ppermute | solution.py:54
  465.7 22.4 %collective-permute-start.44 = (bf16[2,512,256]{2,1,0:T(8,128)(2,1)S(1)}, bf16[2,512,256]{2,1,0:T(8,128)(2,1)S(1)}, u32[]{:S(2)}, u32[]{:S(2)}) collective-permute-start(bf16[2,512,256]{2,1,0:T(8,128)(2,1)S(1)} %fusion.19), channel_id=1, source_target_pairs={{2,0},{4,2},{6,4},{7,6},{5,7},{3,5},{1,3},{0,1},{10,8},{12,10},{14... | collective-permute-start | bytes 1572872 | tf_op jit(solution)/shard_map/ppermute | solution.py:54
  466.4 22.3 %collective-permute-start.30 = (bf16[2,512,256]{2,1,0:T(8,128)(2,1)S(1)}, bf16[2,512,256]{2,1,0:T(8,128)(2,1)S(1)}, u32[]{:S(2)}, u32[]{:S(2)}) collective-permute-start(bf16[2,512,256]{2,1,0:T(8,128)(2,1)S(1)} %fusion.27), channel_id=1, source_target_pairs={{0,2},{2,4},{4,6},{6,7},{7,5},{5,3},{3,1},{1,0},{8,10},{10,12},{12... | collective-permute-start | bytes 1572872 | tf_op jit(solution)/shard_map/ppermute | solution.py:54
  475.3 22.3 %collective-permute-start.3 = (bf16[2,512,256]{2,1,0:T(8,128)(2,1)S(1)}, bf16[2,512,256]{2,1,0:T(8,128)(2,1)S(1)}, u32[]{:S(2)}, u32[]{:S(2)}) collective-permute-start(bf16[2,512,256]{2,1,0:T(8,128)(2,1)S(1)} %fusion.40), channel_id=1, source_target_pairs={{0,2},{2,4},{4,6},{6,7},{7,5},{5,3},{3,1},{1,0},{8,10},{10,12},{12... | collective-permute-start | bytes 1572872 | tf_op jit(solution)/shard_map/ppermute | solution.py:54
  477.0 22.3 %collective-permute-start.17 = (bf16[2,512,256]{2,1,0:T(8,128)(2,1)S(1)}, bf16[2,512,256]{2,1,0:T(8,128)(2,1)S(1)}, u32[]{:S(2)}, u32[]{:S(2)}) collective-permute-start(bf16[2,512,256]{2,1,0:T(8,128)(2,1)S(1)} %fusion.33), channel_id=1, source_target_pairs={{2,0},{4,2},{6,4},{7,6},{5,7},{3,5},{1,3},{0,1},{10,8},{12,10},{14... | collective-permute-start | bytes 1572872 | tf_op jit(solution)/shard_map/ppermute | solution.py:54
  488.1 22.4 %collective-permute-start.45 = (bf16[2,512,256]{2,1,0:T(8,128)(2,1)S(1)}, bf16[2,512,256]{2,1,0:T(8,128)(2,1)S(1)}, u32[]{:S(2)}, u32[]{:S(2)}) collective-permute-start(bf16[2,512,256]{2,1,0:T(8,128)(2,1)S(1)} %fusion.18), channel_id=1, source_target_pairs={{2,0},{4,2},{6,4},{7,6},{5,7},{3,5},{1,3},{0,1},{10,8},{12,10},{14... | collective-permute-start | bytes 1572872 | tf_op jit(solution)/shard_map/ppermute | solution.py:54
  488.9 22.3 %collective-permute-start.31 = (bf16[2,512,256]{2,1,0:T(8,128)(2,1)S(1)}, bf16[2,512,256]{2,1,0:T(8,128)(2,1)S(1)}, u32[]{:S(2)}, u32[]{:S(2)}) collective-permute-start(bf16[2,512,256]{2,1,0:T(8,128)(2,1)S(1)} %fusion.26), channel_id=1, source_target_pairs={{0,2},{2,4},{4,6},{6,7},{7,5},{5,3},{3,1},{1,0},{8,10},{10,12},{12... | collective-permute-start | bytes 1572872 | tf_op jit(solution)/shard_map/ppermute | solution.py:54
  497.8 22.3 %collective-permute-start.4 = (bf16[2,512,256]{2,1,0:T(8,128)(2,1)S(1)}, bf16[2,512,256]{2,1,0:T(8,128)(2,1)S(1)}, u32[]{:S(2)}, u32[]{:S(2)}) collective-permute-start(bf16[2,512,256]{2,1,0:T(8,128)(2,1)S(1)} %fusion.39), channel_id=1, source_target_pairs={{0,2},{2,4},{4,6},{6,7},{7,5},{5,3},{3,1},{1,0},{8,10},{10,12},{12... | collective-permute-start | bytes 1572872 | tf_op jit(solution)/shard_map/ppermute | solution.py:54
  499.5 22.3 %collective-permute-start.18 = (bf16[2,512,256]{2,1,0:T(8,128)(2,1)S(1)}, bf16[2,512,256]{2,1,0:T(8,128)(2,1)S(1)}, u32[]{:S(2)}, u32[]{:S(2)}) collective-permute-start(bf16[2,512,256]{2,1,0:T(8,128)(2,1)S(1)} %fusion.32), channel_id=1, source_target_pairs={{2,0},{4,2},{6,4},{7,6},{5,7},{3,5},{1,3},{0,1},{10,8},{12,10},{14... | collective-permute-start | bytes 1572872 | tf_op jit(solution)/shard_map/ppermute | solution.py:54
  510.6 22.4 %collective-permute-start.46 = (bf16[2,512,256]{2,1,0:T(8,128)(2,1)S(1)}, bf16[2,512,256]{2,1,0:T(8,128)(2,1)S(1)}, u32[]{:S(2)}, u32[]{:S(2)}) collective-permute-start(bf16[2,512,256]{2,1,0:T(8,128)(2,1)S(1)} %fusion.17), channel_id=1, source_target_pairs={{2,0},{4,2},{6,4},{7,6},{5,7},{3,5},{1,3},{0,1},{10,8},{12,10},{14... | collective-permute-start | bytes 1572872 | tf_op jit(solution)/shard_map/ppermute | solution.py:54
  511.4 22.3 %collective-permute-start.32 = (bf16[2,512,256]{2,1,0:T(8,128)(2,1)S(1)}, bf16[2,512,256]{2,1,0:T(8,128)(2,1)S(1)}, u32[]{:S(2)}, u32[]{:S(2)}) collective-permute-start(bf16[2,512,256]{2,1,0:T(8,128)(2,1)S(1)} %fusion.25), channel_id=1, source_target_pairs={{0,2},{2,4},{4,6},{6,7},{7,5},{5,3},{3,1},{1,0},{8,10},{10,12},{12... | collective-permute-start | bytes 1572872 | tf_op jit(solution)/shard_map/ppermute | solution.py:54
  520.2 22.3 %collective-permute-start.5 = (bf16[2,512,256]{2,1,0:T(8,128)(2,1)S(1)}, bf16[2,512,256]{2,1,0:T(8,128)(2,1)S(1)}, u32[]{:S(2)}, u32[]{:S(2)}) collective-permute-start(bf16[2,512,256]{2,1,0:T(8,128)(2,1)S(1)} %fusion.38), channel_id=1, source_target_pairs={{0,2},{2,4},{4,6},{6,7},{7,5},{5,3},{3,1},{1,0},{8,10},{10,12},{12... | collective-permute-start | bytes 1572872 | tf_op jit(solution)/shard_map/ppermute | solution.py:54
  521.9 22.3 %collective-permute-start.19 = (bf16[2,512,256]{2,1,0:T(8,128)(2,1)S(1)}, bf16[2,512,256]{2,1,0:T(8,128)(2,1)S(1)}, u32[]{:S(2)}, u32[]{:S(2)}) collective-permute-start(bf16[2,512,256]{2,1,0:T(8,128)(2,1)S(1)} %fusion.31), channel_id=1, source_target_pairs={{2,0},{4,2},{6,4},{7,6},{5,7},{3,5},{1,3},{0,1},{10,8},{12,10},{14... | collective-permute-start | bytes 1572872 | tf_op jit(solution)/shard_map/ppermute | solution.py:54
  533.1 22.4 %collective-permute-start.47 = (bf16[2,512,256]{2,1,0:T(8,128)(2,1)S(1)}, bf16[2,512,256]{2,1,0:T(8,128)(2,1)S(1)}, u32[]{:S(2)}, u32[]{:S(2)}) collective-permute-start(bf16[2,512,256]{2,1,0:T(8,128)(2,1)S(1)} %fusion.16), channel_id=1, source_target_pairs={{2,0},{4,2},{6,4},{7,6},{5,7},{3,5},{1,3},{0,1},{10,8},{12,10},{14... | collective-permute-start | bytes 1572872 | tf_op jit(solution)/shard_map/ppermute | solution.py:54
  533.8 22.3 %collective-permute-start.33 = (bf16[2,512,256]{2,1,0:T(8,128)(2,1)S(1)}, bf16[2,512,256]{2,1,0:T(8,128)(2,1)S(1)}, u32[]{:S(2)}, u32[]{:S(2)}) collective-permute-start(bf16[2,512,256]{2,1,0:T(8,128)(2,1)S(1)} %fusion.24), channel_id=1, source_target_pairs={{0,2},{2,4},{4,6},{6,7},{7,5},{5,3},{3,1},{1,0},{8,10},{10,12},{12... | collective-permute-start | bytes 1572872 | tf_op jit(solution)/shard_map/ppermute | solution.py:54
  542.7 22.3 %collective-permute-start.6 = (bf16[2,512,256]{2,1,0:T(8,128)(2,1)S(1)}, bf16[2,512,256]{2,1,0:T(8,128)(2,1)S(1)}, u32[]{:S(2)}, u32[]{:S(2)}) collective-permute-start(bf16[2,512,256]{2,1,0:T(8,128)(2,1)S(1)} %fusion.37), channel_id=1, source_target_pairs={{0,2},{2,4},{4,6},{6,7},{7,5},{5,3},{3,1},{1,0},{8,10},{10,12},{12... | collective-permute-start | bytes 1572872 | tf_op jit(solution)/shard_map/ppermute | solution.py:54
  544.4 22.3 %collective-permute-start.20 = (bf16[2,512,256]{2,1,0:T(8,128)(2,1)S(1)}, bf16[2,512,256]{2,1,0:T(8,128)(2,1)S(1)}, u32[]{:S(2)}, u32[]{:S(2)}) collective-permute-start(bf16[2,512,256]{2,1,0:T(8,128)(2,1)S(1)} %fusion.30), channel_id=1, source_target_pairs={{2,0},{4,2},{6,4},{7,6},{5,7},{3,5},{1,3},{0,1},{10,8},{12,10},{14... | collective-permute-start | bytes 1572872 | tf_op jit(solution)/shard_map/ppermute | solution.py:54
  555.6 22.4 %collective-permute-start.48 = (bf16[2,512,256]{2,1,0:T(8,128)(2,1)S(1)}, bf16[2,512,256]{2,1,0:T(8,128)(2,1)S(1)}, u32[]{:S(2)}, u32[]{:S(2)}) collective-permute-start(bf16[2,512,256]{2,1,0:T(8,128)(2,1)S(1)} %fusion.15), channel_id=1, source_target_pairs={{2,0},{4,2},{6,4},{7,6},{5,7},{3,5},{1,3},{0,1},{10,8},{12,10},{14... | collective-permute-start | bytes 1572872 | tf_op jit(solution)/shard_map/ppermute | solution.py:54
  556.3 23.3 %collective-permute-start.34 = (bf16[2,512,256]{2,1,0:T(8,128)(2,1)S(1)}, bf16[2,512,256]{2,1,0:T(8,128)(2,1)S(1)}, u32[]{:S(2)}, u32[]{:S(2)}) collective-permute-start(bf16[2,512,256]{2,1,0:T(8,128)(2,1)S(1)} %fusion.23), channel_id=1, source_target_pairs={{0,2},{2,4},{4,6},{6,7},{7,5},{5,3},{3,1},{1,0},{8,10},{10,12},{12... | collective-permute-start | bytes 1572872 | tf_op jit(solution)/shard_map/ppermute | solution.py:54
  565.2 22.3 %collective-permute-start.7 = (bf16[2,512,256]{2,1,0:T(8,128)(2,1)S(1)}, bf16[2,512,256]{2,1,0:T(8,128)(2,1)S(1)}, u32[]{:S(2)}, u32[]{:S(2)}) collective-permute-start(bf16[2,512,256]{2,1,0:T(8,128)(2,1)S(1)} %broadcast_select_fusion.27), channel_id=1, source_target_pairs={{0,2},{2,4},{4,6},{6,7},{7,5},{5,3},{3,1},{1,0},{8,10},{10,12},{12... | collective-permute-start | bytes 1572872 | tf_op jit(solution)/shard_map/ppermute | solution.py:54
  567.9 22.3 %collective-permute-start.21 = (bf16[2,512,256]{2,1,0:T(8,128)(2,1)S(1)}, bf16[2,512,256]{2,1,0:T(8,128)(2,1)S(1)}, u32[]{:S(2)}, u32[]{:S(2)}) collective-permute-start(bf16[2,512,256]{2,1,0:T(8,128)(2,1)S(1)} %broadcast_select_fusion.20), channel_id=1, source_target_pairs={{2,0},{4,2},{6,4},{7,6},{5,7},{3,5},{1,3},{0,1},{10,8},{12,10},{14... | collective-permute-start | bytes 1572872 | tf_op jit(solution)/shard_map/ppermute | solution.py:54
  703.7 24.1 %collective-permute-start.27 = (bf16[2,512,256]{2,1,0:T(8,128)(2,1)S(1)}, bf16[2,512,256]{2,1,0:T(8,128)(2,1)S(1)}, u32[]{:S(2)}, u32[]{:S(2)}) collective-permute-start(bf16[2,512,256]{2,1,0:T(8,128)(2,1)S(1)} %broadcast_select_fusion.14), channel_id=1, source_target_pairs={{2,0},{4,2},{6,4},{7,6},{5,7},{3,5},{1,3},{0,1},{10,8},{12,10},{14... | collective-permute-start | bytes 1572872 | tf_op jit(solution)/shard_map/ppermute | solution.py:54
  713.9 30.2 %collective-permute-start.55 = (bf16[2,512,256]{2,1,0:T(8,128)(2,1)S(1)}, bf16[2,512,256]{2,1,0:T(8,128)(2,1)S(1)}, u32[]{:S(2)}, u32[]{:S(2)}) collective-permute-start(bf16[2,512,256]{2,1,0:T(8,128)(2,1)S(1)} %broadcast_select_fusion), channel_id=1, source_target_pairs={{2,0},{4,2},{6,4},{7,6},{5,7},{3,5},{1,3},{0,1},{10,8},{12,10},{14... | collective-permute-start | bytes 1572872 | tf_op jit(solution)/shard_map/ppermute | solution.py:54
  (40 other events, 1164.1 us)
Sparse Core Ops, SparseCore 0:
  136.2 104.9 all-gather.2
  255.8 104.6 all-gather.4

commit v8 on v7

--- a/solution.py
+++ b/solution.py
@@ -65,33 +65,41 @@
     return [jnp.concatenate([halves[0][p], halves[1][p]], axis=1) for p in range(len(values))]
 
 
-def spectrum_kernel(weight_ref, first_ref, second_ref, prior_ref, out_ref):
-    piece = first_ref.shape[1]
-    for half, source_ref in enumerate((first_ref, second_ref)):
-        early = source_ref[0].astype(jnp.float32)
-        late = source_ref[1].astype(jnp.float32)
-        rows = pl.ds(half * piece, piece)
-        for part in range(2):
-            total = weight_ref[2 * part] * early + weight_ref[2 * part + 1] * late
-            total = total.astype(jnp.bfloat16).astype(jnp.float32)
-            out_ref[part, rows, :] = (prior_ref[part, rows, :].astype(jnp.float32) + total).astype(jnp.bfloat16)
+def spectrum_kernel(weight_ref, source_ref, prior_ref, *rest):
+    out_ref = rest[-1]
+    early = source_ref[0].astype(jnp.float32)
+    late = source_ref[1].astype(jnp.float32)
+    for part in range(2):
+        total = weight_ref[2 * part] * early + weight_ref[2 * part + 1] * late
+        total = total.astype(jnp.bfloat16).astype(jnp.float32)
+        out_ref[part] = (prior_ref[part].astype(jnp.float32) + total).astype(jnp.bfloat16)
 
 
 def make_spectrum(weights, first, second, prior_block, piece):
     parts, shots, columns = prior_block.shape
     groups = first.shape[1] // piece
     half_spec = pl.BlockSpec((parts, piece, columns), lambda g: (0, g, 0))
-    whole_spec = pl.BlockSpec((parts, 2 * piece, columns), lambda g: (0, g, 0))
-    return pl.pallas_call(
-        spectrum_kernel,
-        grid=(groups,),
-        in_specs=[pl.BlockSpec(memory_space=pltpu.SMEM), half_spec, half_spec, whole_spec],
-        out_specs=whole_spec,
-        out_shape=jax.ShapeDtypeStruct(prior_block.shape, jnp.bfloat16),
-        cost_estimate=pl.CostEstimate(
-            flops=8 * parts * shots * columns, transcendentals=0, bytes_accessed=6 * parts * shots * columns
-        ),
-    )(weights.reshape(-1), first, second, prior_block)
+    cost = pl.CostEstimate(flops=4 * parts * shots * columns, transcendentals=0, bytes_accessed=3 * parts * shots * columns)
+    result = None
+    for half, source in enumerate((first, second)):
+        place_spec = pl.BlockSpec((parts, piece, columns), lambda g, half=half: (0, 2 * g + half, 0))
+        operands = [weights.reshape(-1), source, prior_block]
+        in_specs = [pl.BlockSpec(memory_space=pltpu.SMEM), half_spec, place_spec]
+        aliases = {}
+        if result is not None:
+            operands.append(result)
+            in_specs.append(pl.BlockSpec(memory_space=pl.ANY))
+            aliases = {3: 0}
+        result = pl.pallas_call(
+            spectrum_kernel,
+            grid=(groups,),
+            in_specs=in_specs,
+            out_specs=place_spec,
+            out_shape=jax.ShapeDtypeStruct(prior_block.shape, jnp.bfloat16),
+            input_output_aliases=aliases,
+            cost_estimate=cost,
+        )(*operands)
+    return result
 
 
 def to_bf16(value):

time: 813 us -> 796 us (0.979)
  waiting for transfers between devices: 276 us -> 245 us
  Pallas kernels: 48 us -> 60.5 us
    all_gather x2, waiting for transfers between devices: 90.7 us -> 60.3 us  [body(): halves.append(lax.all_gather(by_row, 'freq', axis=1, tiled=True))]
    pallas_call x1 -> x2, Pallas kernels: 48 us -> 60.5 us  [make_spectrum(): pl.pallas_call(spectrum_kernel, grid=(groups,), in_specs=in_specs, out_sp...]
  transfers between devices with their start and end apart: 58 -> 58, of which waited for: 29 -> 29; matrix products, arithmetic and copies ran while one was open for 13% -> 13% of each run, Pallas kernels for 0% -> 4%
where the time goes in v8:
time: 796 us; the launch traced here: 791 us
  waiting for transfers between devices  245 us (31%)
  blocking collectives  198 us (25%)
  local copies, waits for them, and re-layouts  98.9 us (12%)
  Pallas kernels  60.5 us (8%)
  starting transfers between devices  59.8 us (8%)
  other arithmetic  57.5 us (7%)
  matrix products  45.9 us (6%)
  between operations  25.9 us (3%)
    all_to_all x2, blocking collectives, body(): lax.all_to_all(chunk, 'row', split_axis=2, concat_axis=1, tiled=True)  198 us
    ppermute x56, waiting for transfers between devices, broadcast(): held = lax.ppermute(send, 'row', pairs)  185 us
    pallas_call x2, Pallas kernels, make_spectrum(): pl.pallas_call(spectrum_kernel, grid=(groups,), in_specs=in_specs, out_sp...  60.5 us
    all_gather x2, waiting for transfers between devices, body(): halves.append(lax.all_gather(by_row, 'freq', axis=1, tiled=True))  60.3 us
    ppermute x56, starting transfers between devices, broadcast(): held = lax.ppermute(send, 'row', pairs)  59.8 us
    unnamed x82, local copies, waits for them, and re-layouts  52.3 us
    dot_general x1, matrix products, body(): lax.dot_general(left_pair, jnp.concatenate(shared, axis=1), dims, preferr...  45.9 us
    select_n x56, other arithmetic, broadcast(): jnp.where(distance[p] == 0, own[p][:, min(step, chunks - 1)], held[p])  35.4 us
  transfers between devices with their start and end apart: 58, of which 29 were waited for; matrix products, arithmetic and copies ran while one was open for 13% of the time, Pallas kernels for 4%

profile of v8, /device:TPU:0, one launch (start us, length us, event | category | flops | bytes accessed | tf_op | source)
XLA Modules:
  0.0 791.3 jit_solution(6829033329893822017)
XLA Ops:
  7.2 6.0 fusion.51
  13.2 11.2 %copy.232 = bf16[2,128,8192]{1,0,2:T(2,128)(2,1)} copy(bf16[2,128,8192]{2,1,0:T(8,128)(2,1)} %get-tuple-element.18) | data formatting | bytes 8388608
  24.4 100.5 %all_to_all.36 = bf16[2,128,8192]{1,0,2:T(2,128)(2,1)} all-to-all(bf16[2,128,8192]{1,0,2:T(2,128)(2,1)} %copy.232), channel_id=1, replica_groups=mesh['freq'=4,'row'=8] {'row'}, dimensions={2} | all-to-all | bytes 8388608 | tf_op jit(solution)/shard_map/all_to_all | solution.py:123
  124.9 11.2 %copy.177 = bf16[2,128,8,1024]{3,1,2,0:T(8,128)(2,1)} copy(bf16[2,128,8,1024]{1,0,3,2:T(2,128)(2,1)} %bitcast.447) | data formatting | bytes 8388608 | tf_op jit(solution)/shard_map/all_to_all | solution.py:123
  136.2 11.4 %copy.231 = bf16[2,128,8192]{1,0,2:T(2,128)(2,1)} copy(bf16[2,128,8192]{2,1,0:T(8,128)(2,1)} %get-tuple-element.19) | data formatting | bytes 8388608
  147.6 97.0 %all_to_all.37 = bf16[2,128,8192]{1,0,2:T(2,128)(2,1)} all-to-all(bf16[2,128,8192]{1,0,2:T(2,128)(2,1)} %copy.231), channel_id=1, replica_groups=mesh['freq'=4,'row'=8] {'row'}, dimensions={2} | all-to-all | bytes 8388608 | tf_op jit(solution)/shard_map/all_to_all | solution.py:123
  244.6 11.1 %copy.175 = bf16[2,128,8,1024]{3,1,2,0:T(8,128)(2,1)} copy(bf16[2,128,8,1024]{1,0,3,2:T(2,128)(2,1)} %bitcast.448) | data formatting | bytes 8388608 | tf_op jit(solution)/shard_map/all_to_all | solution.py:123
  269.8 30.6 %shard_map.68.rest_0_ = bf16[2,8192,1024]{2,1,0:T(8,128)(2,1)} custom-call(f32[4]{0:T(128)} %reshape.183.weight_ref, bf16[2,4096,1024]{2,1,0:T(8,128)(2,1)} %all-gather.5.cloned.1.call-done.source_ref, bf16[2,8192,1024]{2,1,0:T(8,128)(2,1)} %bitcast.383), custom_call_target="tpu_custom_call" | custom-call | flops 67108864 | bytes 50331648 | tf_op jit(solution)/shard_map/pallas_call | solution.py:93
  300.3 60.3 %all-gather.3.cloned.1.call-done.source_ref = bf16[2,4096,1024]{2,1,0:T(8,128)(2,1)} async-done(((bf16[2,1024,1024]{2,1,0:T(8,128)(2,1)}), bf16[2,4096,1024]{2,1,0:T(8,128)(2,1)}) %all-gather.3.cloned.1.call-update) | async-done | bytes 16777232 | tf_op jit(solution)/shard_map/all_gather | solution.py:124
  360.6 29.9 %shard_map.69 = bf16[2,8192,1024]{2,1,0:T(8,128)(2,1)} custom-call(f32[4]{0:T(128)} %reshape.183.weight_ref, bf16[2,4096,1024]{2,1,0:T(8,128)(2,1)} %all-gather.3.cloned.1.call-done.source_ref, bf16[2,8192,1024]{2,1,0:T(8,128)(2,1)} %bitcast.384, bf16[2,8192,1024]{2,1,0:T(8,128)(2,1)} %shard_map.68.rest_0_), custom_call_target="tpu_custom_call", output_to_operand_aliasing={{}: (3, {})} | custom-call | flops 67108864 | bytes 50331648 | tf_op jit(solution)/shard_map/pallas_call | solution.py:93
  390.5 6.5 constant_dynamic-slice_fusion
  414.5 10.5 %collective-permute-done.42 = bf16[2,512,256]{2,1,0:T(8,128)(2,1)S(1)} collective-permute-done((bf16[2,512,256]{2,1,0:T(8,128)(2,1)S(1)}, bf16[2,512,256]{2,1,0:T(8,128)(2,1)S(1)}, u32[]{:S(2)}, u32[]{:S(2)}) %collective-permute-start.42) | collective-permute-done | bytes 524320 | tf_op jit(solution)/shard_map/ppermute | solution.py:54
  429.1 5.4 collective-permute-done.1
  437.0 10.5 %collective-permute-done.43 = bf16[2,512,256]{2,1,0:T(8,128)(2,1)S(1)} collective-permute-done((bf16[2,512,256]{2,1,0:T(8,128)(2,1)S(1)}, bf16[2,512,256]{2,1,0:T(8,128)(2,1)S(1)}, u32[]{:S(2)}, u32[]{:S(2)}) %collective-permute-start.43) | collective-permute-done | bytes 524320 | tf_op jit(solution)/shard_map/ppermute | solution.py:54
  451.5 5.4 collective-permute-done.2
  459.4 10.5 %collective-permute-done.44 = bf16[2,512,256]{2,1,0:T(8,128)(2,1)S(1)} collective-permute-done((bf16[2,512,256]{2,1,0:T(8,128)(2,1)S(1)}, bf16[2,512,256]{2,1,0:T(8,128)(2,1)S(1)}, u32[]{:S(2)}, u32[]{:S(2)}) %collective-permute-start.44) | collective-permute-done | bytes 524320 | tf_op jit(solution)/shard_map/ppermute | solution.py:54
  474.0 5.4 collective-permute-done.3
  481.9 10.5 %collective-permute-done.45 = bf16[2,512,256]{2,1,0:T(8,128)(2,1)S(1)} collective-permute-done((bf16[2,512,256]{2,1,0:T(8,128)(2,1)S(1)}, bf16[2,512,256]{2,1,0:T(8,128)(2,1)S(1)}, u32[]{:S(2)}, u32[]{:S(2)}) %collective-permute-start.45) | collective-permute-done | bytes 524320 | tf_op jit(solution)/shard_map/ppermute | solution.py:54
  496.5 5.4 collective-permute-done.4
  504.4 10.5 %collective-permute-done.46 = bf16[2,512,256]{2,1,0:T(8,128)(2,1)S(1)} collective-permute-done((bf16[2,512,256]{2,1,0:T(8,128)(2,1)S(1)}, bf16[2,512,256]{2,1,0:T(8,128)(2,1)S(1)}, u32[]{:S(2)}, u32[]{:S(2)}) %collective-permute-start.46) | collective-permute-done | bytes 524320 | tf_op jit(solution)/shard_map/ppermute | solution.py:54
  519.0 5.4 collective-permute-done.5
  526.8 10.5 %collective-permute-done.47 = bf16[2,512,256]{2,1,0:T(8,128)(2,1)S(1)} collective-permute-done((bf16[2,512,256]{2,1,0:T(8,128)(2,1)S(1)}, bf16[2,512,256]{2,1,0:T(8,128)(2,1)S(1)}, u32[]{:S(2)}, u32[]{:S(2)}) %collective-permute-start.47) | collective-permute-done | bytes 524320 | tf_op jit(solution)/shard_map/ppermute | solution.py:54
  541.4 5.4 collective-permute-done.6
  550.3 9.5 %collective-permute-done.48 = bf16[2,512,256]{2,1,0:T(8,128)(2,1)S(1)} collective-permute-done((bf16[2,512,256]{2,1,0:T(8,128)(2,1)S(1)}, bf16[2,512,256]{2,1,0:T(8,128)(2,1)S(1)}, u32[]{:S(2)}, u32[]{:S(2)}) %collective-permute-start.48) | collective-permute-done | bytes 524320 | tf_op jit(solution)/shard_map/ppermute | solution.py:54
  573.8 8.4 %collective-permute-done.49 = bf16[2,512,256]{2,1,0:T(8,128)(2,1)S(1)} collective-permute-done((bf16[2,512,256]{2,1,0:T(8,128)(2,1)S(1)}, bf16[2,512,256]{2,1,0:T(8,128)(2,1)S(1)}, u32[]{:S(2)}, u32[]{:S(2)}) %collective-permute-start.49) | collective-permute-done | bytes 524320 | tf_op jit(solution)/shard_map/ppermute | solution.py:54
  596.3 8.4 %collective-permute-done.50 = bf16[2,512,256]{2,1,0:T(8,128)(2,1)S(1)} collective-permute-done((bf16[2,512,256]{2,1,0:T(8,128)(2,1)S(1)}, bf16[2,512,256]{2,1,0:T(8,128)(2,1)S(1)}, u32[]{:S(2)}, u32[]{:S(2)}) %collective-permute-start.50) | collective-permute-done | bytes 524320 | tf_op jit(solution)/shard_map/ppermute | solution.py:54
  618.7 8.4 %collective-permute-done.51 = bf16[2,512,256]{2,1,0:T(8,128)(2,1)S(1)} collective-permute-done((bf16[2,512,256]{2,1,0:T(8,128)(2,1)S(1)}, bf16[2,512,256]{2,1,0:T(8,128)(2,1)S(1)}, u32[]{:S(2)}, u32[]{:S(2)}) %collective-permute-start.51) | collective-permute-done | bytes 524320 | tf_op jit(solution)/shard_map/ppermute | solution.py:54
  641.2 8.4 %collective-permute-done.52 = bf16[2,512,256]{2,1,0:T(8,128)(2,1)S(1)} collective-permute-done((bf16[2,512,256]{2,1,0:T(8,128)(2,1)S(1)}, bf16[2,512,256]{2,1,0:T(8,128)(2,1)S(1)}, u32[]{:S(2)}, u32[]{:S(2)}) %collective-permute-start.52) | collective-permute-done | bytes 524320 | tf_op jit(solution)/shard_map/ppermute | solution.py:54
  663.7 8.4 %collective-permute-done.53 = bf16[2,512,256]{2,1,0:T(8,128)(2,1)S(1)} collective-permute-done((bf16[2,512,256]{2,1,0:T(8,128)(2,1)S(1)}, bf16[2,512,256]{2,1,0:T(8,128)(2,1)S(1)}, u32[]{:S(2)}, u32[]{:S(2)}) %collective-permute-start.53) | collective-permute-done | bytes 524320 | tf_op jit(solution)/shard_map/ppermute | solution.py:54
  686.2 8.4 %collective-permute-done.54 = bf16[2,512,256]{2,1,0:T(8,128)(2,1)S(1)} collective-permute-done((bf16[2,512,256]{2,1,0:T(8,128)(2,1)S(1)}, bf16[2,512,256]{2,1,0:T(8,128)(2,1)S(1)}, u32[]{:S(2)}, u32[]{:S(2)}) %collective-permute-start.54) | collective-permute-done | bytes 524320 | tf_op jit(solution)/shard_map/ppermute | solution.py:54
  729.9 8.7 %fusion.7 = (bf16[8192,256]{1,0:T(8,128)(2,1)}, bf16[8192,256]{1,0:T(8,128)(2,1)}, bf16[8192,256]{1,0:T(8,128)(2,1)}, bf16[8192,256]{1,0:T(8,128)(2,1)}) fusion(bf16[2,4096,256]{2,1,0:T(8,128)(2,1)} %bitcast.452, bf16[2,4096,256]{2,1,0:T(8,128)(2,1)S(1)} %bitcast.449, bf16[2,4096,256]{2,1,0:T(8,128)(2,1)} %bitcast.451, bf16[2,4096,256]{2,1,0:T(8,128)(2,1)S(1)} %bitcast.450), kind=kLoop, calls=%fused_computation.13 | loop fusion | flops 33554432 | bytes 33554432 | tf_op jit(solution)/shard_map/squeeze | solution.py:143
  738.6 45.9 %convert_bitcast_fusion = bf16[1,2,1024,8192]{3,2,1,0:T(8,128)(2,1)} fusion(bf16[8192,256]{1,0:T(8,128)(2,1)} %get-tuple-element.17, bf16[8192,256]{1,0:T(8,128)(2,1)} %get-tuple-element.16, bf16[8192,256]{1,0:T(8,128)(2,1)} %get-tuple-element.29, bf16[8192,256]{1,0:T(8,128)(2,1)} %get-tuple-element.30, bf16[1,1024,1024]{2,1,0:T(8,128)(2,1)} %get-tuple-element.21, ...), kind=kOutput, calls=%fused_computation | convolution fusion | flops 34445721600 | bytes 54525952 | tf_op jit(solution)/shard_map/dot_general | solution.py:146
  (254 shorter events, 179.6 us)
Async XLA Ops:
  7.2 262.6 %all-gather.5.cloned.1.call-start = ((), (), s32[]{:S(2)}) async-start(), calls=%async_computation.3 | async-start | bytes 20971520 | tf_op jit(solution)/shard_map/all_gather | solution.py:124
  136.1 224.5 %all-gather.3.cloned.1.call-start = ((), (), s32[]{:S(2)}) async-start(), calls=%async_computation.2 | async-start | bytes 20971520 | tf_op jit(solution)/shard_map/all_gather | solution.py:124
  399.5 25.4 %collective-permute-start.42 = (bf16[2,512,256]{2,1,0:T(8,128)(2,1)S(1)}, bf16[2,512,256]{2,1,0:T(8,128)(2,1)S(1)}, u32[]{:S(2)}, u32[]{:S(2)}) collective-permute-start(bf16[2,512,256]{2,1,0:T(8,128)(2,1)S(1)} %fusion.22), channel_id=1, source_target_pairs={{2,0},{4,2},{6,4},{7,6},{5,7},{3,5},{1,3},{0,1},{10,8},{12,10},{14... | collective-permute-start | bytes 1572872 | tf_op jit(solution)/shard_map/ppermute | solution.py:54
  401.1 24.5 %collective-permute-start.28 = (bf16[2,512,256]{2,1,0:T(8,128)(2,1)S(1)}, bf16[2,512,256]{2,1,0:T(8,128)(2,1)S(1)}, u32[]{:S(2)}, u32[]{:S(2)}) collective-permute-start(bf16[2,512,256]{2,1,0:T(8,128)(2,1)S(1)} %fusion.29), channel_id=1, source_target_pairs={{0,2},{2,4},{4,6},{6,7},{7,5},{5,3},{3,1},{1,0},{8,10},{10,12},{12... | collective-permute-start | bytes 1572872 | tf_op jit(solution)/shard_map/ppermute | solution.py:54
  412.2 22.3 %collective-permute-start.1 = (bf16[2,512,256]{2,1,0:T(8,128)(2,1)S(1)}, bf16[2,512,256]{2,1,0:T(8,128)(2,1)S(1)}, u32[]{:S(2)}, u32[]{:S(2)}) collective-permute-start(bf16[2,512,256]{2,1,0:T(8,128)(2,1)S(1)} %fusion.42), channel_id=1, source_target_pairs={{0,2},{2,4},{4,6},{6,7},{7,5},{5,3},{3,1},{1,0},{8,10},{10,12},{12... | collective-permute-start | bytes 1572872 | tf_op jit(solution)/shard_map/ppermute | solution.py:54
  413.9 22.3 %collective-permute-start.15 = (bf16[2,512,256]{2,1,0:T(8,128)(2,1)S(1)}, bf16[2,512,256]{2,1,0:T(8,128)(2,1)S(1)}, u32[]{:S(2)}, u32[]{:S(2)}) collective-permute-start(bf16[2,512,256]{2,1,0:T(8,128)(2,1)S(1)} %fusion.35), channel_id=1, source_target_pairs={{2,0},{4,2},{6,4},{7,6},{5,7},{3,5},{1,3},{0,1},{10,8},{12,10},{14... | collective-permute-start | bytes 1572872 | tf_op jit(solution)/shard_map/ppermute | solution.py:54
  425.0 22.4 %collective-permute-start.43 = (bf16[2,512,256]{2,1,0:T(8,128)(2,1)S(1)}, bf16[2,512,256]{2,1,0:T(8,128)(2,1)S(1)}, u32[]{:S(2)}, u32[]{:S(2)}) collective-permute-start(bf16[2,512,256]{2,1,0:T(8,128)(2,1)S(1)} %fusion.20), channel_id=1, source_target_pairs={{2,0},{4,2},{6,4},{7,6},{5,7},{3,5},{1,3},{0,1},{10,8},{12,10},{14... | collective-permute-start | bytes 1572872 | tf_op jit(solution)/shard_map/ppermute | solution.py:54
  425.8 22.3 %collective-permute-start.29 = (bf16[2,512,256]{2,1,0:T(8,128)(2,1)S(1)}, bf16[2,512,256]{2,1,0:T(8,128)(2,1)S(1)}, u32[]{:S(2)}, u32[]{:S(2)}) collective-permute-start(bf16[2,512,256]{2,1,0:T(8,128)(2,1)S(1)} %fusion.28), channel_id=1, source_target_pairs={{0,2},{2,4},{4,6},{6,7},{7,5},{5,3},{3,1},{1,0},{8,10},{10,12},{12... | collective-permute-start | bytes 1572872 | tf_op jit(solution)/shard_map/ppermute | solution.py:54
  434.7 22.3 %collective-permute-start.2 = (bf16[2,512,256]{2,1,0:T(8,128)(2,1)S(1)}, bf16[2,512,256]{2,1,0:T(8,128)(2,1)S(1)}, u32[]{:S(2)}, u32[]{:S(2)}) collective-permute-start(bf16[2,512,256]{2,1,0:T(8,128)(2,1)S(1)} %fusion.41), channel_id=1, source_target_pairs={{0,2},{2,4},{4,6},{6,7},{7,5},{5,3},{3,1},{1,0},{8,10},{10,12},{12... | collective-permute-start | bytes 1572872 | tf_op jit(solution)/shard_map/ppermute | solution.py:54
  436.4 22.3 %collective-permute-start.16 = (bf16[2,512,256]{2,1,0:T(8,128)(2,1)S(1)}, bf16[2,512,256]{2,1,0:T(8,128)(2,1)S(1)}, u32[]{:S(2)}, u32[]{:S(2)}) collective-permute-start(bf16[2,512,256]{2,1,0:T(8,128)(2,1)S(1)} %fusion.34), channel_id=1, source_target_pairs={{2,0},{4,2},{6,4},{7,6},{5,7},{3,5},{1,3},{0,1},{10,8},{12,10},{14... | collective-permute-start | bytes 1572872 | tf_op jit(solution)/shard_map/ppermute | solution.py:54
  447.5 22.4 %collective-permute-start.44 = (bf16[2,512,256]{2,1,0:T(8,128)(2,1)S(1)}, bf16[2,512,256]{2,1,0:T(8,128)(2,1)S(1)}, u32[]{:S(2)}, u32[]{:S(2)}) collective-permute-start(bf16[2,512,256]{2,1,0:T(8,128)(2,1)S(1)} %fusion.19), channel_id=1, source_target_pairs={{2,0},{4,2},{6,4},{7,6},{5,7},{3,5},{1,3},{0,1},{10,8},{12,10},{14... | collective-permute-start | bytes 1572872 | tf_op jit(solution)/shard_map/ppermute | solution.py:54
  448.2 22.3 %collective-permute-start.30 = (bf16[2,512,256]{2,1,0:T(8,128)(2,1)S(1)}, bf16[2,512,256]{2,1,0:T(8,128)(2,1)S(1)}, u32[]{:S(2)}, u32[]{:S(2)}) collective-permute-start(bf16[2,512,256]{2,1,0:T(8,128)(2,1)S(1)} %fusion.27), channel_id=1, source_target_pairs={{0,2},{2,4},{4,6},{6,7},{7,5},{5,3},{3,1},{1,0},{8,10},{10,12},{12... | collective-permute-start | bytes 1572872 | tf_op jit(solution)/shard_map/ppermute | solution.py:54
  457.1 22.3 %collective-permute-start.3 = (bf16[2,512,256]{2,1,0:T(8,128)(2,1)S(1)}, bf16[2,512,256]{2,1,0:T(8,128)(2,1)S(1)}, u32[]{:S(2)}, u32[]{:S(2)}) collective-permute-start(bf16[2,512,256]{2,1,0:T(8,128)(2,1)S(1)} %fusion.40), channel_id=1, source_target_pairs={{0,2},{2,4},{4,6},{6,7},{7,5},{5,3},{3,1},{1,0},{8,10},{10,12},{12... | collective-permute-start | bytes 1572872 | tf_op jit(solution)/shard_map/ppermute | solution.py:54
  458.8 22.3 %collective-permute-start.17 = (bf16[2,512,256]{2,1,0:T(8,128)(2,1)S(1)}, bf16[2,512,256]{2,1,0:T(8,128)(2,1)S(1)}, u32[]{:S(2)}, u32[]{:S(2)}) collective-permute-start(bf16[2,512,256]{2,1,0:T(8,128)(2,1)S(1)} %fusion.33), channel_id=1, source_target_pairs={{2,0},{4,2},{6,4},{7,6},{5,7},{3,5},{1,3},{0,1},{10,8},{12,10},{14... | collective-permute-start | bytes 1572872 | tf_op jit(solution)/shard_map/ppermute | solution.py:54
  470.0 22.4 %collective-permute-start.45 = (bf16[2,512,256]{2,1,0:T(8,128)(2,1)S(1)}, bf16[2,512,256]{2,1,0:T(8,128)(2,1)S(1)}, u32[]{:S(2)}, u32[]{:S(2)}) collective-permute-start(bf16[2,512,256]{2,1,0:T(8,128)(2,1)S(1)} %fusion.18), channel_id=1, source_target_pairs={{2,0},{4,2},{6,4},{7,6},{5,7},{3,5},{1,3},{0,1},{10,8},{12,10},{14... | collective-permute-start | bytes 1572872 | tf_op jit(solution)/shard_map/ppermute | solution.py:54
  470.7 22.3 %collective-permute-start.31 = (bf16[2,512,256]{2,1,0:T(8,128)(2,1)S(1)}, bf16[2,512,256]{2,1,0:T(8,128)(2,1)S(1)}, u32[]{:S(2)}, u32[]{:S(2)}) collective-permute-start(bf16[2,512,256]{2,1,0:T(8,128)(2,1)S(1)} %fusion.26), channel_id=1, source_target_pairs={{0,2},{2,4},{4,6},{6,7},{7,5},{5,3},{3,1},{1,0},{8,10},{10,12},{12... | collective-permute-start | bytes 1572872 | tf_op jit(solution)/shard_map/ppermute | solution.py:54
  479.6 22.3 %collective-permute-start.4 = (bf16[2,512,256]{2,1,0:T(8,128)(2,1)S(1)}, bf16[2,512,256]{2,1,0:T(8,128)(2,1)S(1)}, u32[]{:S(2)}, u32[]{:S(2)}) collective-permute-start(bf16[2,512,256]{2,1,0:T(8,128)(2,1)S(1)} %fusion.39), channel_id=1, source_target_pairs={{0,2},{2,4},{4,6},{6,7},{7,5},{5,3},{3,1},{1,0},{8,10},{10,12},{12... | collective-permute-start | bytes 1572872 | tf_op jit(solution)/shard_map/ppermute | solution.py:54
  481.3 22.3 %collective-permute-start.18 = (bf16[2,512,256]{2,1,0:T(8,128)(2,1)S(1)}, bf16[2,512,256]{2,1,0:T(8,128)(2,1)S(1)}, u32[]{:S(2)}, u32[]{:S(2)}) collective-permute-start(bf16[2,512,256]{2,1,0:T(8,128)(2,1)S(1)} %fusion.32), channel_id=1, source_target_pairs={{2,0},{4,2},{6,4},{7,6},{5,7},{3,5},{1,3},{0,1},{10,8},{12,10},{14... | collective-permute-start | bytes 1572872 | tf_op jit(solution)/shard_map/ppermute | solution.py:54
  492.4 22.4 %collective-permute-start.46 = (bf16[2,512,256]{2,1,0:T(8,128)(2,1)S(1)}, bf16[2,512,256]{2,1,0:T(8,128)(2,1)S(1)}, u32[]{:S(2)}, u32[]{:S(2)}) collective-permute-start(bf16[2,512,256]{2,1,0:T(8,128)(2,1)S(1)} %fusion.17), channel_id=1, source_target_pairs={{2,0},{4,2},{6,4},{7,6},{5,7},{3,5},{1,3},{0,1},{10,8},{12,10},{14... | collective-permute-start | bytes 1572872 | tf_op jit(solution)/shard_map/ppermute | solution.py:54
  493.2 22.3 %collective-permute-start.32 = (bf16[2,512,256]{2,1,0:T(8,128)(2,1)S(1)}, bf16[2,512,256]{2,1,0:T(8,128)(2,1)S(1)}, u32[]{:S(2)}, u32[]{:S(2)}) collective-permute-start(bf16[2,512,256]{2,1,0:T(8,128)(2,1)S(1)} %fusion.25), channel_id=1, source_target_pairs={{0,2},{2,4},{4,6},{6,7},{7,5},{5,3},{3,1},{1,0},{8,10},{10,12},{12... | collective-permute-start | bytes 1572872 | tf_op jit(solution)/shard_map/ppermute | solution.py:54
  502.1 22.3 %collective-permute-start.5 = (bf16[2,512,256]{2,1,0:T(8,128)(2,1)S(1)}, bf16[2,512,256]{2,1,0:T(8,128)(2,1)S(1)}, u32[]{:S(2)}, u32[]{:S(2)}) collective-permute-start(bf16[2,512,256]{2,1,0:T(8,128)(2,1)S(1)} %fusion.38), channel_id=1, source_target_pairs={{0,2},{2,4},{4,6},{6,7},{7,5},{5,3},{3,1},{1,0},{8,10},{10,12},{12... | collective-permute-start | bytes 1572872 | tf_op jit(solution)/shard_map/ppermute | solution.py:54
  503.8 22.3 %collective-permute-start.19 = (bf16[2,512,256]{2,1,0:T(8,128)(2,1)S(1)}, bf16[2,512,256]{2,1,0:T(8,128)(2,1)S(1)}, u32[]{:S(2)}, u32[]{:S(2)}) collective-permute-start(bf16[2,512,256]{2,1,0:T(8,128)(2,1)S(1)} %fusion.31), channel_id=1, source_target_pairs={{2,0},{4,2},{6,4},{7,6},{5,7},{3,5},{1,3},{0,1},{10,8},{12,10},{14... | collective-permute-start | bytes 1572872 | tf_op jit(solution)/shard_map/ppermute | solution.py:54
  514.9 22.4 %collective-permute-start.47 = (bf16[2,512,256]{2,1,0:T(8,128)(2,1)S(1)}, bf16[2,512,256]{2,1,0:T(8,128)(2,1)S(1)}, u32[]{:S(2)}, u32[]{:S(2)}) collective-permute-start(bf16[2,512,256]{2,1,0:T(8,128)(2,1)S(1)} %fusion.16), channel_id=1, source_target_pairs={{2,0},{4,2},{6,4},{7,6},{5,7},{3,5},{1,3},{0,1},{10,8},{12,10},{14... | collective-permute-start | bytes 1572872 | tf_op jit(solution)/shard_map/ppermute | solution.py:54
  515.7 22.3 %collective-permute-start.33 = (bf16[2,512,256]{2,1,0:T(8,128)(2,1)S(1)}, bf16[2,512,256]{2,1,0:T(8,128)(2,1)S(1)}, u32[]{:S(2)}, u32[]{:S(2)}) collective-permute-start(bf16[2,512,256]{2,1,0:T(8,128)(2,1)S(1)} %fusion.24), channel_id=1, source_target_pairs={{0,2},{2,4},{4,6},{6,7},{7,5},{5,3},{3,1},{1,0},{8,10},{10,12},{12... | collective-permute-start | bytes 1572872 | tf_op jit(solution)/shard_map/ppermute | solution.py:54
  524.5 22.3 %collective-permute-start.6 = (bf16[2,512,256]{2,1,0:T(8,128)(2,1)S(1)}, bf16[2,512,256]{2,1,0:T(8,128)(2,1)S(1)}, u32[]{:S(2)}, u32[]{:S(2)}) collective-permute-start(bf16[2,512,256]{2,1,0:T(8,128)(2,1)S(1)} %fusion.37), channel_id=1, source_target_pairs={{0,2},{2,4},{4,6},{6,7},{7,5},{5,3},{3,1},{1,0},{8,10},{10,12},{12... | collective-permute-start | bytes 1572872 | tf_op jit(solution)/shard_map/ppermute | solution.py:54
  526.2 22.3 %collective-permute-start.20 = (bf16[2,512,256]{2,1,0:T(8,128)(2,1)S(1)}, bf16[2,512,256]{2,1,0:T(8,128)(2,1)S(1)}, u32[]{:S(2)}, u32[]{:S(2)}) collective-permute-start(bf16[2,512,256]{2,1,0:T(8,128)(2,1)S(1)} %fusion.30), channel_id=1, source_target_pairs={{2,0},{4,2},{6,4},{7,6},{5,7},{3,5},{1,3},{0,1},{10,8},{12,10},{14... | collective-permute-start | bytes 1572872 | tf_op jit(solution)/shard_map/ppermute | solution.py:54
  537.4 22.4 %collective-permute-start.48 = (bf16[2,512,256]{2,1,0:T(8,128)(2,1)S(1)}, bf16[2,512,256]{2,1,0:T(8,128)(2,1)S(1)}, u32[]{:S(2)}, u32[]{:S(2)}) collective-permute-start(bf16[2,512,256]{2,1,0:T(8,128)(2,1)S(1)} %fusion.15), channel_id=1, source_target_pairs={{2,0},{4,2},{6,4},{7,6},{5,7},{3,5},{1,3},{0,1},{10,8},{12,10},{14... | collective-permute-start | bytes 1572872 | tf_op jit(solution)/shard_map/ppermute | solution.py:54
  538.1 23.3 %collective-permute-start.34 = (bf16[2,512,256]{2,1,0:T(8,128)(2,1)S(1)}, bf16[2,512,256]{2,1,0:T(8,128)(2,1)S(1)}, u32[]{:S(2)}, u32[]{:S(2)}) collective-permute-start(bf16[2,512,256]{2,1,0:T(8,128)(2,1)S(1)} %fusion.23), channel_id=1, source_target_pairs={{0,2},{2,4},{4,6},{6,7},{7,5},{5,3},{3,1},{1,0},{8,10},{10,12},{12... | collective-permute-start | bytes 1572872 | tf_op jit(solution)/shard_map/ppermute | solution.py:54
  547.0 22.3 %collective-permute-start.7 = (bf16[2,512,256]{2,1,0:T(8,128)(2,1)S(1)}, bf16[2,512,256]{2,1,0:T(8,128)(2,1)S(1)}, u32[]{:S(2)}, u32[]{:S(2)}) collective-permute-start(bf16[2,512,256]{2,1,0:T(8,128)(2,1)S(1)} %broadcast_select_fusion.27), channel_id=1, source_target_pairs={{0,2},{2,4},{4,6},{6,7},{7,5},{5,3},{3,1},{1,0},{8,10},{10,12},{12... | collective-permute-start | bytes 1572872 | tf_op jit(solution)/shard_map/ppermute | solution.py:54
  549.7 22.3 %collective-permute-start.21 = (bf16[2,512,256]{2,1,0:T(8,128)(2,1)S(1)}, bf16[2,512,256]{2,1,0:T(8,128)(2,1)S(1)}, u32[]{:S(2)}, u32[]{:S(2)}) collective-permute-start(bf16[2,512,256]{2,1,0:T(8,128)(2,1)S(1)} %broadcast_select_fusion.20), channel_id=1, source_target_pairs={{2,0},{4,2},{6,4},{7,6},{5,7},{3,5},{1,3},{0,1},{10,8},{12,10},{14... | collective-permute-start | bytes 1572872 | tf_op jit(solution)/shard_map/ppermute | solution.py:54
  685.6 24.1 %collective-permute-start.27 = (bf16[2,512,256]{2,1,0:T(8,128)(2,1)S(1)}, bf16[2,512,256]{2,1,0:T(8,128)(2,1)S(1)}, u32[]{:S(2)}, u32[]{:S(2)}) collective-permute-start(bf16[2,512,256]{2,1,0:T(8,128)(2,1)S(1)} %broadcast_select_fusion.14), channel_id=1, source_target_pairs={{2,0},{4,2},{6,4},{7,6},{5,7},{3,5},{1,3},{0,1},{10,8},{12,10},{14... | collective-permute-start | bytes 1572872 | tf_op jit(solution)/shard_map/ppermute | solution.py:54
  695.7 30.2 %collective-permute-start.55 = (bf16[2,512,256]{2,1,0:T(8,128)(2,1)S(1)}, bf16[2,512,256]{2,1,0:T(8,128)(2,1)S(1)}, u32[]{:S(2)}, u32[]{:S(2)}) collective-permute-start(bf16[2,512,256]{2,1,0:T(8,128)(2,1)S(1)} %broadcast_select_fusion), channel_id=1, source_target_pairs={{2,0},{4,2},{6,4},{7,6},{5,7},{3,5},{1,3},{0,1},{10,8},{12,10},{14... | collective-permute-start | bytes 1572872 | tf_op jit(solution)/shard_map/ppermute | solution.py:54
  (40 other events, 1163.8 us)
Sparse Core Ops, SparseCore 0:
  136.2 104.9 all-gather.4
  255.9 104.7 all-gather.2

commit v9 on v8

--- a/solution.py
+++ b/solution.py
@@ -47,10 +47,10 @@
         held = [jnp.zeros_like(piece[:, 0]) for piece in own]
         arrived = [[] for _ in values]
         for step in range(steps):
-            send = [
-                jnp.where(distance[p] == 0, own[p][:, min(step, chunks - 1)], held[p])
-                for p in range(len(values))
-            ]
+            if step < chunks:
+                send = [jnp.where(distance[p] == 0, own[p][:, step], held[p]) for p in range(len(values))]
+            else:
+                send = held
             held = lax.ppermute(send, "row", pairs)
             for p in range(len(values)):
                 arrived[p].append(held[p])

time: 796 us -> 795 us (level)
  waiting for transfers between devices: 245 us -> 257 us
    ppermute x56, waiting for transfers between devices: 185 us -> 197 us  [broadcast(): held = lax.ppermute(send, 'row', pairs)]
    select_n x56 -> x32, other arithmetic: 35.4 us -> 28.4 us  [broadcast(): jnp.where(distance[p] == 0, own[p][:, step], held[p])]
    unnamed x82 -> x78, local copies, waits for them, and re-layouts: 52.3 us -> 47 us
  transfers between devices with their start and end apart: 58 -> 58, of which waited for: 29 -> 35; matrix products, arithmetic and copies ran while one was open for 13% -> 12% of each run, Pallas kernels for 4% -> 4%
where the time goes in v9:
time: 795 us; the launch traced here: 791 us
  waiting for transfers between devices  257 us (32%)
  blocking collectives  198 us (25%)
  local copies, waits for them, and re-layouts  94.9 us (12%)
  Pallas kernels  60.2 us (8%)
  starting transfers between devices  58.7 us (7%)
  other arithmetic  50.5 us (6%)
  matrix products  45.9 us (6%)
  between operations  26.4 us (3%)
    all_to_all x2, blocking collectives, body(): lax.all_to_all(chunk, 'row', split_axis=2, concat_axis=1, tiled=True)  198 us
    ppermute x56, waiting for transfers between devices, broadcast(): held = lax.ppermute(send, 'row', pairs)  197 us
    all_gather x2, waiting for transfers between devices, body(): halves.append(lax.all_gather(by_row, 'freq', axis=1, tiled=True))  60.4 us
    pallas_call x2, Pallas kernels, make_spectrum(): pl.pallas_call(spectrum_kernel, grid=(groups,), in_specs=in_specs, out_sp...  60.2 us
    ppermute x56, starting transfers between devices, broadcast(): held = lax.ppermute(send, 'row', pairs)  58.6 us
    unnamed x78, local copies, waits for them, and re-layouts  47 us
    dot_general x1, matrix products, body(): lax.dot_general(left_pair, jnp.concatenate(shared, axis=1), dims, preferr...  45.9 us
    select_n x32, other arithmetic, broadcast(): jnp.where(distance[p] == 0, own[p][:, step], held[p])  28.4 us
  transfers between devices with their start and end apart: 58, of which 35 were waited for; matrix products, arithmetic and copies ran while one was open for 12% of the time, Pallas kernels for 4%

profile of v9, /device:TPU:0, one launch (start us, length us, event | category | flops | bytes accessed | tf_op | source)
XLA Modules:
  0.0 791.1 jit_solution(2250424624518512763)
XLA Ops:
  7.2 6.0 fusion.55
  13.2 11.2 %copy.232 = bf16[2,128,8192]{1,0,2:T(2,128)(2,1)} copy(bf16[2,128,8192]{2,1,0:T(8,128)(2,1)} %get-tuple-element.18) | data formatting | bytes 8388608
  24.4 100.5 %all_to_all.36 = bf16[2,128,8192]{1,0,2:T(2,128)(2,1)} all-to-all(bf16[2,128,8192]{1,0,2:T(2,128)(2,1)} %copy.232), channel_id=1, replica_groups=mesh['freq'=4,'row'=8] {'row'}, dimensions={2} | all-to-all | bytes 8388608 | tf_op jit(solution)/shard_map/all_to_all | solution.py:123
  124.9 11.1 %copy.177 = bf16[2,128,8,1024]{3,1,2,0:T(8,128)(2,1)} copy(bf16[2,128,8,1024]{1,0,3,2:T(2,128)(2,1)} %bitcast.375) | data formatting | bytes 8388608 | tf_op jit(solution)/shard_map/all_to_all | solution.py:123
  136.1 11.4 %copy.231 = bf16[2,128,8192]{1,0,2:T(2,128)(2,1)} copy(bf16[2,128,8192]{2,1,0:T(8,128)(2,1)} %get-tuple-element.19) | data formatting | bytes 8388608
  147.6 97.0 %all_to_all.37 = bf16[2,128,8192]{1,0,2:T(2,128)(2,1)} all-to-all(bf16[2,128,8192]{1,0,2:T(2,128)(2,1)} %copy.231), channel_id=1, replica_groups=mesh['freq'=4,'row'=8] {'row'}, dimensions={2} | all-to-all | bytes 8388608 | tf_op jit(solution)/shard_map/all_to_all | solution.py:123
  244.6 11.2 %copy.175 = bf16[2,128,8,1024]{3,1,2,0:T(8,128)(2,1)} copy(bf16[2,128,8,1024]{1,0,3,2:T(2,128)(2,1)} %bitcast.376) | data formatting | bytes 8388608 | tf_op jit(solution)/shard_map/all_to_all | solution.py:123
  270.0 30.3 %shard_map.68.rest_0_ = bf16[2,8192,1024]{2,1,0:T(8,128)(2,1)} custom-call(f32[4]{0:T(128)} %reshape.183.weight_ref, bf16[2,4096,1024]{2,1,0:T(8,128)(2,1)} %all-gather.5.cloned.1.call-done.source_ref, bf16[2,8192,1024]{2,1,0:T(8,128)(2,1)} %bitcast.335), custom_call_target="tpu_custom_call" | custom-call | flops 67108864 | bytes 50331648 | tf_op jit(solution)/shard_map/pallas_call | solution.py:93
  300.3 60.4 %all-gather.3.cloned.1.call-done.source_ref = bf16[2,4096,1024]{2,1,0:T(8,128)(2,1)} async-done(((bf16[2,1024,1024]{2,1,0:T(8,128)(2,1)}), bf16[2,4096,1024]{2,1,0:T(8,128)(2,1)}) %all-gather.3.cloned.1.call-update) | async-done | bytes 16777232 | tf_op jit(solution)/shard_map/all_gather | solution.py:124
  360.6 29.9 %shard_map.69 = bf16[2,8192,1024]{2,1,0:T(8,128)(2,1)} custom-call(f32[4]{0:T(128)} %reshape.183.weight_ref, bf16[2,4096,1024]{2,1,0:T(8,128)(2,1)} %all-gather.3.cloned.1.call-done.source_ref, bf16[2,8192,1024]{2,1,0:T(8,128)(2,1)} %bitcast.336, bf16[2,8192,1024]{2,1,0:T(8,128)(2,1)} %shard_map.68.rest_0_), custom_call_target="tpu_custom_call", output_to_operand_aliasing={{}: (3, {})} | custom-call | flops 67108864 | bytes 50331648 | tf_op jit(solution)/shard_map/pallas_call | solution.py:93
  390.6 6.5 constant_dynamic-slice_fusion
  414.5 10.5 %collective-permute-done.42 = bf16[2,512,256]{2,1,0:T(8,128)(2,1)S(1)} collective-permute-done((bf16[2,512,256]{2,1,0:T(8,128)(2,1)S(1)}, bf16[2,512,256]{2,1,0:T(8,128)(2,1)S(1)}, u32[]{:S(2)}, u32[]{:S(2)}) %collective-permute-start.42) | collective-permute-done | bytes 524320 | tf_op jit(solution)/shard_map/ppermute | solution.py:54
  439.0 8.4 %collective-permute-done.43 = bf16[2,512,256]{2,1,0:T(8,128)(2,1)S(1)} collective-permute-done((bf16[2,512,256]{2,1,0:T(8,128)(2,1)S(1)}, bf16[2,512,256]{2,1,0:T(8,128)(2,1)S(1)}, u32[]{:S(2)}, u32[]{:S(2)}) %collective-permute-start.43) | collective-permute-done | bytes 524320 | tf_op jit(solution)/shard_map/ppermute | solution.py:54
  461.5 8.4 %collective-permute-done.44 = bf16[2,512,256]{2,1,0:T(8,128)(2,1)S(1)} collective-permute-done((bf16[2,512,256]{2,1,0:T(8,128)(2,1)S(1)}, bf16[2,512,256]{2,1,0:T(8,128)(2,1)S(1)}, u32[]{:S(2)}, u32[]{:S(2)}) %collective-permute-start.44) | collective-permute-done | bytes 524320 | tf_op jit(solution)/shard_map/ppermute | solution.py:54
  483.9 8.4 %collective-permute-done.45 = bf16[2,512,256]{2,1,0:T(8,128)(2,1)S(1)} collective-permute-done((bf16[2,512,256]{2,1,0:T(8,128)(2,1)S(1)}, bf16[2,512,256]{2,1,0:T(8,128)(2,1)S(1)}, u32[]{:S(2)}, u32[]{:S(2)}) %collective-permute-start.45) | collective-permute-done | bytes 524320 | tf_op jit(solution)/shard_map/ppermute | solution.py:54
  506.4 8.4 %collective-permute-done.46 = bf16[2,512,256]{2,1,0:T(8,128)(2,1)S(1)} collective-permute-done((bf16[2,512,256]{2,1,0:T(8,128)(2,1)S(1)}, bf16[2,512,256]{2,1,0:T(8,128)(2,1)S(1)}, u32[]{:S(2)}, u32[]{:S(2)}) %collective-permute-start.46) | collective-permute-done | bytes 524320 | tf_op jit(solution)/shard_map/ppermute | solution.py:54
  528.9 8.4 %collective-permute-done.47 = bf16[2,512,256]{2,1,0:T(8,128)(2,1)S(1)} collective-permute-done((bf16[2,512,256]{2,1,0:T(8,128)(2,1)S(1)}, bf16[2,512,256]{2,1,0:T(8,128)(2,1)S(1)}, u32[]{:S(2)}, u32[]{:S(2)}) %collective-permute-start.47) | collective-permute-done | bytes 524320 | tf_op jit(solution)/shard_map/ppermute | solution.py:54
  551.4 8.4 %collective-permute-done.48 = bf16[2,512,256]{2,1,0:T(8,128)(2,1)S(1)} collective-permute-done((bf16[2,512,256]{2,1,0:T(8,128)(2,1)S(1)}, bf16[2,512,256]{2,1,0:T(8,128)(2,1)S(1)}, u32[]{:S(2)}, u32[]{:S(2)}) %collective-permute-start.48) | collective-permute-done | bytes 524320 | tf_op jit(solution)/shard_map/ppermute | solution.py:54
  572.5 9.8 %collective-permute-done.49 = bf16[2,512,256]{2,1,0:T(8,128)(2,1)S(1)} collective-permute-done((bf16[2,512,256]{2,1,0:T(8,128)(2,1)S(1)}, bf16[2,512,256]{2,1,0:T(8,128)(2,1)S(1)}, u32[]{:S(2)}, u32[]{:S(2)}) %collective-permute-start.49) | collective-permute-done | bytes 524320 | tf_op jit(solution)/shard_map/ppermute | solution.py:54
  585.2 6.7 collective-permute-done.8
  595.0 9.8 %collective-permute-done.50 = bf16[2,512,256]{2,1,0:T(8,128)(2,1)S(1)} collective-permute-done((bf16[2,512,256]{2,1,0:T(8,128)(2,1)S(1)}, bf16[2,512,256]{2,1,0:T(8,128)(2,1)S(1)}, u32[]{:S(2)}, u32[]{:S(2)}) %collective-permute-start.50) | collective-permute-done | bytes 524320 | tf_op jit(solution)/shard_map/ppermute | solution.py:54
  607.6 6.7 collective-permute-done.9
  617.4 9.8 %collective-permute-done.51 = bf16[2,512,256]{2,1,0:T(8,128)(2,1)S(1)} collective-permute-done((bf16[2,512,256]{2,1,0:T(8,128)(2,1)S(1)}, bf16[2,512,256]{2,1,0:T(8,128)(2,1)S(1)}, u32[]{:S(2)}, u32[]{:S(2)}) %collective-permute-start.51) | collective-permute-done | bytes 524320 | tf_op jit(solution)/shard_map/ppermute | solution.py:54
  630.1 6.6 collective-permute-done.10
  639.9 9.8 %collective-permute-done.52 = bf16[2,512,256]{2,1,0:T(8,128)(2,1)S(1)} collective-permute-done((bf16[2,512,256]{2,1,0:T(8,128)(2,1)S(1)}, bf16[2,512,256]{2,1,0:T(8,128)(2,1)S(1)}, u32[]{:S(2)}, u32[]{:S(2)}) %collective-permute-start.52) | collective-permute-done | bytes 524320 | tf_op jit(solution)/shard_map/ppermute | solution.py:54
  652.6 6.7 collective-permute-done.11
  662.3 9.8 %collective-permute-done.53 = bf16[2,512,256]{2,1,0:T(8,128)(2,1)S(1)} collective-permute-done((bf16[2,512,256]{2,1,0:T(8,128)(2,1)S(1)}, bf16[2,512,256]{2,1,0:T(8,128)(2,1)S(1)}, u32[]{:S(2)}, u32[]{:S(2)}) %collective-permute-start.53) | collective-permute-done | bytes 524320 | tf_op jit(solution)/shard_map/ppermute | solution.py:54
  675.1 6.7 collective-permute-done.12
  684.8 9.8 %collective-permute-done.54 = bf16[2,512,256]{2,1,0:T(8,128)(2,1)S(1)} collective-permute-done((bf16[2,512,256]{2,1,0:T(8,128)(2,1)S(1)}, bf16[2,512,256]{2,1,0:T(8,128)(2,1)S(1)}, u32[]{:S(2)}, u32[]{:S(2)}) %collective-permute-start.54) | collective-permute-done | bytes 524320 | tf_op jit(solution)/shard_map/ppermute | solution.py:54
  697.6 6.6 collective-permute-done.13
  729.7 8.7 %fusion.7 = (bf16[8192,256]{1,0:T(8,128)(2,1)}, bf16[8192,256]{1,0:T(8,128)(2,1)}, bf16[8192,256]{1,0:T(8,128)(2,1)}, bf16[8192,256]{1,0:T(8,128)(2,1)}) fusion(bf16[2,4096,256]{2,1,0:T(8,128)(2,1)} %bitcast.380, bf16[2,4096,256]{2,1,0:T(8,128)(2,1)S(1)} %bitcast.377, bf16[2,4096,256]{2,1,0:T(8,128)(2,1)} %bitcast.379, bf16[2,4096,256]{2,1,0:T(8,128)(2,1)S(1)} %bitcast.378), kind=kLoop, calls=%fused_computation.13 | loop fusion | flops 33554432 | bytes 33554432 | tf_op jit(solution)/shard_map/squeeze | solution.py:143
  738.3 45.9 %convert_bitcast_fusion = bf16[1,2,1024,8192]{3,2,1,0:T(8,128)(2,1)} fusion(bf16[8192,256]{1,0:T(8,128)(2,1)} %get-tuple-element.17, bf16[8192,256]{1,0:T(8,128)(2,1)} %get-tuple-element.16, bf16[8192,256]{1,0:T(8,128)(2,1)} %get-tuple-element.29, bf16[8192,256]{1,0:T(8,128)(2,1)} %get-tuple-element.30, bf16[1,1024,1024]{2,1,0:T(8,128)(2,1)} %get-tuple-element.21, ...), kind=kOutput, calls=%fused_computation | convolution fusion | flops 34445721600 | bytes 54525952 | tf_op jit(solution)/shard_map/dot_general | solution.py:146
  (226 shorter events, 174.7 us)
Async XLA Ops:
  7.2 262.8 %all-gather.5.cloned.1.call-start = ((), (), s32[]{:S(2)}) async-start(), calls=%async_computation.3 | async-start | bytes 20971520 | tf_op jit(solution)/shard_map/all_gather | solution.py:124
  136.1 224.5 %all-gather.3.cloned.1.call-start = ((), (), s32[]{:S(2)}) async-start(), calls=%async_computation.2 | async-start | bytes 20971520 | tf_op jit(solution)/shard_map/all_gather | solution.py:124
  399.5 25.4 %collective-permute-start.42 = (bf16[2,512,256]{2,1,0:T(8,128)(2,1)S(1)}, bf16[2,512,256]{2,1,0:T(8,128)(2,1)S(1)}, u32[]{:S(2)}, u32[]{:S(2)}) collective-permute-start(bf16[2,512,256]{2,1,0:T(8,128)(2,1)S(1)} %fusion.23), channel_id=1, source_target_pairs={{2,0},{4,2},{6,4},{7,6},{5,7},{3,5},{1,3},{0,1},{10,8},{12,10},{14... | collective-permute-start | bytes 1572872 | tf_op jit(solution)/shard_map/ppermute | solution.py:54
  401.2 24.5 %collective-permute-start.28 = (bf16[2,512,256]{2,1,0:T(8,128)(2,1)S(1)}, bf16[2,512,256]{2,1,0:T(8,128)(2,1)S(1)}, u32[]{:S(2)}, u32[]{:S(2)}) collective-permute-start(bf16[2,512,256]{2,1,0:T(8,128)(2,1)S(1)} %fusion.31), channel_id=1, source_target_pairs={{0,2},{2,4},{4,6},{6,7},{7,5},{5,3},{3,1},{1,0},{8,10},{10,12},{12... | collective-permute-start | bytes 1572872 | tf_op jit(solution)/shard_map/ppermute | solution.py:54
  412.2 22.3 %collective-permute-start.1 = (bf16[2,512,256]{2,1,0:T(8,128)(2,1)S(1)}, bf16[2,512,256]{2,1,0:T(8,128)(2,1)S(1)}, u32[]{:S(2)}, u32[]{:S(2)}) collective-permute-start(bf16[2,512,256]{2,1,0:T(8,128)(2,1)S(1)} %fusion.46), channel_id=1, source_target_pairs={{0,2},{2,4},{4,6},{6,7},{7,5},{5,3},{3,1},{1,0},{8,10},{10,12},{12... | collective-permute-start | bytes 1572872 | tf_op jit(solution)/shard_map/ppermute | solution.py:54
  413.9 23.3 %collective-permute-start.15 = (bf16[2,512,256]{2,1,0:T(8,128)(2,1)S(1)}, bf16[2,512,256]{2,1,0:T(8,128)(2,1)S(1)}, u32[]{:S(2)}, u32[]{:S(2)}) collective-permute-start(bf16[2,512,256]{2,1,0:T(8,128)(2,1)S(1)} %fusion.38), channel_id=1, source_target_pairs={{2,0},{4,2},{6,4},{7,6},{5,7},{3,5},{1,3},{0,1},{10,8},{12,10},{14... | collective-permute-start | bytes 1572872 | tf_op jit(solution)/shard_map/ppermute | solution.py:54
  425.1 22.4 %collective-permute-start.43 = (bf16[2,512,256]{2,1,0:T(8,128)(2,1)S(1)}, bf16[2,512,256]{2,1,0:T(8,128)(2,1)S(1)}, u32[]{:S(2)}, u32[]{:S(2)}) collective-permute-start(bf16[2,512,256]{2,1,0:T(8,128)(2,1)S(1)} %fusion.21), channel_id=1, source_target_pairs={{2,0},{4,2},{6,4},{7,6},{5,7},{3,5},{1,3},{0,1},{10,8},{12,10},{14... | collective-permute-start | bytes 1572872 | tf_op jit(solution)/shard_map/ppermute | solution.py:54
  425.8 23.3 %collective-permute-start.29 = (bf16[2,512,256]{2,1,0:T(8,128)(2,1)S(1)}, bf16[2,512,256]{2,1,0:T(8,128)(2,1)S(1)}, u32[]{:S(2)}, u32[]{:S(2)}) collective-permute-start(bf16[2,512,256]{2,1,0:T(8,128)(2,1)S(1)} %fusion.30), channel_id=1, source_target_pairs={{0,2},{2,4},{4,6},{6,7},{7,5},{5,3},{3,1},{1,0},{8,10},{10,12},{12... | collective-permute-start | bytes 1572872 | tf_op jit(solution)/shard_map/ppermute | solution.py:54
  540.2 21.5 %collective-permute-start.34 = (bf16[2,512,256]{2,1,0:T(8,128)(2,1)S(1)}, bf16[2,512,256]{2,1,0:T(8,128)(2,1)S(1)}, u32[]{:S(2)}, u32[]{:S(2)}) collective-permute-start(bf16[2,512,256]{2,1,0:T(8,128)(2,1)S(1)} %fusion.25), channel_id=1, source_target_pairs={{0,2},{2,4},{4,6},{6,7},{7,5},{5,3},{3,1},{1,0},{8,10},{10,12},{12... | collective-permute-start | bytes 1572872 | tf_op jit(solution)/shard_map/ppermute | solution.py:54
  569.4 22.5 %collective-permute-start.8 = (bf16[2,512,256]{2,1,0:T(8,128)(2,1)S(1)}, bf16[2,512,256]{2,1,0:T(8,128)(2,1)S(1)}, u32[]{:S(2)}, u32[]{:S(2)}) collective-permute-start(bf16[2,512,256]{2,1,0:T(8,128)(2,1)S(1)} %collective-permute-done.7), channel_id=1, source_target_pairs={{0,2},{2,4},{4,6},{6,7},{7,5},{5,3},{3,1},{1,0},{8,10},{10,12},{12... | collective-permute-start | bytes 1572872 | tf_op jit(solution)/shard_map/ppermute | solution.py:54
  571.0 22.5 %collective-permute-start.22 = (bf16[2,512,256]{2,1,0:T(8,128)(2,1)S(1)}, bf16[2,512,256]{2,1,0:T(8,128)(2,1)S(1)}, u32[]{:S(2)}, u32[]{:S(2)}) collective-permute-start(bf16[2,512,256]{2,1,0:T(8,128)(2,1)S(1)} %collective-permute-done.21), channel_id=1, source_target_pairs={{2,0},{4,2},{6,4},{7,6},{5,7},{3,5},{1,3},{0,1},{10,8},{12,10},{14... | collective-permute-start | bytes 1572872 | tf_op jit(solution)/shard_map/ppermute | solution.py:54
  582.3 22.5 %collective-permute-start.50 = (bf16[2,512,256]{2,1,0:T(8,128)(2,1)S(1)}, bf16[2,512,256]{2,1,0:T(8,128)(2,1)S(1)}, u32[]{:S(2)}, u32[]{:S(2)}) collective-permute-start(bf16[2,512,256]{2,1,0:T(8,128)(2,1)S(1)} %collective-permute-done.49), channel_id=1, source_target_pairs={{2,0},{4,2},{6,4},{7,6},{5,7},{3,5},{1,3},{0,1},{10,8},{12,10},{14... | collective-permute-start | bytes 1572872 | tf_op jit(solution)/shard_map/ppermute | solution.py:54
  582.8 22.5 %collective-permute-start.36 = (bf16[2,512,256]{2,1,0:T(8,128)(2,1)S(1)}, bf16[2,512,256]{2,1,0:T(8,128)(2,1)S(1)}, u32[]{:S(2)}, u32[]{:S(2)}) collective-permute-start(bf16[2,512,256]{2,1,0:T(8,128)(2,1)S(1)} %collective-permute-done.35), channel_id=1, source_target_pairs={{0,2},{2,4},{4,6},{6,7},{7,5},{5,3},{3,1},{1,0},{8,10},{10,12},{12... | collective-permute-start | bytes 1572872 | tf_op jit(solution)/shard_map/ppermute | solution.py:54
  591.8 22.5 %collective-permute-start.9 = (bf16[2,512,256]{2,1,0:T(8,128)(2,1)S(1)}, bf16[2,512,256]{2,1,0:T(8,128)(2,1)S(1)}, u32[]{:S(2)}, u32[]{:S(2)}) collective-permute-start(bf16[2,512,256]{2,1,0:T(8,128)(2,1)S(1)} %collective-permute-done.8), channel_id=1, source_target_pairs={{0,2},{2,4},{4,6},{6,7},{7,5},{5,3},{3,1},{1,0},{8,10},{10,12},{12... | collective-permute-start | bytes 1572872 | tf_op jit(solution)/shard_map/ppermute | solution.py:54
  593.5 22.5 %collective-permute-start.23 = (bf16[2,512,256]{2,1,0:T(8,128)(2,1)S(1)}, bf16[2,512,256]{2,1,0:T(8,128)(2,1)S(1)}, u32[]{:S(2)}, u32[]{:S(2)}) collective-permute-start(bf16[2,512,256]{2,1,0:T(8,128)(2,1)S(1)} %collective-permute-done.22), channel_id=1, source_target_pairs={{2,0},{4,2},{6,4},{7,6},{5,7},{3,5},{1,3},{0,1},{10,8},{12,10},{14... | collective-permute-start | bytes 1572872 | tf_op jit(solution)/shard_map/ppermute | solution.py:54
  604.7 22.5 %collective-permute-start.51 = (bf16[2,512,256]{2,1,0:T(8,128)(2,1)S(1)}, bf16[2,512,256]{2,1,0:T(8,128)(2,1)S(1)}, u32[]{:S(2)}, u32[]{:S(2)}) collective-permute-start(bf16[2,512,256]{2,1,0:T(8,128)(2,1)S(1)} %collective-permute-done.50), channel_id=1, source_target_pairs={{2,0},{4,2},{6,4},{7,6},{5,7},{3,5},{1,3},{0,1},{10,8},{12,10},{14... | collective-permute-start | bytes 1572872 | tf_op jit(solution)/shard_map/ppermute | solution.py:54
  605.3 22.5 %collective-permute-start.37 = (bf16[2,512,256]{2,1,0:T(8,128)(2,1)S(1)}, bf16[2,512,256]{2,1,0:T(8,128)(2,1)S(1)}, u32[]{:S(2)}, u32[]{:S(2)}) collective-permute-start(bf16[2,512,256]{2,1,0:T(8,128)(2,1)S(1)} %collective-permute-done.36), channel_id=1, source_target_pairs={{0,2},{2,4},{4,6},{6,7},{7,5},{5,3},{3,1},{1,0},{8,10},{10,12},{12... | collective-permute-start | bytes 1572872 | tf_op jit(solution)/shard_map/ppermute | solution.py:54
  614.3 22.5 %collective-permute-start.10 = (bf16[2,512,256]{2,1,0:T(8,128)(2,1)S(1)}, bf16[2,512,256]{2,1,0:T(8,128)(2,1)S(1)}, u32[]{:S(2)}, u32[]{:S(2)}) collective-permute-start(bf16[2,512,256]{2,1,0:T(8,128)(2,1)S(1)} %collective-permute-done.9), channel_id=1, source_target_pairs={{0,2},{2,4},{4,6},{6,7},{7,5},{5,3},{3,1},{1,0},{8,10},{10,12},{12... | collective-permute-start | bytes 1572872 | tf_op jit(solution)/shard_map/ppermute | solution.py:54
  616.0 22.5 %collective-permute-start.24 = (bf16[2,512,256]{2,1,0:T(8,128)(2,1)S(1)}, bf16[2,512,256]{2,1,0:T(8,128)(2,1)S(1)}, u32[]{:S(2)}, u32[]{:S(2)}) collective-permute-start(bf16[2,512,256]{2,1,0:T(8,128)(2,1)S(1)} %collective-permute-done.23), channel_id=1, source_target_pairs={{2,0},{4,2},{6,4},{7,6},{5,7},{3,5},{1,3},{0,1},{10,8},{12,10},{14... | collective-permute-start | bytes 1572872 | tf_op jit(solution)/shard_map/ppermute | solution.py:54
  627.2 22.5 %collective-permute-start.52 = (bf16[2,512,256]{2,1,0:T(8,128)(2,1)S(1)}, bf16[2,512,256]{2,1,0:T(8,128)(2,1)S(1)}, u32[]{:S(2)}, u32[]{:S(2)}) collective-permute-start(bf16[2,512,256]{2,1,0:T(8,128)(2,1)S(1)} %collective-permute-done.51), channel_id=1, source_target_pairs={{2,0},{4,2},{6,4},{7,6},{5,7},{3,5},{1,3},{0,1},{10,8},{12,10},{14... | collective-permute-start | bytes 1572872 | tf_op jit(solution)/shard_map/ppermute | solution.py:54
  627.8 22.5 %collective-permute-start.38 = (bf16[2,512,256]{2,1,0:T(8,128)(2,1)S(1)}, bf16[2,512,256]{2,1,0:T(8,128)(2,1)S(1)}, u32[]{:S(2)}, u32[]{:S(2)}) collective-permute-start(bf16[2,512,256]{2,1,0:T(8,128)(2,1)S(1)} %collective-permute-done.37), channel_id=1, source_target_pairs={{0,2},{2,4},{4,6},{6,7},{7,5},{5,3},{3,1},{1,0},{8,10},{10,12},{12... | collective-permute-start | bytes 1572872 | tf_op jit(solution)/shard_map/ppermute | solution.py:54
  636.8 22.5 %collective-permute-start.11 = (bf16[2,512,256]{2,1,0:T(8,128)(2,1)S(1)}, bf16[2,512,256]{2,1,0:T(8,128)(2,1)S(1)}, u32[]{:S(2)}, u32[]{:S(2)}) collective-permute-start(bf16[2,512,256]{2,1,0:T(8,128)(2,1)S(1)} %collective-permute-done.10), channel_id=1, source_target_pairs={{0,2},{2,4},{4,6},{6,7},{7,5},{5,3},{3,1},{1,0},{8,10},{10,12},{12... | collective-permute-start | bytes 1572872 | tf_op jit(solution)/shard_map/ppermute | solution.py:54
  638.5 22.5 %collective-permute-start.25 = (bf16[2,512,256]{2,1,0:T(8,128)(2,1)S(1)}, bf16[2,512,256]{2,1,0:T(8,128)(2,1)S(1)}, u32[]{:S(2)}, u32[]{:S(2)}) collective-permute-start(bf16[2,512,256]{2,1,0:T(8,128)(2,1)S(1)} %collective-permute-done.24), channel_id=1, source_target_pairs={{2,0},{4,2},{6,4},{7,6},{5,7},{3,5},{1,3},{0,1},{10,8},{12,10},{14... | collective-permute-start | bytes 1572872 | tf_op jit(solution)/shard_map/ppermute | solution.py:54
  649.7 22.5 %collective-permute-start.53 = (bf16[2,512,256]{2,1,0:T(8,128)(2,1)S(1)}, bf16[2,512,256]{2,1,0:T(8,128)(2,1)S(1)}, u32[]{:S(2)}, u32[]{:S(2)}) collective-permute-start(bf16[2,512,256]{2,1,0:T(8,128)(2,1)S(1)} %collective-permute-done.52), channel_id=1, source_target_pairs={{2,0},{4,2},{6,4},{7,6},{5,7},{3,5},{1,3},{0,1},{10,8},{12,10},{14... | collective-permute-start | bytes 1572872 | tf_op jit(solution)/shard_map/ppermute | solution.py:54
  650.2 22.5 %collective-permute-start.39 = (bf16[2,512,256]{2,1,0:T(8,128)(2,1)S(1)}, bf16[2,512,256]{2,1,0:T(8,128)(2,1)S(1)}, u32[]{:S(2)}, u32[]{:S(2)}) collective-permute-start(bf16[2,512,256]{2,1,0:T(8,128)(2,1)S(1)} %collective-permute-done.38), channel_id=1, source_target_pairs={{0,2},{2,4},{4,6},{6,7},{7,5},{5,3},{3,1},{1,0},{8,10},{10,12},{12... | collective-permute-start | bytes 1572872 | tf_op jit(solution)/shard_map/ppermute | solution.py:54
  659.2 22.5 %collective-permute-start.12 = (bf16[2,512,256]{2,1,0:T(8,128)(2,1)S(1)}, bf16[2,512,256]{2,1,0:T(8,128)(2,1)S(1)}, u32[]{:S(2)}, u32[]{:S(2)}) collective-permute-start(bf16[2,512,256]{2,1,0:T(8,128)(2,1)S(1)} %collective-permute-done.11), channel_id=1, source_target_pairs={{0,2},{2,4},{4,6},{6,7},{7,5},{5,3},{3,1},{1,0},{8,10},{10,12},{12... | collective-permute-start | bytes 1572872 | tf_op jit(solution)/shard_map/ppermute | solution.py:54
  660.9 22.5 %collective-permute-start.26 = (bf16[2,512,256]{2,1,0:T(8,128)(2,1)S(1)}, bf16[2,512,256]{2,1,0:T(8,128)(2,1)S(1)}, u32[]{:S(2)}, u32[]{:S(2)}) collective-permute-start(bf16[2,512,256]{2,1,0:T(8,128)(2,1)S(1)} %collective-permute-done.25), channel_id=1, source_target_pairs={{2,0},{4,2},{6,4},{7,6},{5,7},{3,5},{1,3},{0,1},{10,8},{12,10},{14... | collective-permute-start | bytes 1572872 | tf_op jit(solution)/shard_map/ppermute | solution.py:54
  672.2 22.5 %collective-permute-start.54 = (bf16[2,512,256]{2,1,0:T(8,128)(2,1)S(1)}, bf16[2,512,256]{2,1,0:T(8,128)(2,1)S(1)}, u32[]{:S(2)}, u32[]{:S(2)}) collective-permute-start(bf16[2,512,256]{2,1,0:T(8,128)(2,1)S(1)} %collective-permute-done.53), channel_id=1, source_target_pairs={{2,0},{4,2},{6,4},{7,6},{5,7},{3,5},{1,3},{0,1},{10,8},{12,10},{14... | collective-permute-start | bytes 1572872 | tf_op jit(solution)/shard_map/ppermute | solution.py:54
  672.7 22.5 %collective-permute-start.40 = (bf16[2,512,256]{2,1,0:T(8,128)(2,1)S(1)}, bf16[2,512,256]{2,1,0:T(8,128)(2,1)S(1)}, u32[]{:S(2)}, u32[]{:S(2)}) collective-permute-start(bf16[2,512,256]{2,1,0:T(8,128)(2,1)S(1)} %collective-permute-done.39), channel_id=1, source_target_pairs={{0,2},{2,4},{4,6},{6,7},{7,5},{5,3},{3,1},{1,0},{8,10},{10,12},{12... | collective-permute-start | bytes 1572872 | tf_op jit(solution)/shard_map/ppermute | solution.py:54
  681.7 22.5 %collective-permute-start.13 = (bf16[2,512,256]{2,1,0:T(8,128)(2,1)S(1)}, bf16[2,512,256]{2,1,0:T(8,128)(2,1)S(1)}, u32[]{:S(2)}, u32[]{:S(2)}) collective-permute-start(bf16[2,512,256]{2,1,0:T(8,128)(2,1)S(1)} %collective-permute-done.12), channel_id=1, source_target_pairs={{0,2},{2,4},{4,6},{6,7},{7,5},{5,3},{3,1},{1,0},{8,10},{10,12},{12... | collective-permute-start | bytes 1572872 | tf_op jit(solution)/shard_map/ppermute | solution.py:54
  683.4 24.4 %collective-permute-start.27 = (bf16[2,512,256]{2,1,0:T(8,128)(2,1)S(1)}, bf16[2,512,256]{2,1,0:T(8,128)(2,1)}, u32[]{:S(2)}, u32[]{:S(2)}) collective-permute-start(bf16[2,512,256]{2,1,0:T(8,128)(2,1)S(1)} %collective-permute-done.26), channel_id=1, source_target_pairs={{2,0},{4,2},{6,4},{7,6},{5,7},{3,5},{1,3},{0,1},{10,8},{12,10},{14... | collective-permute-start | bytes 1572872 | tf_op jit(solution)/shard_map/ppermute | solution.py:54
  694.6 31.0 %collective-permute-start.55 = (bf16[2,512,256]{2,1,0:T(8,128)(2,1)S(1)}, bf16[2,512,256]{2,1,0:T(8,128)(2,1)S(1)}, u32[]{:S(2)}, u32[]{:S(2)}) collective-permute-start(bf16[2,512,256]{2,1,0:T(8,128)(2,1)S(1)} %collective-permute-done.54), channel_id=1, source_target_pairs={{2,0},{4,2},{6,4},{7,6},{5,7},{3,5},{1,3},{0,1},{10,8},{12,10},{14... | collective-permute-start | bytes 1572872 | tf_op jit(solution)/shard_map/ppermute | solution.py:54
  (38 other events, 780.3 us)
Sparse Core Ops, SparseCore 0:
  136.2 104.9 all-gather.4
  255.9 104.7 all-gather.2

commit v10 on v9

--- a/solution.py
+++ b/solution.py
@@ -12,7 +12,7 @@
 STEPS = 2
 BLOCK_START = 1022
 PIECES = 2
-RING_CHUNKS = 8
+RING_CHUNKS = 16
 
 
 def ring_order(count):

time: 795 us -> 727 us (0.914)
  waiting for transfers between devices: 257 us -> 148 us
  starting transfers between devices: 58.7 us -> 93.3 us
  other arithmetic: 50.5 us -> 76.9 us
  local copies, waits for them, and re-layouts: 94.9 us -> 73.3 us
    ppermute x56 -> x88, waiting for transfers between devices: 197 us -> 87.9 us  [broadcast(): held = lax.ppermute(send, 'row', pairs)]
    ppermute x56 -> x88, starting transfers between devices: 58.6 us -> 93.3 us  [broadcast(): held = lax.ppermute(send, 'row', pairs)]
    select_n x32 -> x64, other arithmetic: 28.4 us -> 57.6 us  [broadcast(): jnp.where(distance[p] == 0, own[p][:, step], held[p])]
    unnamed x78 -> x112, local copies, waits for them, and re-layouts: 47 us -> 26.8 us
  transfers between devices with their start and end apart: 58 -> 90, of which waited for: 35 -> 30; matrix products, arithmetic and copies ran while one was open for 12% -> 14% of each run, Pallas kernels for 4% -> 4%
where the time goes in v10:
time: 727 us; the launch traced here: 722 us
  blocking collectives  198 us (27%)
  waiting for transfers between devices  148 us (20%)
  starting transfers between devices  93.3 us (13%)
  other arithmetic  76.9 us (11%)
  local copies, waits for them, and re-layouts  73.3 us (10%)
  Pallas kernels  60.1 us (8%)
  matrix products  45.9 us (6%)
  between operations  26.6 us (4%)
    all_to_all x2, blocking collectives, body(): lax.all_to_all(chunk, 'row', split_axis=2, concat_axis=1, tiled=True)  198 us
    ppermute x88, starting transfers between devices, broadcast(): held = lax.ppermute(send, 'row', pairs)  93.3 us
    ppermute x88, waiting for transfers between devices, broadcast(): held = lax.ppermute(send, 'row', pairs)  87.9 us
    all_gather x2, waiting for transfers between devices, body(): halves.append(lax.all_gather(by_row, 'freq', axis=1, tiled=True))  60.4 us
    pallas_call x2, Pallas kernels, make_spectrum(): pl.pallas_call(spectrum_kernel, grid=(groups,), in_specs=in_specs, out_sp...  60.1 us
    select_n x64, other arithmetic, broadcast(): jnp.where(distance[p] == 0, own[p][:, step], held[p])  57.6 us
    dot_general x1, matrix products, body(): lax.dot_general(left_pair, jnp.concatenate(shared, axis=1), dims, preferr...  45.9 us
    unnamed x112, local copies, waits for them, and re-layouts  26.8 us
  transfers between devices with their start and end apart: 90, of which 30 were waited for; matrix products, arithmetic and copies ran while one was open for 14% of the time, Pallas kernels for 4%

profile of v10, /device:TPU:0, one launch (start us, length us, event | category | flops | bytes accessed | tf_op | source)
XLA Modules:
  0.0 722.1 jit_solution(8309164401519910249)
XLA Ops:
  7.2 6.0 fusion.87
  13.2 11.2 %copy.392 = bf16[2,128,8192]{1,0,2:T(2,128)(2,1)} copy(bf16[2,128,8192]{2,1,0:T(8,128)(2,1)} %get-tuple-element.18) | data formatting | bytes 8388608
  24.4 100.5 %all_to_all.36 = bf16[2,128,8192]{1,0,2:T(2,128)(2,1)} all-to-all(bf16[2,128,8192]{1,0,2:T(2,128)(2,1)} %copy.392), channel_id=1, replica_groups=mesh['freq'=4,'row'=8] {'row'}, dimensions={2} | all-to-all | bytes 8388608 | tf_op jit(solution)/shard_map/all_to_all | solution.py:123
  124.9 11.1 %copy.297 = bf16[2,128,8,1024]{3,1,2,0:T(8,128)(2,1)} copy(bf16[2,128,8,1024]{1,0,3,2:T(2,128)(2,1)} %bitcast.631) | data formatting | bytes 8388608 | tf_op jit(solution)/shard_map/all_to_all | solution.py:123
  136.1 11.4 %copy.391 = bf16[2,128,8192]{1,0,2:T(2,128)(2,1)} copy(bf16[2,128,8192]{2,1,0:T(8,128)(2,1)} %get-tuple-element.19) | data formatting | bytes 8388608
  147.6 97.0 %all_to_all.37 = bf16[2,128,8192]{1,0,2:T(2,128)(2,1)} all-to-all(bf16[2,128,8192]{1,0,2:T(2,128)(2,1)} %copy.391), channel_id=1, replica_groups=mesh['freq'=4,'row'=8] {'row'}, dimensions={2} | all-to-all | bytes 8388608 | tf_op jit(solution)/shard_map/all_to_all | solution.py:123
  244.6 11.1 %copy.295 = bf16[2,128,8,1024]{3,1,2,0:T(8,128)(2,1)} copy(bf16[2,128,8,1024]{1,0,3,2:T(2,128)(2,1)} %bitcast.632) | data formatting | bytes 8388608 | tf_op jit(solution)/shard_map/all_to_all | solution.py:123
  270.0 30.2 %shard_map.68.rest_0_ = bf16[2,8192,1024]{2,1,0:T(8,128)(2,1)} custom-call(f32[4]{0:T(128)} %reshape.183.weight_ref, bf16[2,4096,1024]{2,1,0:T(8,128)(2,1)} %all-gather.5.cloned.1.call-done.source_ref, bf16[2,8192,1024]{2,1,0:T(8,128)(2,1)} %bitcast.559), custom_call_target="tpu_custom_call" | custom-call | flops 67108864 | bytes 50331648 | tf_op jit(solution)/shard_map/pallas_call | solution.py:93
  300.2 60.4 %all-gather.3.cloned.1.call-done.source_ref = bf16[2,4096,1024]{2,1,0:T(8,128)(2,1)} async-done(((bf16[2,1024,1024]{2,1,0:T(8,128)(2,1)}), bf16[2,4096,1024]{2,1,0:T(8,128)(2,1)}) %all-gather.3.cloned.1.call-update) | async-done | bytes 16777232 | tf_op jit(solution)/shard_map/all_gather | solution.py:124
  360.6 29.9 %shard_map.69 = bf16[2,8192,1024]{2,1,0:T(8,128)(2,1)} custom-call(f32[4]{0:T(128)} %reshape.183.weight_ref, bf16[2,4096,1024]{2,1,0:T(8,128)(2,1)} %all-gather.3.cloned.1.call-done.source_ref, bf16[2,8192,1024]{2,1,0:T(8,128)(2,1)} %bitcast.560, bf16[2,8192,1024]{2,1,0:T(8,128)(2,1)} %shard_map.68.rest_0_), custom_call_target="tpu_custom_call", output_to_operand_aliasing={{}: (3, {})} | custom-call | flops 67108864 | bytes 50331648 | tf_op jit(solution)/shard_map/pallas_call | solution.py:93
  390.5 6.5 constant_dynamic-slice_fusion
  409.8 3.7 collective-permute-done.66
  421.8 3.0 collective-permute-done.67
  444.5 3.1 collective-permute-done.69
  467.4 3.1 collective-permute-done.71
  490.2 3.1 collective-permute-done.73
  501.7 2.8 collective-permute-done.74
  524.2 2.9 collective-permute-done.76
  578.6 4.7 collective-permute-done.81
  585.4 3.4 collective-permute-done.16
  590.9 3.6 collective-permute-done.82
  596.7 3.4 collective-permute-done.17
  602.2 3.6 collective-permute-done.83
  607.9 3.4 collective-permute-done.18
  613.4 3.6 collective-permute-done.84
  619.1 3.4 collective-permute-done.19
  624.6 3.6 collective-permute-done.85
  630.4 3.4 collective-permute-done.20
  635.9 3.6 collective-permute-done.86
  641.6 2.8 collective-permute-done.21
  660.6 8.8 %fusion.7 = (bf16[8192,256]{1,0:T(8,128)(2,1)}, bf16[8192,256]{1,0:T(8,128)(2,1)}, bf16[8192,256]{1,0:T(8,128)(2,1)}, bf16[8192,256]{1,0:T(8,128)(2,1)}) fusion(bf16[2,4096,256]{2,1,0:T(8,128)(2,1)} %bitcast.636, bf16[2,4096,256]{2,1,0:T(8,128)(2,1)S(1)} %bitcast.633, bf16[2,4096,256]{2,1,0:T(8,128)(2,1)} %bitcast.635, bf16[2,4096,256]{2,1,0:T(8,128)(2,1)S(1)} %bitcast.634), kind=kLoop, calls=%fused_computation.13 | loop fusion | flops 33554432 | bytes 33554432 | tf_op jit(solution)/shard_map/squeeze | solution.py:143
  669.4 45.9 %convert_bitcast_fusion = bf16[1,2,1024,8192]{3,2,1,0:T(8,128)(2,1)} fusion(bf16[8192,256]{1,0:T(8,128)(2,1)} %get-tuple-element.17, bf16[8192,256]{1,0:T(8,128)(2,1)} %get-tuple-element.16, bf16[8192,256]{1,0:T(8,128)(2,1)} %get-tuple-element.29, bf16[8192,256]{1,0:T(8,128)(2,1)} %get-tuple-element.30, bf16[1,1024,1024]{2,1,0:T(8,128)(2,1)} %get-tuple-element.21, ...), kind=kOutput, calls=%fused_computation | convolution fusion | flops 34445721600 | bytes 54525952 | tf_op jit(solution)/shard_map/dot_general | solution.py:146
  (356 shorter events, 201.2 us)
Async XLA Ops:
  7.2 262.8 %all-gather.5.cloned.1.call-start = ((), (), s32[]{:S(2)}) async-start(), calls=%async_computation.3 | async-start | bytes 20971520 | tf_op jit(solution)/shard_map/all_gather | solution.py:124
  136.1 224.5 %all-gather.3.cloned.1.call-start = ((), (), s32[]{:S(2)}) async-start(), calls=%async_computation.2 | async-start | bytes 20971520 | tf_op jit(solution)/shard_map/all_gather | solution.py:124
  399.4 14.2 %collective-permute-start.66 = (bf16[2,256,256]{2,1,0:T(8,128)(2,1)S(1)}, bf16[2,256,256]{2,1,0:T(8,128)(2,1)S(1)}, u32[]{:S(2)}, u32[]{:S(2)}) collective-permute-start(bf16[2,256,256]{2,1,0:T(8,128)(2,1)S(1)} %fusion.31), channel_id=1, source_target_pairs={{2,0},{4,2},{6,4},{7,6},{5,7},{3,5},{1,3},{0,1},{10,8},{12,10},{14... | collective-permute-start | bytes 786440 | tf_op jit(solution)/shard_map/ppermute | solution.py:54
  400.9 13.3 %collective-permute-start.44 = (bf16[2,256,256]{2,1,0:T(8,128)(2,1)S(1)}, bf16[2,256,256]{2,1,0:T(8,128)(2,1)S(1)}, u32[]{:S(2)}, u32[]{:S(2)}) collective-permute-start(bf16[2,256,256]{2,1,0:T(8,128)(2,1)S(1)} %fusion.47), channel_id=1, source_target_pairs={{0,2},{2,4},{4,6},{6,7},{7,5},{5,3},{3,1},{1,0},{8,10},{10,12},{12... | collective-permute-start | bytes 786440 | tf_op jit(solution)/shard_map/ppermute | solution.py:54
  409.2 10.9 %collective-permute-start.23 = (bf16[2,256,256]{2,1,0:T(8,128)(2,1)S(1)}, bf16[2,256,256]{2,1,0:T(8,128)(2,1)S(1)}, u32[]{:S(2)}, u32[]{:S(2)}) collective-permute-start(bf16[2,256,256]{2,1,0:T(8,128)(2,1)S(1)} %fusion.62), channel_id=1, source_target_pairs={{2,0},{4,2},{6,4},{7,6},{5,7},{3,5},{1,3},{0,1},{10,8},{12,10},{14... | collective-permute-start | bytes 786440 | tf_op jit(solution)/shard_map/ppermute | solution.py:54
  413.6 11.2 %collective-permute-start.67 = (bf16[2,256,256]{2,1,0:T(8,128)(2,1)S(1)}, bf16[2,256,256]{2,1,0:T(8,128)(2,1)S(1)}, u32[]{:S(2)}, u32[]{:S(2)}) collective-permute-start(bf16[2,256,256]{2,1,0:T(8,128)(2,1)S(1)} %fusion.29), channel_id=1, source_target_pairs={{2,0},{4,2},{6,4},{7,6},{5,7},{3,5},{1,3},{0,1},{10,8},{12,10},{14... | collective-permute-start | bytes 786440 | tf_op jit(solution)/shard_map/ppermute | solution.py:54
  414.3 12.1 %collective-permute-start.45 = (bf16[2,256,256]{2,1,0:T(8,128)(2,1)S(1)}, bf16[2,256,256]{2,1,0:T(8,128)(2,1)S(1)}, u32[]{:S(2)}, u32[]{:S(2)}) collective-permute-start(bf16[2,256,256]{2,1,0:T(8,128)(2,1)S(1)} %fusion.46), channel_id=1, source_target_pairs={{0,2},{2,4},{4,6},{6,7},{7,5},{5,3},{3,1},{1,0},{8,10},{10,12},{12... | collective-permute-start | bytes 786440 | tf_op jit(solution)/shard_map/ppermute | solution.py:54
  437.1 10.6 %collective-permute-start.69 = (bf16[2,256,256]{2,1,0:T(8,128)(2,1)S(1)}, bf16[2,256,256]{2,1,0:T(8,128)(2,1)S(1)}, u32[]{:S(2)}, u32[]{:S(2)}) collective-permute-start(bf16[2,256,256]{2,1,0:T(8,128)(2,1)S(1)} %fusion.27), channel_id=1, source_target_pairs={{2,0},{4,2},{6,4},{7,6},{5,7},{3,5},{1,3},{0,1},{10,8},{12,10},{14... | collective-permute-start | bytes 786440 | tf_op jit(solution)/shard_map/ppermute | solution.py:54
  461.5 10.6 %collective-permute-start.49 = (bf16[2,256,256]{2,1,0:T(8,128)(2,1)S(1)}, bf16[2,256,256]{2,1,0:T(8,128)(2,1)S(1)}, u32[]{:S(2)}, u32[]{:S(2)}) collective-permute-start(bf16[2,256,256]{2,1,0:T(8,128)(2,1)S(1)} %fusion.42), channel_id=1, source_target_pairs={{0,2},{2,4},{4,6},{6,7},{7,5},{5,3},{3,1},{1,0},{8,10},{10,12},{12... | collective-permute-start | bytes 786440 | tf_op jit(solution)/shard_map/ppermute | solution.py:54
  576.3 12.5 %collective-permute-start.16 = (bf16[2,256,256]{2,1,0:T(8,128)(2,1)S(1)}, bf16[2,256,256]{2,1,0:T(8,128)(2,1)S(1)}, u32[]{:S(2)}, u32[]{:S(2)}) collective-permute-start(bf16[2,256,256]{2,1,0:T(8,128)(2,1)S(1)} %collective-permute-done.15), channel_id=1, source_target_pairs={{0,2},{2,4},{4,6},{6,7},{7,5},{5,3},{3,1},{1,0},{8,10},{10,12},{12... | collective-permute-start | bytes 786440 | tf_op jit(solution)/shard_map/ppermute | solution.py:54
  577.7 12.4 %collective-permute-start.38 = (bf16[2,256,256]{2,1,0:T(8,128)(2,1)S(1)}, bf16[2,256,256]{2,1,0:T(8,128)(2,1)S(1)}, u32[]{:S(2)}, u32[]{:S(2)}) collective-permute-start(bf16[2,256,256]{2,1,0:T(8,128)(2,1)S(1)} %collective-permute-done.37), channel_id=1, source_target_pairs={{2,0},{4,2},{6,4},{7,6},{5,7},{3,5},{1,3},{0,1},{10,8},{12,10},{14... | collective-permute-start | bytes 786440 | tf_op jit(solution)/shard_map/ppermute | solution.py:54
  583.3 11.2 %collective-permute-start.82 = (bf16[2,256,256]{2,1,0:T(8,128)(2,1)S(1)}, bf16[2,256,256]{2,1,0:T(8,128)(2,1)S(1)}, u32[]{:S(2)}, u32[]{:S(2)}) collective-permute-start(bf16[2,256,256]{2,1,0:T(8,128)(2,1)S(1)} %collective-permute-done.81), channel_id=1, source_target_pairs={{2,0},{4,2},{6,4},{7,6},{5,7},{3,5},{1,3},{0,1},{10,8},{12,10},{14... | collective-permute-start | bytes 786440 | tf_op jit(solution)/shard_map/ppermute | solution.py:54
  584.2 11.2 %collective-permute-start.60 = (bf16[2,256,256]{2,1,0:T(8,128)(2,1)S(1)}, bf16[2,256,256]{2,1,0:T(8,128)(2,1)S(1)}, u32[]{:S(2)}, u32[]{:S(2)}) collective-permute-start(bf16[2,256,256]{2,1,0:T(8,128)(2,1)S(1)} %collective-permute-done.59), channel_id=1, source_target_pairs={{0,2},{2,4},{4,6},{6,7},{7,5},{5,3},{3,1},{1,0},{8,10},{10,12},{12... | collective-permute-start | bytes 786440 | tf_op jit(solution)/shard_map/ppermute | solution.py:54
  588.8 11.2 %collective-permute-start.17 = (bf16[2,256,256]{2,1,0:T(8,128)(2,1)S(1)}, bf16[2,256,256]{2,1,0:T(8,128)(2,1)S(1)}, u32[]{:S(2)}, u32[]{:S(2)}) collective-permute-start(bf16[2,256,256]{2,1,0:T(8,128)(2,1)S(1)} %collective-permute-done.16), channel_id=1, source_target_pairs={{0,2},{2,4},{4,6},{6,7},{7,5},{5,3},{3,1},{1,0},{8,10},{10,12},{12... | collective-permute-start | bytes 786440 | tf_op jit(solution)/shard_map/ppermute | solution.py:54
  590.1 11.2 %collective-permute-start.39 = (bf16[2,256,256]{2,1,0:T(8,128)(2,1)S(1)}, bf16[2,256,256]{2,1,0:T(8,128)(2,1)S(1)}, u32[]{:S(2)}, u32[]{:S(2)}) collective-permute-start(bf16[2,256,256]{2,1,0:T(8,128)(2,1)S(1)} %collective-permute-done.38), channel_id=1, source_target_pairs={{2,0},{4,2},{6,4},{7,6},{5,7},{3,5},{1,3},{0,1},{10,8},{12,10},{14... | collective-permute-start | bytes 786440 | tf_op jit(solution)/shard_map/ppermute | solution.py:54
  594.5 11.2 %collective-permute-start.83 = (bf16[2,256,256]{2,1,0:T(8,128)(2,1)S(1)}, bf16[2,256,256]{2,1,0:T(8,128)(2,1)S(1)}, u32[]{:S(2)}, u32[]{:S(2)}) collective-permute-start(bf16[2,256,256]{2,1,0:T(8,128)(2,1)S(1)} %collective-permute-done.82), channel_id=1, source_target_pairs={{2,0},{4,2},{6,4},{7,6},{5,7},{3,5},{1,3},{0,1},{10,8},{12,10},{14... | collective-permute-start | bytes 786440 | tf_op jit(solution)/shard_map/ppermute | solution.py:54
  595.4 11.2 %collective-permute-start.61 = (bf16[2,256,256]{2,1,0:T(8,128)(2,1)S(1)}, bf16[2,256,256]{2,1,0:T(8,128)(2,1)S(1)}, u32[]{:S(2)}, u32[]{:S(2)}) collective-permute-start(bf16[2,256,256]{2,1,0:T(8,128)(2,1)S(1)} %collective-permute-done.60), channel_id=1, source_target_pairs={{0,2},{2,4},{4,6},{6,7},{7,5},{5,3},{3,1},{1,0},{8,10},{10,12},{12... | collective-permute-start | bytes 786440 | tf_op jit(solution)/shard_map/ppermute | solution.py:54
  600.0 11.2 %collective-permute-start.18 = (bf16[2,256,256]{2,1,0:T(8,128)(2,1)S(1)}, bf16[2,256,256]{2,1,0:T(8,128)(2,1)S(1)}, u32[]{:S(2)}, u32[]{:S(2)}) collective-permute-start(bf16[2,256,256]{2,1,0:T(8,128)(2,1)S(1)} %collective-permute-done.17), channel_id=1, source_target_pairs={{0,2},{2,4},{4,6},{6,7},{7,5},{5,3},{3,1},{1,0},{8,10},{10,12},{12... | collective-permute-start | bytes 786440 | tf_op jit(solution)/shard_map/ppermute | solution.py:54
  601.4 11.2 %collective-permute-start.40 = (bf16[2,256,256]{2,1,0:T(8,128)(2,1)S(1)}, bf16[2,256,256]{2,1,0:T(8,128)(2,1)S(1)}, u32[]{:S(2)}, u32[]{:S(2)}) collective-permute-start(bf16[2,256,256]{2,1,0:T(8,128)(2,1)S(1)} %collective-permute-done.39), channel_id=1, source_target_pairs={{2,0},{4,2},{6,4},{7,6},{5,7},{3,5},{1,3},{0,1},{10,8},{12,10},{14... | collective-permute-start | bytes 786440 | tf_op jit(solution)/shard_map/ppermute | solution.py:54
  605.8 11.2 %collective-permute-start.84 = (bf16[2,256,256]{2,1,0:T(8,128)(2,1)S(1)}, bf16[2,256,256]{2,1,0:T(8,128)(2,1)S(1)}, u32[]{:S(2)}, u32[]{:S(2)}) collective-permute-start(bf16[2,256,256]{2,1,0:T(8,128)(2,1)S(1)} %collective-permute-done.83), channel_id=1, source_target_pairs={{2,0},{4,2},{6,4},{7,6},{5,7},{3,5},{1,3},{0,1},{10,8},{12,10},{14... | collective-permute-start | bytes 786440 | tf_op jit(solution)/shard_map/ppermute | solution.py:54
  606.7 11.2 %collective-permute-start.62 = (bf16[2,256,256]{2,1,0:T(8,128)(2,1)S(1)}, bf16[2,256,256]{2,1,0:T(8,128)(2,1)S(1)}, u32[]{:S(2)}, u32[]{:S(2)}) collective-permute-start(bf16[2,256,256]{2,1,0:T(8,128)(2,1)S(1)} %collective-permute-done.61), channel_id=1, source_target_pairs={{0,2},{2,4},{4,6},{6,7},{7,5},{5,3},{3,1},{1,0},{8,10},{10,12},{12... | collective-permute-start | bytes 786440 | tf_op jit(solution)/shard_map/ppermute | solution.py:54
  611.3 11.2 %collective-permute-start.19 = (bf16[2,256,256]{2,1,0:T(8,128)(2,1)S(1)}, bf16[2,256,256]{2,1,0:T(8,128)(2,1)S(1)}, u32[]{:S(2)}, u32[]{:S(2)}) collective-permute-start(bf16[2,256,256]{2,1,0:T(8,128)(2,1)S(1)} %collective-permute-done.18), channel_id=1, source_target_pairs={{0,2},{2,4},{4,6},{6,7},{7,5},{5,3},{3,1},{1,0},{8,10},{10,12},{12... | collective-permute-start | bytes 786440 | tf_op jit(solution)/shard_map/ppermute | solution.py:54
  612.6 11.2 %collective-permute-start.41 = (bf16[2,256,256]{2,1,0:T(8,128)(2,1)S(1)}, bf16[2,256,256]{2,1,0:T(8,128)(2,1)S(1)}, u32[]{:S(2)}, u32[]{:S(2)}) collective-permute-start(bf16[2,256,256]{2,1,0:T(8,128)(2,1)S(1)} %collective-permute-done.40), channel_id=1, source_target_pairs={{2,0},{4,2},{6,4},{7,6},{5,7},{3,5},{1,3},{0,1},{10,8},{12,10},{14... | collective-permute-start | bytes 786440 | tf_op jit(solution)/shard_map/ppermute | solution.py:54
  617.0 11.2 %collective-permute-start.85 = (bf16[2,256,256]{2,1,0:T(8,128)(2,1)S(1)}, bf16[2,256,256]{2,1,0:T(8,128)(2,1)S(1)}, u32[]{:S(2)}, u32[]{:S(2)}) collective-permute-start(bf16[2,256,256]{2,1,0:T(8,128)(2,1)S(1)} %collective-permute-done.84), channel_id=1, source_target_pairs={{2,0},{4,2},{6,4},{7,6},{5,7},{3,5},{1,3},{0,1},{10,8},{12,10},{14... | collective-permute-start | bytes 786440 | tf_op jit(solution)/shard_map/ppermute | solution.py:54
  617.9 11.2 %collective-permute-start.63 = (bf16[2,256,256]{2,1,0:T(8,128)(2,1)S(1)}, bf16[2,256,256]{2,1,0:T(8,128)(2,1)S(1)}, u32[]{:S(2)}, u32[]{:S(2)}) collective-permute-start(bf16[2,256,256]{2,1,0:T(8,128)(2,1)S(1)} %collective-permute-done.62), channel_id=1, source_target_pairs={{0,2},{2,4},{4,6},{6,7},{7,5},{5,3},{3,1},{1,0},{8,10},{10,12},{12... | collective-permute-start | bytes 786440 | tf_op jit(solution)/shard_map/ppermute | solution.py:54
  622.5 11.2 %collective-permute-start.20 = (bf16[2,256,256]{2,1,0:T(8,128)(2,1)S(1)}, bf16[2,256,256]{2,1,0:T(8,128)(2,1)S(1)}, u32[]{:S(2)}, u32[]{:S(2)}) collective-permute-start(bf16[2,256,256]{2,1,0:T(8,128)(2,1)S(1)} %collective-permute-done.19), channel_id=1, source_target_pairs={{0,2},{2,4},{4,6},{6,7},{7,5},{5,3},{3,1},{1,0},{8,10},{10,12},{12... | collective-permute-start | bytes 786440 | tf_op jit(solution)/shard_map/ppermute | solution.py:54
  623.8 11.2 %collective-permute-start.42 = (bf16[2,256,256]{2,1,0:T(8,128)(2,1)S(1)}, bf16[2,256,256]{2,1,0:T(8,128)(2,1)S(1)}, u32[]{:S(2)}, u32[]{:S(2)}) collective-permute-start(bf16[2,256,256]{2,1,0:T(8,128)(2,1)S(1)} %collective-permute-done.41), channel_id=1, source_target_pairs={{2,0},{4,2},{6,4},{7,6},{5,7},{3,5},{1,3},{0,1},{10,8},{12,10},{14... | collective-permute-start | bytes 786440 | tf_op jit(solution)/shard_map/ppermute | solution.py:54
  628.2 11.2 %collective-permute-start.86 = (bf16[2,256,256]{2,1,0:T(8,128)(2,1)S(1)}, bf16[2,256,256]{2,1,0:T(8,128)(2,1)S(1)}, u32[]{:S(2)}, u32[]{:S(2)}) collective-permute-start(bf16[2,256,256]{2,1,0:T(8,128)(2,1)S(1)} %collective-permute-done.85), channel_id=1, source_target_pairs={{2,0},{4,2},{6,4},{7,6},{5,7},{3,5},{1,3},{0,1},{10,8},{12,10},{14... | collective-permute-start | bytes 786440 | tf_op jit(solution)/shard_map/ppermute | solution.py:54
  629.1 11.2 %collective-permute-start.64 = (bf16[2,256,256]{2,1,0:T(8,128)(2,1)S(1)}, bf16[2,256,256]{2,1,0:T(8,128)(2,1)S(1)}, u32[]{:S(2)}, u32[]{:S(2)}) collective-permute-start(bf16[2,256,256]{2,1,0:T(8,128)(2,1)S(1)} %collective-permute-done.63), channel_id=1, source_target_pairs={{0,2},{2,4},{4,6},{6,7},{7,5},{5,3},{3,1},{1,0},{8,10},{10,12},{12... | collective-permute-start | bytes 786440 | tf_op jit(solution)/shard_map/ppermute | solution.py:54
  633.7 10.7 %collective-permute-start.21 = (bf16[2,256,256]{2,1,0:T(8,128)(2,1)S(1)}, bf16[2,256,256]{2,1,0:T(8,128)(2,1)S(1)}, u32[]{:S(2)}, u32[]{:S(2)}) collective-permute-start(bf16[2,256,256]{2,1,0:T(8,128)(2,1)S(1)} %collective-permute-done.20), channel_id=1, source_target_pairs={{0,2},{2,4},{4,6},{6,7},{7,5},{5,3},{3,1},{1,0},{8,10},{10,12},{12... | collective-permute-start | bytes 786440 | tf_op jit(solution)/shard_map/ppermute | solution.py:54
  639.5 17.1 %collective-permute-start.87 = (bf16[2,256,256]{2,1,0:T(8,128)(2,1)S(1)}, bf16[2,256,256]{2,1,0:T(8,128)(2,1)S(1)}, u32[]{:S(2)}, u32[]{:S(2)}) collective-permute-start(bf16[2,256,256]{2,1,0:T(8,128)(2,1)S(1)} %collective-permute-done.86), channel_id=1, source_target_pairs={{2,0},{4,2},{6,4},{7,6},{5,7},{3,5},{1,3},{0,1},{10,8},{12,10},{14... | collective-permute-start | bytes 786440 | tf_op jit(solution)/shard_map/ppermute | solution.py:54
  640.4 12.0 %collective-permute-start.65 = (bf16[2,256,256]{2,1,0:T(8,128)(2,1)S(1)}, bf16[2,256,256]{2,1,0:T(8,128)(2,1)}, u32[]{:S(2)}, u32[]{:S(2)}) collective-permute-start(bf16[2,256,256]{2,1,0:T(8,128)(2,1)S(1)} %collective-permute-done.64), channel_id=1, source_target_pairs={{0,2},{2,4},{4,6},{6,7},{7,5},{5,3},{3,1},{1,0},{8,10},{10,12},{12... | collective-permute-start | bytes 786440 | tf_op jit(solution)/shard_map/ppermute | solution.py:54
  (71 other events, 747.1 us)
Sparse Core Ops, SparseCore 0:
  136.2 104.9 all-gather.4
  255.8 104.7 all-gather.2

commit v11 on v10

--- a/solution.py
+++ b/solution.py
@@ -12,7 +12,7 @@
 STEPS = 2
 BLOCK_START = 1022
 PIECES = 2
-RING_CHUNKS = 16
+RING_CHUNKS = 32
 
 
 def ring_order(count):

time: 727 us -> 807 us (1.11); the launches traced: 722 us -> 793 us
  waiting for transfers between devices: 148 us -> 68.6 us
  starting transfers between devices: 93.3 us -> 163 us
  other arithmetic: 76.9 us -> 133 us
  local copies, waits for them, and re-layouts: 73.3 us -> 97.5 us
    ppermute x88 -> x152, waiting for transfers between devices: 87.9 us -> 8.22 us  [broadcast(): held = lax.ppermute(send, 'row', pairs)]
    ppermute x88 -> x152, starting transfers between devices: 93.3 us -> 163 us  [broadcast(): held = lax.ppermute(send, 'row', pairs)]
    select_n x64 -> x128, other arithmetic: 57.6 us -> 112 us  [broadcast(): jnp.where(distance[p] == 0, own[p][:, step], held[p])]
    unnamed x112 -> x180, local copies, waits for them, and re-layouts: 26.8 us -> 52.3 us
  transfers between devices with their start and end apart: 90 -> 154, of which waited for: 30 -> 13; matrix products, arithmetic and copies ran while one was open for 14% -> 23% of each run, Pallas kernels for 4% -> 4%
where the time goes in v11:
time: 807 us; the launch traced here: 793 us
  blocking collectives  198 us (25%)
  starting transfers between devices  163 us (20%)
  other arithmetic  133 us (16%)
  local copies, waits for them, and re-layouts  97.5 us (12%)
  waiting for transfers between devices  68.6 us (9%)
  Pallas kernels  60.7 us (8%)
  matrix products  45.9 us (6%)
  between operations  27.1 us (3%)
    all_to_all x2, blocking collectives, body(): lax.all_to_all(chunk, 'row', split_axis=2, concat_axis=1, tiled=True)  198 us
    ppermute x152, starting transfers between devices, broadcast(): held = lax.ppermute(send, 'row', pairs)  163 us
    select_n x128, other arithmetic, broadcast(): jnp.where(distance[p] == 0, own[p][:, step], held[p])  112 us
    pallas_call x2, Pallas kernels, make_spectrum(): pl.pallas_call(spectrum_kernel, grid=(groups,), in_specs=in_specs, out_sp...  60.7 us
    all_gather x2, waiting for transfers between devices, body(): halves.append(lax.all_gather(by_row, 'freq', axis=1, tiled=True))  60.3 us
    unnamed x180, local copies, waits for them, and re-layouts  52.3 us
    dot_general x1, matrix products, body(): lax.dot_general(left_pair, jnp.concatenate(shared, axis=1), dims, preferr...  45.9 us
    all_to_all x2, local copies, waits for them, and re-layouts, body(): lax.all_to_all(chunk, 'row', split_axis=2, concat_axis=1, tiled=True)  22.3 us
  transfers between devices with their start and end apart: 154, of which 13 were waited for; matrix products, arithmetic and copies ran while one was open for 23% of the time, Pallas kernels for 4%

profile of v11, /device:TPU:0, one launch (start us, length us, event | category | flops | bytes accessed | tf_op | source)
XLA Modules:
  0.0 793.1 jit_solution(16459146983244691432)
XLA Ops:
  7.2 6.0 fusion.151
  13.2 11.2 %copy.712 = bf16[2,128,8192]{1,0,2:T(2,128)(2,1)} copy(bf16[2,128,8192]{2,1,0:T(8,128)(2,1)} %get-tuple-element.18) | data formatting | bytes 8388608
  24.4 100.5 %all_to_all.36 = bf16[2,128,8192]{1,0,2:T(2,128)(2,1)} all-to-all(bf16[2,128,8192]{1,0,2:T(2,128)(2,1)} %copy.712), channel_id=1, replica_groups=mesh['freq'=4,'row'=8] {'row'}, dimensions={2} | all-to-all | bytes 8388608 | tf_op jit(solution)/shard_map/all_to_all | solution.py:123
  124.9 11.2 %copy.537 = bf16[2,128,8,1024]{3,1,2,0:T(8,128)(2,1)} copy(bf16[2,128,8,1024]{1,0,3,2:T(2,128)(2,1)} %bitcast.1143) | data formatting | bytes 8388608 | tf_op jit(solution)/shard_map/all_to_all | solution.py:123
  136.2 11.4 %copy.711 = bf16[2,128,8192]{1,0,2:T(2,128)(2,1)} copy(bf16[2,128,8192]{2,1,0:T(8,128)(2,1)} %get-tuple-element.19) | data formatting | bytes 8388608
  147.6 97.0 %all_to_all.37 = bf16[2,128,8192]{1,0,2:T(2,128)(2,1)} all-to-all(bf16[2,128,8192]{1,0,2:T(2,128)(2,1)} %copy.711), channel_id=1, replica_groups=mesh['freq'=4,'row'=8] {'row'}, dimensions={2} | all-to-all | bytes 8388608 | tf_op jit(solution)/shard_map/all_to_all | solution.py:123
  244.6 11.1 %copy.535 = bf16[2,128,8,1024]{3,1,2,0:T(8,128)(2,1)} copy(bf16[2,128,8,1024]{1,0,3,2:T(2,128)(2,1)} %bitcast.1144) | data formatting | bytes 8388608 | tf_op jit(solution)/shard_map/all_to_all | solution.py:123
  269.5 30.8 %shard_map.68.rest_0_ = bf16[2,8192,1024]{2,1,0:T(8,128)(2,1)} custom-call(f32[4]{0:T(128)} %reshape.183.weight_ref, bf16[2,4096,1024]{2,1,0:T(8,128)(2,1)} %all-gather.5.cloned.1.call-done.source_ref, bf16[2,8192,1024]{2,1,0:T(8,128)(2,1)} %bitcast.1007), custom_call_target="tpu_custom_call" | custom-call | flops 67108864 | bytes 50331648 | tf_op jit(solution)/shard_map/pallas_call | solution.py:93
  300.3 60.3 %all-gather.3.cloned.1.call-done.source_ref = bf16[2,4096,1024]{2,1,0:T(8,128)(2,1)} async-done(((bf16[2,1024,1024]{2,1,0:T(8,128)(2,1)}), bf16[2,4096,1024]{2,1,0:T(8,128)(2,1)}) %all-gather.3.cloned.1.call-update) | async-done | bytes 16777232 | tf_op jit(solution)/shard_map/all_gather | solution.py:124
  360.6 29.9 %shard_map.69 = bf16[2,8192,1024]{2,1,0:T(8,128)(2,1)} custom-call(f32[4]{0:T(128)} %reshape.183.weight_ref, bf16[2,4096,1024]{2,1,0:T(8,128)(2,1)} %all-gather.3.cloned.1.call-done.source_ref, bf16[2,8192,1024]{2,1,0:T(8,128)(2,1)} %bitcast.1008, bf16[2,8192,1024]{2,1,0:T(8,128)(2,1)} %shard_map.68.rest_0_), custom_call_target="tpu_custom_call", output_to_operand_aliasing={{}: (3, {})} | custom-call | flops 67108864 | bytes 50331648 | tf_op jit(solution)/shard_map/pallas_call | solution.py:93
  390.5 2.1 dynamic-slice_bitcast_fusion.3
  394.2 6.6 constant_dynamic-slice_fusion
  405.1 3.7 maximum_bitcast_fusion.2
  418.5 1.8 collective-permute-start.116
  427.3 1.8 collective-permute-start.117
  436.0 1.8 collective-permute-start.118
  444.8 1.8 collective-permute-start.119
  453.6 1.8 collective-permute-start.120
  462.4 1.7 collective-permute-start.121
  506.3 1.9 collective-permute-start.126
  646.9 1.7 collective-permute-start.142
  655.7 1.7 collective-permute-start.143
  664.5 1.7 collective-permute-start.144
  673.5 1.7 collective-permute-start.145
  712.1 2.8 collective-permute-done.113
  716.5 2.9 dynamic-slice_select_fusion.1
  720.0 2.9 dynamic-slice_select_fusion.3
  724.2 2.4 copy.571
  726.6 2.4 copy.605
  729.1 1.8 copy-done.1
  731.3 8.6 %fusion.7 = (bf16[8192,256]{1,0:T(8,128)(2,1)}, bf16[8192,256]{1,0:T(8,128)(2,1)}, bf16[8192,256]{1,0:T(8,128)(2,1)}, bf16[8192,256]{1,0:T(8,128)(2,1)}) fusion(bf16[2,4096,256]{2,1,0:T(8,128)(2,1)S(1)} %bitcast.1146, bf16[2,4096,256]{2,1,0:T(8,128)(2,1)S(1)} %bitcast.1145, bf16[2,4096,256]{2,1,0:T(8,128)(2,1)} %bitcast.1148, bf16[2,4096,256]{2,1,0:T(8,128)(2,1)} %bitcast.1147), kind=kLoop, calls=%fused_computation.13 | loop fusion | flops 33554432 | bytes 33554432 | tf_op jit(solution)/shard_map/squeeze | solution.py:143
  740.0 45.9 %convert_bitcast_fusion = bf16[1,2,1024,8192]{3,2,1,0:T(8,128)(2,1)} fusion(bf16[8192,256]{1,0:T(8,128)(2,1)} %get-tuple-element.17, bf16[8192,256]{1,0:T(8,128)(2,1)} %get-tuple-element.16, bf16[8192,256]{1,0:T(8,128)(2,1)} %get-tuple-element.29, bf16[8192,256]{1,0:T(8,128)(2,1)} %get-tuple-element.30, bf16[1,1024,1024]{2,1,0:T(8,128)(2,1)} %get-tuple-element.21, ...), kind=kOutput, calls=%fused_computation | convolution fusion | flops 34445721600 | bytes 54525952 | tf_op jit(solution)/shard_map/dot_general | solution.py:146
  (617 shorter events, 295.2 us)
Async XLA Ops:
  7.2 262.3 %all-gather.5.cloned.1.call-start = ((), (), s32[]{:S(2)}) async-start(), calls=%async_computation.3 | async-start | bytes 20971520 | tf_op jit(solution)/shard_map/all_gather | solution.py:124
  136.1 224.5 %all-gather.3.cloned.1.call-start = ((), (), s32[]{:S(2)}) async-start(), calls=%async_computation.2 | async-start | bytes 20971520 | tf_op jit(solution)/shard_map/all_gather | solution.py:124
  400.8 8.0 %collective-permute-start.38 = (bf16[2,128,256]{2,1,0:T(8,128)(2,1)S(1)}, bf16[2,128,256]{2,1,0:T(8,128)(2,1)S(1)}, u32[]{:S(2)}, u32[]{:S(2)}) collective-permute-start(bf16[2,128,256]{2,1,0:T(8,128)(2,1)S(1)} %fusion.111), channel_id=1, source_target_pairs={{2,0},{4,2},{6,4},{7,6},{5,7},{3,5},{1,3},{0,1},{10,8},{12,10},{14... | collective-permute-start | bytes 393224 | tf_op jit(solution)/shard_map/ppermute | solution.py:54
  402.3 8.0 %collective-permute-start.114 = (bf16[2,128,256]{2,1,0:T(8,128)(2,1)S(1)}, bf16[2,128,256]{2,1,0:T(8,128)(2,1)S(1)}, u32[]{:S(2)}, u32[]{:S(2)}) collective-permute-start(bf16[2,128,256]{2,1,0:T(8,128)(2,1)S(1)} %fusion.47), channel_id=1, source_target_pairs={{2,0},{4,2},{6,4},{7,6},{5,7},{3,5},{1,3},{0,1},{10,8},{12,10},{14... | collective-permute-start | bytes 393224 | tf_op jit(solution)/shard_map/ppermute | solution.py:54
  403.9 8.0 %collective-permute-start = (bf16[2,128,256]{2,1,0:T(8,128)(2,1)S(1)}, bf16[2,128,256]{2,1,0:T(8,128)(2,1)S(1)}, u32[]{:S(2)}, u32[]{:S(2)}) collective-permute-start(bf16[2,128,256]{2,1,0:T(8,128)(2,1)S(1)} %fusion.143), channel_id=1, source_target_pairs={{0,2},{2,4},{4,6},{6,7},{7,5},{5,3},{3,1},{1,0},{8,10},{10,12},{12... | collective-permute-start | bytes 393224 | tf_op jit(solution)/shard_map/ppermute | solution.py:54
  404.5 8.1 %collective-permute-start.76 = (bf16[2,128,256]{2,1,0:T(8,128)(2,1)S(1)}, bf16[2,128,256]{2,1,0:T(8,128)(2,1)S(1)}, u32[]{:S(2)}, u32[]{:S(2)}) collective-permute-start(bf16[2,128,256]{2,1,0:T(8,128)(2,1)S(1)} %fusion.79), channel_id=1, source_target_pairs={{0,2},{2,4},{4,6},{6,7},{7,5},{5,3},{3,1},{1,0},{8,10},{10,12},{12... | collective-permute-start | bytes 393224 | tf_op jit(solution)/shard_map/ppermute | solution.py:54
  412.0 8.2 %collective-permute-start.1 = (bf16[2,128,256]{2,1,0:T(8,128)(2,1)S(1)}, bf16[2,128,256]{2,1,0:T(8,128)(2,1)S(1)}, u32[]{:S(2)}, u32[]{:S(2)}) collective-permute-start(bf16[2,128,256]{2,1,0:T(8,128)(2,1)S(1)} %fusion.142), channel_id=1, source_target_pairs={{0,2},{2,4},{4,6},{6,7},{7,5},{5,3},{3,1},{1,0},{8,10},{10,12},{12... | collective-permute-start | bytes 393224 | tf_op jit(solution)/shard_map/ppermute | solution.py:54
  412.6 8.9 %collective-permute-start.77 = (bf16[2,128,256]{2,1,0:T(8,128)(2,1)S(1)}, bf16[2,128,256]{2,1,0:T(8,128)(2,1)S(1)}, u32[]{:S(2)}, u32[]{:S(2)}) collective-permute-start(bf16[2,128,256]{2,1,0:T(8,128)(2,1)S(1)} %fusion.78), channel_id=1, source_target_pairs={{0,2},{2,4},{4,6},{6,7},{7,5},{5,3},{3,1},{1,0},{8,10},{10,12},{12... | collective-permute-start | bytes 393224 | tf_op jit(solution)/shard_map/ppermute | solution.py:54
  415.0 9.8 %collective-permute-start.40 = (bf16[2,128,256]{2,1,0:T(8,128)(2,1)S(1)}, bf16[2,128,256]{2,1,0:T(8,128)(2,1)S(1)}, u32[]{:S(2)}, u32[]{:S(2)}) collective-permute-start(bf16[2,128,256]{2,1,0:T(8,128)(2,1)S(1)} %fusion.109), channel_id=1, source_target_pairs={{2,0},{4,2},{6,4},{7,6},{5,7},{3,5},{1,3},{0,1},{10,8},{12,10},{14... | collective-permute-start | bytes 393224 | tf_op jit(solution)/shard_map/ppermute | solution.py:54
  418.5 7.9 collective-permute-start.116
  427.3 7.9 collective-permute-start.117
  444.8 7.9 collective-permute-start.119
  448.8 7.9 collective-permute-start.81
  453.6 7.9 collective-permute-start.120
  488.7 7.9 collective-permute-start.124
  500.2 8.0 %collective-permute-start.11 = (bf16[2,128,256]{2,1,0:T(8,128)(2,1)S(1)}, bf16[2,128,256]{2,1,0:T(8,128)(2,1)S(1)}, u32[]{:S(2)}, u32[]{:S(2)}) collective-permute-start(bf16[2,128,256]{2,1,0:T(8,128)(2,1)S(1)} %fusion.132), channel_id=1, source_target_pairs={{0,2},{2,4},{4,6},{6,7},{7,5},{5,3},{3,1},{1,0},{8,10},{10,12},{12... | collective-permute-start | bytes 393224 | tf_op jit(solution)/shard_map/ppermute | solution.py:54
  501.6 8.0 %collective-permute-start.87 = (bf16[2,128,256]{2,1,0:T(8,128)(2,1)S(1)}, bf16[2,128,256]{2,1,0:T(8,128)(2,1)S(1)}, u32[]{:S(2)}, u32[]{:S(2)}) collective-permute-start(bf16[2,128,256]{2,1,0:T(8,128)(2,1)S(1)} %fusion.68), channel_id=1, source_target_pairs={{0,2},{2,4},{4,6},{6,7},{7,5},{5,3},{3,1},{1,0},{8,10},{10,12},{12... | collective-permute-start | bytes 393224 | tf_op jit(solution)/shard_map/ppermute | solution.py:54
  504.7 8.0 %collective-permute-start.50 = (bf16[2,128,256]{2,1,0:T(8,128)(2,1)S(1)}, bf16[2,128,256]{2,1,0:T(8,128)(2,1)S(1)}, u32[]{:S(2)}, u32[]{:S(2)}) collective-permute-start(bf16[2,128,256]{2,1,0:T(8,128)(2,1)S(1)} %fusion.99), channel_id=1, source_target_pairs={{2,0},{4,2},{6,4},{7,6},{5,7},{3,5},{1,3},{0,1},{10,8},{12,10},{14... | collective-permute-start | bytes 393224 | tf_op jit(solution)/shard_map/ppermute | solution.py:54
  506.3 8.0 %collective-permute-start.126 = (bf16[2,128,256]{2,1,0:T(8,128)(2,1)S(1)}, bf16[2,128,256]{2,1,0:T(8,128)(2,1)S(1)}, u32[]{:S(2)}, u32[]{:S(2)}) collective-permute-start(bf16[2,128,256]{2,1,0:T(8,128)(2,1)S(1)} %fusion.34), channel_id=1, source_target_pairs={{2,0},{4,2},{6,4},{7,6},{5,7},{3,5},{1,3},{0,1},{10,8},{12,10},{14... | collective-permute-start | bytes 393224 | tf_op jit(solution)/shard_map/ppermute | solution.py:54
  532.8 7.9 collective-permute-start.129
  567.9 7.9 collective-permute-start.133
  594.2 7.9 collective-permute-start.136
  603.0 7.9 collective-permute-start.137
  629.4 7.9 collective-permute-start.140
  662.9 8.0 %collective-permute-start.68 = (bf16[2,128,256]{2,1,0:T(8,128)(2,1)S(1)}, bf16[2,128,256]{2,1,0:T(8,128)(2,1)S(1)}, u32[]{:S(2)}, u32[]{:S(2)}) collective-permute-start(bf16[2,128,256]{2,1,0:T(8,128)(2,1)S(1)} %fusion.81), channel_id=1, source_target_pairs={{2,0},{4,2},{6,4},{7,6},{5,7},{3,5},{1,3},{0,1},{10,8},{12,10},{14... | collective-permute-start | bytes 393224 | tf_op jit(solution)/shard_map/ppermute | solution.py:54
  664.5 8.1 %collective-permute-start.144 = (bf16[2,128,256]{2,1,0:T(8,128)(2,1)S(1)}, bf16[2,128,256]{2,1,0:T(8,128)(2,1)S(1)}, u32[]{:S(2)}, u32[]{:S(2)}) collective-permute-start(bf16[2,128,256]{2,1,0:T(8,128)(2,1)S(1)} %fusion.16), channel_id=1, source_target_pairs={{2,0},{4,2},{6,4},{7,6},{5,7},{3,5},{1,3},{0,1},{10,8},{12,10},{14... | collective-permute-start | bytes 393224 | tf_op jit(solution)/shard_map/ppermute | solution.py:54
  667.2 8.1 %collective-permute-start.30 = (bf16[2,128,256]{2,1,0:T(8,128)(2,1)S(1)}, bf16[2,128,256]{2,1,0:T(8,128)(2,1)S(1)}, u32[]{:S(2)}, u32[]{:S(2)}) collective-permute-start(bf16[2,128,256]{2,1,0:T(8,128)(2,1)S(1)} %fusion.113), channel_id=1, source_target_pairs={{0,2},{2,4},{4,6},{6,7},{7,5},{5,3},{3,1},{1,0},{8,10},{10,12},{12... | collective-permute-start | bytes 393224 | tf_op jit(solution)/shard_map/ppermute | solution.py:54
  668.5 8.4 %collective-permute-start.106 = (bf16[2,128,256]{2,1,0:T(8,128)(2,1)S(1)}, bf16[2,128,256]{2,1,0:T(8,128)(2,1)S(1)}, u32[]{:S(2)}, u32[]{:S(2)}) collective-permute-start(bf16[2,128,256]{2,1,0:T(8,128)(2,1)S(1)} %fusion.49), channel_id=1, source_target_pairs={{0,2},{2,4},{4,6},{6,7},{7,5},{5,3},{3,1},{1,0},{8,10},{10,12},{12... | collective-permute-start | bytes 393224 | tf_op jit(solution)/shard_map/ppermute | solution.py:54
  671.9 8.1 %collective-permute-start.69 = (bf16[2,128,256]{2,1,0:T(8,128)(2,1)S(1)}, bf16[2,128,256]{2,1,0:T(8,128)(2,1)S(1)}, u32[]{:S(2)}, u32[]{:S(2)}) collective-permute-start(bf16[2,128,256]{2,1,0:T(8,128)(2,1)S(1)} %fusion.80), channel_id=1, source_target_pairs={{2,0},{4,2},{6,4},{7,6},{5,7},{3,5},{1,3},{0,1},{10,8},{12,10},{14... | collective-permute-start | bytes 393224 | tf_op jit(solution)/shard_map/ppermute | solution.py:54
  706.4 16.5 %collective-permute-start.75 = (bf16[2,128,256]{2,1,0:T(8,128)(2,1)S(1)}, bf16[2,128,256]{2,1,0:T(8,128)(2,1)S(1)}, u32[]{:S(2)}, u32[]{:S(2)}) collective-permute-start(bf16[2,128,256]{2,1,0:T(8,128)(2,1)S(1)} %collective-permute-done.74), channel_id=1, source_target_pairs={{2,0},{4,2},{6,4},{7,6},{5,7},{3,5},{1,3},{0,1},{10,8},{12,10},{14... | collective-permute-start | bytes 393224 | tf_op jit(solution)/shard_map/ppermute | solution.py:54
  707.8 21.2 %collective-permute-start.151 = (bf16[2,128,256]{2,1,0:T(8,128)(2,1)S(1)}, bf16[2,128,256]{2,1,0:T(8,128)(2,1)S(1)}, u32[]{:S(2)}, u32[]{:S(2)}) collective-permute-start(bf16[2,128,256]{2,1,0:T(8,128)(2,1)S(1)} %collective-permute-done.150), channel_id=1, source_target_pairs={{2,0},{4,2},{6,4},{7,6},{5,7},{3,5},{1,3},{0,1},{10,8},{12,10},{14... | collective-permute-start | bytes 393224 | tf_op jit(solution)/shard_map/ppermute | solution.py:54
  708.5 10.9 %collective-permute-start.37 = (bf16[2,128,256]{2,1,0:T(8,128)(2,1)S(1)}, bf16[2,128,256]{2,1,0:T(8,128)(2,1)S(1)}, u32[]{:S(2)}, u32[]{:S(2)}) collective-permute-start(bf16[2,128,256]{2,1,0:T(8,128)(2,1)S(1)} %collective-permute-done.36), channel_id=1, source_target_pairs={{0,2},{2,4},{4,6},{6,7},{7,5},{5,3},{3,1},{1,0},{8,10},{10,12},{12... | collective-permute-start | bytes 393224 | tf_op jit(solution)/shard_map/ppermute | solution.py:54
  (137 other events, 1050.7 us)
Sparse Core Ops, SparseCore 0:
  136.3 104.9 all-gather.4
  255.9 104.7 all-gather.2
